TPU v7x, 512 devices: a whole 4x4x16 slice. The times are simulated.
512 devices in a mesh: section: 8 (over x, y_hi), vocab: 64 (over z, y_lo, core).
Axes of the slice: x: 4, y: 4 (y_hi: 2, y_lo: 2; y = y_hi * 2 + y_lo), z: 16, core: 2. Of those that a mesh axis runs over, the one named last changes fastest.
Arguments:
- hidden: bfloat16 [512, 8192], P('vocab', 'section'), may hold values from -6 to 6
- head_weight: bfloat16 [98304, 8192], P('vocab', 'section'), may hold values from -3 to 3
- lengths: int32 [8], replicated, may hold values from 16 to 64
- pairing: int32 [4], replicated, may hold values from 0 to 3, each once
Outputs:
- hidden_grad: float32 [512, 8192], P('vocab', 'section')
- loss: float32 [], replicated
Inputs may be any that keep to these rules, and one draw needn't show every extreme that they name: Every sequence has at least one live token; positions from lengths on are padding. `pairing`: a permutation: each document matches exactly one query.
All inputs are finite; a program needn't handle non-finite values.
Results may differ from a plain program's by a relative error of at most 0.0018.
Values may be sent and summed in bfloat16 or wider, within the bound.
No kernel may reach another device: no remote copies, remote signals or barrier semaphores. Data moves between devices by JAX's collectives and lax.ppermute only.
A program may use at most 64 MiB of HBM per device.

v0:
```python
import jax
import jax.numpy as jnp
from jax import lax
from jax.sharding import PartitionSpec as P

NSEQ = 8


pool_temp = 0.5
score_temp = 0.02
grad_scale = 16.0
eps_norm = 1e-06


def local(hidden, head_weight, lengths, pairing):
    half = NSEQ // 2
    partial_logits = lax.dot_general(
        lax.all_gather(hidden, "vocab", axis=0, tiled=True),
        head_weight,
        (((1,), (1,)), ((), ())),
        preferred_element_type=jnp.float32,
    )
    total_rows = partial_logits.shape[0]
    seq_len = total_rows // NSEQ
    logits = lax.psum(partial_logits, "section")
    columns = logits.shape[1]
    soft = jax.nn.softplus(logits)
    act = jnp.log1p(soft)
    positions = jnp.arange(seq_len, dtype=jnp.int32)
    live = (positions[None, :] < lengths[:, None]).astype(jnp.float32)
    expo = jnp.exp(act / pool_temp).reshape(NSEQ, seq_len, columns) * live[:, :, None]
    totals = jnp.sum(expo, axis=1)
    pooled = pool_temp * jnp.log(totals)
    queries = pooled[:half]
    documents = pooled[half:]
    dots_part = lax.dot_general(
        queries, documents, (((1,), (1,)), ((), ())), precision=lax.Precision.HIGHEST
    )
    norms_part = jnp.sum(pooled * pooled, axis=1)
    dots, norms = lax.psum((dots_part, norms_part), "vocab")
    inv = lax.rsqrt(norms + eps_norm)
    inv_q = inv[:half]
    inv_d = inv[half:]
    scores = dots * inv_q[:, None] * inv_d[None, :] / score_temp
    weights = jnp.exp(scores)
    row_sum = jnp.sum(weights, axis=1)
    probs = weights / row_sum[:, None]
    target = (jnp.arange(half, dtype=jnp.int32)[None, :] == pairing[:, None]).astype(jnp.float32)
    loss = jnp.sum(jnp.log(row_sum) - jnp.sum(scores * target, axis=1))
    dscore = grad_scale * (probs - target)
    gdots = dscore * inv_q[:, None] * inv_d[None, :] / score_temp
    dinv_q = jnp.sum(dscore * dots * inv_d[None, :], axis=1) / score_temp
    dinv_d = jnp.sum(dscore * dots * inv_q[:, None], axis=0) / score_temp
    dinv = jnp.concatenate([dinv_q, dinv_d])
    dnorm = -0.5 * dinv * inv * inv * inv
    dpool_q = (
        jnp.dot(gdots, documents, precision=lax.Precision.HIGHEST)
        + 2.0 * dnorm[:half, None] * queries
    )
    dpool_d = (
        jnp.dot(gdots.T, queries, precision=lax.Precision.HIGHEST)
        + 2.0 * dnorm[half:, None] * documents
    )
    dpooled = jnp.concatenate([dpool_q, dpool_d], axis=0)
    dact = (dpooled[:, None, :] * expo / totals[:, None, :]).reshape(total_rows, columns)
    dlogit = (dact * jax.nn.sigmoid(logits) / (1.0 + soft)).astype(jnp.bfloat16)
    hidden_grad = lax.psum_scatter(
        jnp.dot(dlogit, head_weight, preferred_element_type=jnp.float32),
        "vocab",
        scatter_dimension=0,
        tiled=True,
    )
    return (hidden_grad, loss)


def solution(mesh):
    in_specs = (P("vocab", "section"), P("vocab", "section"), P(), P())
    out_specs = (P("vocab", "section"), P())
    return jax.shard_map(local, mesh=mesh, in_specs=in_specs, out_specs=out_specs, check_vma=False)
```

profile of v0, /device:TPU:1, one launch (start us, length us, event | category | flops | bytes accessed | tf_op | source)
XLA Modules:
  0.0 651.7 jit_solution(2297248620862196060)
XLA Ops:
  7.2 0.0 copy-start
  7.2 0.0 all-gather.2.cloned.1.call-start
  7.2 0.7 all-gather.2.cloned.1.call-update
  7.9 0.0 all-reduce.3.cloned.1.call-start
  8.0 128.5 %all-gather.2.cloned.1.call-done = bf16[512,1024]{1,0:T(8,128)(2,1)} async-done(((bf16[8,1024]{1,0:T(8,128)(2,1)}), bf16[512,1024]{1,0:T(8,128)(2,1)}) %all-gather.2.cloned.1.call-update) | async-done | bytes 1048592 | tf_op jit(solution)/shard_map/all_gather | solution.py:18
  136.5 0.0 copy-done
  136.5 4.7 fusion.17
  141.2 0.0 copy-start.1
  141.2 0.0 all-reduce.3.cloned.1.call-update
  141.2 0.0 copy-start.2
  141.2 0.0 reduce-scatter.2.cloned.1.call-start
  141.3 0.6 copy-done.1
  141.8 0.1 fusion.8
  141.9 0.1 reshape.50
  142.0 156.5 %all-reduce.3.cloned.1.call-done = f32[512,1536]{1,0:T(8,128)} async-done(((f32[512,1536]{1,0:T(8,128)}), f32[512,1536]{1,0:T(8,128)}) %all-reduce.3.cloned.1.call-update) | async-done | bytes 3145744 | tf_op jit(solution)/shard_map/psum | solution.py:25
  298.5 5.1 multiply_reduce_fusion
  303.5 0.1 multiply_reduce_fusion.1
  303.7 0.2 fusion.4
  303.8 106.4 %all-reduce = (f32[8]{0:T(128)S(1)}, f32[4,4]{1,0:T(4,128)S(1)}) all-reduce(f32[8]{0:T(128)S(1)} %get-tuple-element.8, f32[4,4]{1,0:T(4,128)S(1)} %fusion.4), channel_id=1, replica_groups=mesh['section'=8,'vocab'=64] {'vocab'}, use_global_device_ids=true, to_apply=%region_4.5 | all-reduce | flops 24 | bytes 192 | tf_op jit(solution)/shard_map/psum | solution.py:40
  410.3 0.1 broadcast_multiply_fusion.2
  410.3 0.2 exponential_reduce_fusion
  410.5 0.0 copy-done.2
  410.5 0.2 multiply_reduce_fusion.3
  410.7 0.1 multiply_multiply_fusion.5
  410.8 0.1 slice_multiply_fusion.1
  410.9 0.3 convolution_add_fusion.1
  411.1 0.3 convolution_add_fusion
  411.5 5.5 fusion.2
  417.0 3.2 fusion.18
  420.2 0.0 reduce-scatter.2.cloned.1.call-update
  420.3 0.6 subtract_reduce_fusion
  420.9 224.3 %reduce-scatter.2.cloned.1.call-done = f32[8,1024]{1,0:T(8,128)} async-done(((f32[512,1024]{1,0:T(8,128)}), f32[8,1024]{1,0:T(8,128)}) %reduce-scatter.2.cloned.1.call-update) | async-done | bytes 32784 | tf_op jit(solution)/shard_map/reduce_scatter | solution.py:67
  (3 shorter events, 0.0 us)
Async XLA Ops:
  7.2 129.3 %copy-start = (bf16[1536,1024]{1,0:T(8,128)(2,1)S(1)}, bf16[1536,1024]{1,0:T(8,128)(2,1)}, u32[]{:S(2)}) copy-start(bf16[1536,1024]{1,0:T(8,128)(2,1)} %param.5) | copy-start | bytes 9437188
  7.2 129.3 %all-gather.2.cloned.1.call-start = ((), (), s32[]{:S(2)}) async-start(), calls=%async_computation.1 | async-start | bytes 1064960 | tf_op jit(solution)/shard_map/all_gather | solution.py:18
  7.9 290.6 %all-reduce.3.cloned.1.call-start = ((), (), s32[]{:S(2)}) async-start(), calls=%async_computation.2 | async-start | bytes 6291456 | tf_op jit(solution)/shard_map/psum | solution.py:25
  141.2 0.7 copy-start.1
  141.2 269.3 %copy-start.2 = (s32[4]{0:T(128)S(1)}, s32[4]{0:T(128)}, u32[]{:S(2)}) copy-start(s32[4]{0:T(128)} %param.7) | copy-start | bytes 52
  141.2 503.9 %reduce-scatter.2.cloned.1.call-start = ((), (), s32[]{:S(2)}) async-start(), calls=%async_computation.3 | async-start | bytes 2129920 | tf_op jit(solution)/shard_map/reduce_scatter | solution.py:67
Sparse Core Ops, SparseCore 0:
  10.2 126.2 all-gather.1
  141.3 157.0 all-reduce.2
  420.4 224.7 reduce-scatter.1
where the time goes:
time: 655 us; the launch traced here: 652 us
  waiting for transfers between devices  510 us (78%)
  blocking collectives  106 us (16%)
  between operations  13.8 us (2%)
  other arithmetic  12 us (2%)
  matrix products  8.67 us (1%)
    reduce_scatter x1, waiting for transfers between devices, local(): lax.psum_scatter(jnp.dot(dlogit, head_weight, preferred_element_type=jnp....  224 us
    psum x1, waiting for transfers between devices, local(): logits = lax.psum(partial_logits, 'section')  156 us
    all_gather x1, waiting for transfers between devices, local(): lax.all_gather(hidden, 'vocab', axis=0, tiled=True)  128 us
    psum x1, blocking collectives, local(): dots, norms = lax.psum((dots_part, norms_part), 'vocab')  106 us
  transfers between devices with their start and end apart: 3, of which 3 were waited for; matrix products, arithmetic and copies ran while one was open for 0% of the time, Pallas kernels for 0%

commit v1 on v0

--- a/solution.py
+++ b/solution.py
@@ -1,6 +1,7 @@
 import jax
 import jax.numpy as jnp
 from jax import lax
+from jax.sharding import Mesh
 from jax.sharding import PartitionSpec as P
 
 NSEQ = 8
@@ -11,18 +12,24 @@
 grad_scale = 16.0
 eps_norm = 1e-06
 
+SEC = ("x", "yh")
+VOC = ("z", "yl", "c")
+
 
 def local(hidden, head_weight, lengths, pairing):
     half = NSEQ // 2
+    gathered = lax.all_gather(hidden, ("yl", "c"), axis=0, tiled=True)
+    gathered = lax.all_gather(gathered, "z", axis=0, tiled=True)
     partial_logits = lax.dot_general(
-        lax.all_gather(hidden, "vocab", axis=0, tiled=True),
+        gathered,
         head_weight,
         (((1,), (1,)), ((), ())),
         preferred_element_type=jnp.float32,
     )
     total_rows = partial_logits.shape[0]
     seq_len = total_rows // NSEQ
-    logits = lax.psum(partial_logits, "section")
+    logits = lax.psum_scatter(partial_logits, "x", scatter_dimension=1, tiled=True)
+    logits = lax.psum_scatter(logits, "yh", scatter_dimension=1, tiled=True)
     columns = logits.shape[1]
     soft = jax.nn.softplus(logits)
     act = jnp.log1p(soft)
@@ -37,7 +44,10 @@
         queries, documents, (((1,), (1,)), ((), ())), precision=lax.Precision.HIGHEST
     )
     norms_part = jnp.sum(pooled * pooled, axis=1)
-    dots, norms = lax.psum((dots_part, norms_part), "vocab")
+    stats = (dots_part, norms_part)
+    for axis in ("c", "yl", "yh", "x", "z"):
+        stats = lax.psum(stats, axis)
+    dots, norms = stats
     inv = lax.rsqrt(norms + eps_norm)
     inv_q = inv[:half]
     inv_d = inv[half:]
@@ -64,16 +74,18 @@
     dpooled = jnp.concatenate([dpool_q, dpool_d], axis=0)
     dact = (dpooled[:, None, :] * expo / totals[:, None, :]).reshape(total_rows, columns)
     dlogit = (dact * jax.nn.sigmoid(logits) / (1.0 + soft)).astype(jnp.bfloat16)
-    hidden_grad = lax.psum_scatter(
-        jnp.dot(dlogit, head_weight, preferred_element_type=jnp.float32),
-        "vocab",
-        scatter_dimension=0,
-        tiled=True,
-    )
+    dlogit = lax.all_gather(dlogit, SEC, axis=1, tiled=True)
+    partial_grad = jnp.dot(dlogit, head_weight, preferred_element_type=jnp.float32)
+    hidden_grad = lax.psum_scatter(partial_grad, "z", scatter_dimension=0, tiled=True)
+    hidden_grad = lax.psum_scatter(hidden_grad, ("yl", "c"), scatter_dimension=0, tiled=True)
     return (hidden_grad, loss)
 
 
 def solution(mesh):
-    in_specs = (P("vocab", "section"), P("vocab", "section"), P(), P())
-    out_specs = (P("vocab", "section"), P())
-    return jax.shard_map(local, mesh=mesh, in_specs=in_specs, out_specs=out_specs, check_vma=False)
+    n_sec, n_voc = mesh.devices.shape
+    fine = Mesh(
+        mesh.devices.reshape(n_sec // 2, 2, n_voc // 4, 2, 2), SEC + VOC
+    )
+    in_specs = (P(VOC, SEC), P(VOC, SEC), P(), P())
+    out_specs = (P(VOC, SEC), P())
+    return jax.shard_map(local, mesh=fine, in_specs=in_specs, out_specs=out_specs, check_vma=False)

time: 655 us -> 404 us (0.62)
  waiting for transfers between devices: 510 us -> 312 us
  blocking collectives: 106 us -> 57.5 us
  other arithmetic: 12 us -> 4.75 us
    psum x1 -> x0, waiting for transfers between devices: 156 us -> none  [local(): logits = lax.psum(partial_logits, 'section')]
    reduce_scatter x1 -> x3, waiting for transfers between devices: 224 us -> 152 us  [the longest x1 63.7 us: local(): lax.psum_scatter(partial_grad, 'z', scatter_dimension=0, tiled=True)]
    psum x1 -> x5, blocking collectives: 106 us -> 44.8 us  [local(): stats = lax.psum(stats, axis)]
    unnamed x3 -> x7, waiting for transfers between devices: 0.71 us -> 29.3 us
    all_gather x0 -> x1, blocking collectives: none -> 12.7 us  [local(): gathered = lax.all_gather(hidden, ('yl', 'c'), axis=0, tiled=True)]
    all_gather x1 -> x2, waiting for transfers between devices: 128 us -> 131 us  [the longest x1 69.6 us: local(): dlogit = lax.all_gather(dlogit, SEC, axis=1, tiled=True)]
  transfers between devices with their start and end apart: 3 -> 6, of which waited for: 3 -> 6; matrix products, arithmetic and copies ran while one was open for 0% -> 0% of each run, Pallas kernels for 0% -> 0%
where the time goes in v1:
time: 404 us
  waiting for transfers between devices  312 us (77%)
  blocking collectives  57.5 us (14%)
  between operations  14.2 us (4%)
  matrix products  9.88 us (2%)
  local copies, waits for them, and re-layouts  5.15 us (1%)
  other arithmetic  4.75 us (1%)
    all_gather x1, waiting for transfers between devices, local(): dlogit = lax.all_gather(dlogit, SEC, axis=1, tiled=True)  69.6 us
    reduce_scatter x1, waiting for transfers between devices, local(): lax.psum_scatter(partial_grad, 'z', scatter_dimension=0, tiled=True)  63.7 us
    all_gather x1, waiting for transfers between devices, local(): gathered = lax.all_gather(gathered, 'z', axis=0, tiled=True)  60.9 us
    reduce_scatter x1, waiting for transfers between devices, local(): lax.psum_scatter(partial_logits, 'x', scatter_dimension=1, tiled=True)  52.5 us
    psum x5, blocking collectives, local(): stats = lax.psum(stats, axis)  44.8 us
    reduce_scatter x1, waiting for transfers between devices, local(): lax.psum_scatter(hidden_grad, ('yl', 'c'), scatter_dimension=0, tiled=True)  35.8 us
    unnamed x7, waiting for transfers between devices  29.3 us
    all_gather x1, blocking collectives, local(): gathered = lax.all_gather(hidden, ('yl', 'c'), axis=0, tiled=True)  12.7 us
  transfers between devices with their start and end apart: 6, of which 6 were waited for; matrix products, arithmetic and copies ran while one was open for 0% of the time, Pallas kernels for 0%

profile of v1, /device:TPU:1, one launch (start us, length us, event | category | flops | bytes accessed | tf_op | source)
XLA Modules:
  0.0 403.5 jit_solution(7920873863289771938)
XLA Ops:
  7.2 0.0 copy-start
  7.2 0.0 all-gather.3.cloned.1.call-start
  7.2 12.7 %all_gather.9 = bf16[32,1024]{1,0:T(8,128)(2,1)} all-gather(bf16[8,1024]{1,0:T(8,128)(2,1)} %param.4), channel_id=1, replica_groups=mesh['x'=4,'yh'=2,'z'=16,'yl'=2,'c'=2] {'yl','c'}, dimensions={0}, use_global_device_ids=true | all-gather | bytes 81920 | tf_op jit(solution)/shard_map/all_gather | solution.py:21
  20.0 0.0 all-gather.3.cloned.1.call-update
  20.0 0.0 reduce-scatter.7.cloned.1.call-start
  20.0 60.9 %all-gather.3.cloned.1.call-done = bf16[512,1024]{1,0:T(8,128)(2,1)} async-done(((bf16[32,1024]{1,0:T(8,128)(2,1)}), bf16[512,1024]{1,0:T(8,128)(2,1)}) %all-gather.3.cloned.1.call-update) | async-done | bytes 1048592 | tf_op jit(solution)/shard_map/all_gather | solution.py:22
  81.0 0.0 copy-done
  81.0 4.7 %fusion.17 = f32[512,1536]{1,0:T(8,128)} fusion(bf16[512,1024]{1,0:T(8,128)(2,1)} %all-gather.3.cloned.1.call-done, bf16[1536,1024]{1,0:T(8,128)(2,1)S(1)} %copy-done), kind=kOutput, calls=%fused_computation.46 | convolution fusion | flops 1610612736 | bytes 7340032 | tf_op jit(solution)/shard_map/dot_general | solution.py:23
  85.7 0.0 copy-start.1
  85.7 0.0 reduce-scatter.7.cloned.1.call-update
  85.7 0.0 reduce-scatter.13.cloned.1.call-start
  85.8 52.5 %reduce-scatter.7.cloned.1.call-done = f32[512,384]{1,0:T(8,128)} async-done(((f32[512,1536]{1,0:T(8,128)}), f32[512,384]{1,0:T(8,128)}) %reduce-scatter.7.cloned.1.call-update) | async-done | bytes 786448 | tf_op jit(solution)/shard_map/reduce_scatter | solution.py:31
  138.3 2.3 copy.7
  140.6 0.0 reduce-scatter.13.cloned.1.call-update
  140.6 0.0 all-gather.5.cloned.1.call-start
  140.6 0.0 copy-done.1
  140.6 0.1 fusion.3
  140.7 0.1 reshape.50
  140.8 29.2 %reduce-scatter.13.cloned.1.call-done = f32[192,512]{1,0:T(8,128)} async-done(((f32[384,512]{1,0:T(8,128)}), f32[192,512]{1,0:T(8,128)}) %reduce-scatter.13.cloned.1.call-update) | async-done | bytes 393232
  170.0 2.0 copy.8
  172.0 1.6 multiply_reduce_fusion
  173.6 0.1 multiply_reduce_fusion.1
  173.7 0.1 fusion.5
  173.9 2.8 all-reduce.2
  176.6 3.8 all-reduce.3
  180.4 5.3 %all-reduce.4 = (f32[8]{0:T(128)S(1)}, f32[4,4]{1,0:T(4,128)S(1)}) all-reduce(f32[8]{0:T(128)S(1)} %get-tuple-element.11, f32[4,4]{1,0:T(4,128)S(1)} %get-tuple-element.12), channel_id=1, replica_groups=mesh['x'=4,'yh'=2,'z'=16,'yl'=2,'c'=2] {'yh'}, use_global_device_ids=true, to_apply=%region_11.12 | all-reduce | flops 24 | bytes 192 | tf_op jit(solution)/shard_map/psum | solution.py:49
  185.7 8.7 %all-reduce.1 = (f32[8]{0:T(128)S(1)}, f32[4,4]{1,0:T(4,128)S(1)}) all-reduce(f32[8]{0:T(128)S(1)} %get-tuple-element.13, f32[4,4]{1,0:T(4,128)S(1)} %get-tuple-element.14), channel_id=1, replica_groups=mesh['x'=4,'yh'=2,'z'=16,'yl'=2,'c'=2] {'x'}, use_global_device_ids=true, to_apply=%region_12.13 | all-reduce | flops 24 | bytes 192 | tf_op jit(solution)/shard_map/psum | solution.py:49
  194.4 24.3 %all-reduce = (f32[8]{0:T(128)S(1)}, f32[4,4]{1,0:T(4,128)S(1)}) all-reduce(f32[8]{0:T(128)S(1)} %get-tuple-element.7, f32[4,4]{1,0:T(4,128)S(1)} %get-tuple-element.8), channel_id=1, replica_groups=mesh['x'=4,'yh'=2,'z'=16,'yl'=2,'c'=2] {'z'}, use_global_device_ids=true, to_apply=%region_13.14 | all-reduce | flops 24 | bytes 192 | tf_op jit(solution)/shard_map/psum | solution.py:49
  218.7 0.1 broadcast_multiply_fusion.2
  218.7 0.2 exponential_reduce_fusion
  218.9 0.0 copy-done.2
  218.9 0.2 multiply_reduce_fusion.3
  219.2 0.1 multiply_multiply_fusion.5
  219.2 0.1 slice_multiply_fusion.1
  219.3 0.2 convolution_add_fusion.1
  219.5 0.3 convolution_add_fusion
  219.8 1.7 fusion.2
  221.5 0.8 copy.6
  222.3 0.0 all-gather.5.cloned.1.call-update
  222.3 0.0 reduce-scatter.9.cloned.1.call-start
  222.4 69.6 %all-gather.5.cloned.1.call-done = bf16[512,1536]{0,1:T(8,128)(2,1)} async-done(((bf16[512,192]{0,1:T(8,128)(2,1)}), bf16[512,1536]{0,1:T(8,128)(2,1)}) %all-gather.5.cloned.1.call-update) | async-done | bytes 1572880 | tf_op jit(solution)/shard_map/all_gather | solution.py:77
  292.0 4.6 %fusion.18 = f32[512,1024]{1,0:T(8,128)} fusion(bf16[512,1536]{0,1:T(8,128)(2,1)} %all-gather.5.cloned.1.call-done, bf16[1536,1024]{1,0:T(8,128)(2,1)S(1)} %copy-done), kind=kOutput, calls=%fused_computation.47 | convolution fusion | flops 1610612736 | bytes 6815744 | tf_op jit(solution)/shard_map/dot_general | solution.py:78
  296.5 0.0 reduce-scatter.9.cloned.1.call-update
  296.6 0.0 reduce-scatter.11.cloned.1.call-start
  296.6 63.7 %reduce-scatter.9.cloned.1.call-done = f32[32,1024]{1,0:T(8,128)} async-done(((f32[512,1024]{1,0:T(8,128)}), f32[32,1024]{1,0:T(8,128)}) %reduce-scatter.9.cloned.1.call-update) | async-done | bytes 131088 | tf_op jit(solution)/shard_map/reduce_scatter | solution.py:79
  360.3 0.0 reduce-scatter.11.cloned.1.call-update
  360.3 0.6 subtract_reduce_fusion
  360.9 35.8 %reduce-scatter.11.cloned.1.call-done = f32[8,1024]{1,0:T(8,128)} async-done(((f32[32,1024]{1,0:T(8,128)}), f32[8,1024]{1,0:T(8,128)}) %reduce-scatter.11.cloned.1.call-update) | async-done | bytes 32784 | tf_op jit(solution)/shard_map/reduce_scatter | solution.py:80
  (4 shorter events, 0.0 us)
Async XLA Ops:
  7.2 73.8 %copy-start = (bf16[1536,1024]{1,0:T(8,128)(2,1)S(1)}, bf16[1536,1024]{1,0:T(8,128)(2,1)}, u32[]{:S(2)}) copy-start(bf16[1536,1024]{1,0:T(8,128)(2,1)} %param.5) | copy-start | bytes 9437188
  7.2 73.8 %all-gather.3.cloned.1.call-start = ((), (), s32[]{:S(2)}) async-start(), calls=%async_computation.4 | async-start | bytes 1114112 | tf_op jit(solution)/shard_map/all_gather | solution.py:22
  20.0 118.3 %reduce-scatter.7.cloned.1.call-start = ((), (), s32[]{:S(2)}) async-start(), calls=%async_computation.5 | async-start | bytes 3932160 | tf_op jit(solution)/shard_map/reduce_scatter | solution.py:31
  85.7 54.9 %copy-start.1 = (s32[8]{0:T(128)S(1)}, s32[8]{0:T(128)}, u32[]{:S(2)}) copy-start(s32[8]{0:T(128)} %param.6) | copy-start | bytes 100
  85.7 133.2 %copy-start.2 = (s32[4]{0:T(128)S(1)}, s32[4]{0:T(128)}, u32[]{:S(2)}) copy-start(s32[4]{0:T(128)} %param.7) | copy-start | bytes 52
  85.7 84.3 %reduce-scatter.13.cloned.1.call-start = ((), (), s32[]{:S(2)}) async-start(), calls=%async_computation.9 | async-start | bytes 1179648
  140.6 151.4 %all-gather.5.cloned.1.call-start = ((), (), s32[]{:S(2)}) async-start(), calls=%async_computation.6 | async-start | bytes 1769472 | tf_op jit(solution)/shard_map/all_gather | solution.py:77
  222.3 137.9 %reduce-scatter.9.cloned.1.call-start = ((), (), s32[]{:S(2)}) async-start(), calls=%async_computation.7 | async-start | bytes 2228224 | tf_op jit(solution)/shard_map/reduce_scatter | solution.py:79
  296.6 100.1 %reduce-scatter.11.cloned.1.call-start = ((), (), s32[]{:S(2)}) async-start(), calls=%async_computation.8 | async-start | bytes 163840 | tf_op jit(solution)/shard_map/reduce_scatter | solution.py:80
Sparse Core Ops, SparseCore 0:
  20.1 60.8 all-gather.2
  85.9 52.3 reduce-scatter.6
  141.1 28.9 reduce-scatter.12
  222.5 69.4 all-gather.4
  296.7 63.5 reduce-scatter.8
  363.7 32.9 reduce-scatter.10

commit v2 on v1

--- a/solution.py
+++ b/solution.py
@@ -16,6 +16,57 @@
 VOC = ("z", "yl", "c")
 
 
+def _shift(v, axis, n, k):
+    return lax.ppermute(v, axis, [(i, (i + k) % n) for i in range(n)])
+
+
+def _ring_reduce_scatter(x, axis, n):
+    me = lax.axis_index(axis)
+    blocks = jnp.stack(jnp.split(x, n, axis=1))
+    half = blocks.shape[-1] // 2
+    fwd, bwd = blocks[..., :half], blocks[..., half:]
+
+    def block(arr, k):
+        return lax.dynamic_index_in_dim(arr, k % n, 0, keepdims=False)
+
+    acc_f = block(fwd, me - 1)
+    acc_b = block(bwd, me + 1)
+    for step in range(1, n):
+        acc_f = _shift(acc_f, axis, n, 1) + block(fwd, me - 1 - step)
+        acc_b = _shift(acc_b, axis, n, -1) + block(bwd, me + 1 + step)
+    return jnp.concatenate([acc_f, acc_b], axis=1)
+
+
+def _pair_reduce_scatter(x, axis):
+    lo, hi = jnp.split(x, 2, axis=1)
+    first = lax.axis_index(axis) == 0
+    keep = jnp.where(first, lo, hi)
+    send = jnp.where(first, hi, lo)
+    return keep + lax.ppermute(send, axis, [(0, 1), (1, 0)])
+
+
+def _ring_gather_matmul(x, weight, axis, n):
+    me = lax.axis_index(axis)
+    rows = weight.shape[0] // n
+
+    def term(v, owner):
+        w = lax.dynamic_slice_in_dim(weight, (owner % n) * rows, rows, axis=0)
+        return jnp.dot(v, w, preferred_element_type=jnp.float32)
+
+    total = term(x, me)
+    cur_f = cur_b = x
+    n_f = n // 2
+    n_b = n - 1 - n_f
+    for step in range(max(n_f, n_b)):
+        if step < n_f:
+            cur_f = _shift(cur_f, axis, n, 1)
+            total = total + term(cur_f, me - 1 - step)
+        if step < n_b:
+            cur_b = _shift(cur_b, axis, n, -1)
+            total = total + term(cur_b, me + 1 + step)
+    return total
+
+
 def local(hidden, head_weight, lengths, pairing):
     half = NSEQ // 2
     gathered = lax.all_gather(hidden, ("yl", "c"), axis=0, tiled=True)
@@ -28,8 +79,9 @@
     )
     total_rows = partial_logits.shape[0]
     seq_len = total_rows // NSEQ
-    logits = lax.psum_scatter(partial_logits, "x", scatter_dimension=1, tiled=True)
-    logits = lax.psum_scatter(logits, "yh", scatter_dimension=1, tiled=True)
+    n_x = lax.axis_size("x")
+    logits = _ring_reduce_scatter(partial_logits, "x", n_x)
+    logits = _pair_reduce_scatter(logits, "yh")
     columns = logits.shape[1]
     soft = jax.nn.softplus(logits)
     act = jnp.log1p(soft)
@@ -74,8 +126,8 @@
     dpooled = jnp.concatenate([dpool_q, dpool_d], axis=0)
     dact = (dpooled[:, None, :] * expo / totals[:, None, :]).reshape(total_rows, columns)
     dlogit = (dact * jax.nn.sigmoid(logits) / (1.0 + soft)).astype(jnp.bfloat16)
-    dlogit = lax.all_gather(dlogit, SEC, axis=1, tiled=True)
-    partial_grad = jnp.dot(dlogit, head_weight, preferred_element_type=jnp.float32)
+    dlogit = lax.all_gather(dlogit, "yh", axis=1, tiled=True)
+    partial_grad = _ring_gather_matmul(dlogit, head_weight, "x", n_x)
     hidden_grad = lax.psum_scatter(partial_grad, "z", scatter_dimension=0, tiled=True)
     hidden_grad = lax.psum_scatter(hidden_grad, ("yl", "c"), scatter_dimension=0, tiled=True)
     return (hidden_grad, loss)

time: 404 us -> 361 us (0.89)
  waiting for transfers between devices: 312 us -> 190 us
  starting transfers between devices: 0.25 us -> 32.5 us
  local copies, waits for them, and re-layouts: 5.15 us -> 23.4 us
  blocking collectives: 57.5 us -> 73 us
  other arithmetic: 4.75 us -> 17.9 us
    all_gather x1 -> x0, waiting for transfers between devices: 69.6 us -> none  [local(): dlogit = lax.all_gather(dlogit, SEC, axis=1, tiled=True)]
    reduce_scatter x1 -> x0, waiting for transfers between devices: 52.5 us -> none  [local(): lax.psum_scatter(partial_logits, 'x', scatter_dimension=1, tiled=True)]
    ppermute x0 -> x10, starting transfers between devices: none -> 32.4 us  [the longest x9 27.8 us: _shift(): return lax.ppermute(v, axis, [(i, (i + k) % n) for i in range(n)])]
    unnamed x7 -> x3, waiting for transfers between devices: 29.3 us -> 0.05 us
    ppermute x0 -> x10, waiting for transfers between devices: none -> 22.3 us  [the longest x9 16.8 us: _shift(): return lax.ppermute(v, axis, [(i, (i + k) % n) for i in range(n)])]
    dynamic_slice x0 -> x9, local copies, waits for them, and re-layouts: none -> 15.6 us  [block(): return lax.dynamic_index_in_dim(arr, k % n, 0, keepdims=False)]
    psum x5, blocking collectives: 44.8 us -> 53.5 us  [local(): stats = lax.psum(stats, axis)]
    add x0 -> x4, other arithmetic: none -> 7.48 us  [the longest x2 3.87 us: _ring_reduce_scatter(): acc_b = _shift(acc_b, axis, n, -1) + block(bwd, me + 1 + step)]
  transfers between devices with their start and end apart: 6 -> 13, of which waited for: 6 -> 7; matrix products, arithmetic and copies ran while one was open for 0% -> 6% of each run, Pallas kernels for 0% -> 0%
where the time goes in v2:
time: 361 us; the launch traced here: 360 us
  waiting for transfers between devices  190 us (53%)
  blocking collectives  73 us (20%)
  starting transfers between devices  32.5 us (9%)
  local copies, waits for them, and re-layouts  23.4 us (6%)
  other arithmetic  17.9 us (5%)
  between operations  14.2 us (4%)
  matrix products  8.92 us (2%)
    reduce_scatter x1, waiting for transfers between devices, local(): lax.psum_scatter(partial_grad, 'z', scatter_dimension=0, tiled=True)  70.8 us
    all_gather x1, waiting for transfers between devices, local(): gathered = lax.all_gather(gathered, 'z', axis=0, tiled=True)  60.8 us
    psum x5, blocking collectives, local(): stats = lax.psum(stats, axis)  53.5 us
    reduce_scatter x1, waiting for transfers between devices, local(): lax.psum_scatter(hidden_grad, ('yl', 'c'), scatter_dimension=0, tiled=True)  35.9 us
    ppermute x9, starting transfers between devices, _shift(): return lax.ppermute(v, axis, [(i, (i + k) % n) for i in range(n)])  27.8 us
    ppermute x9, waiting for transfers between devices, _shift(): return lax.ppermute(v, axis, [(i, (i + k) % n) for i in range(n)])  16.8 us
    dynamic_slice x9, local copies, waits for them, and re-layouts, block(): return lax.dynamic_index_in_dim(arr, k % n, 0, keepdims=False)  15.6 us
    all_gather x1, blocking collectives, local(): gathered = lax.all_gather(hidden, ('yl', 'c'), axis=0, tiled=True)  12.7 us
  transfers between devices with their start and end apart: 13, of which 7 were waited for; matrix products, arithmetic and copies ran while one was open for 6% of the time, Pallas kernels for 0%

profile of v2, /device:TPU:1, one launch (start us, length us, event | category | flops | bytes accessed | tf_op | source)
XLA Modules:
  0.0 359.8 jit_solution(16309813369068968131)
XLA Ops:
  7.2 12.7 %all_gather.9 = bf16[32,1024]{1,0:T(8,128)(2,1)} all-gather(bf16[8,1024]{1,0:T(8,128)(2,1)} %param.4), channel_id=1, replica_groups=mesh['x'=4,'yh'=2,'z'=16,'yl'=2,'c'=2] {'yl','c'}, dimensions={0}, use_global_device_ids=true | all-gather | bytes 81920 | tf_op jit(solution)/shard_map/all_gather | solution.py:72
  20.2 60.8 %all-gather.2.cloned.1.call-done = bf16[512,1024]{1,0:T(8,128)(2,1)} async-done(((bf16[32,1024]{1,0:T(8,128)(2,1)}), bf16[512,1024]{1,0:T(8,128)(2,1)}) %all-gather.2.cloned.1.call-update) | async-done | bytes 1048592 | tf_op jit(solution)/shard_map/all_gather | solution.py:73
  81.0 3.0 fusion.26
  85.2 2.0 constant_dynamic-slice_fusion
  87.2 2.0 copy.12
  89.2 4.3 %collective-permute-start.3 = (f32[512,192]{0,1:T(8,128)}, f32[512,192]{0,1:T(8,128)}, u32[]{:S(2)}, u32[]{:S(2)}) collective-permute-start(f32[512,192]{0,1:T(8,128)} %bitcast.8), channel_id=1, source_target_pairs={{0,384},{128,0},{256,128},{384,256},{1,385},{129,1},{257,129},{385... | collective-permute-start | bytes 1179656 | tf_op jit(solution)/shard_map/ppermute | solution.py:20
  93.5 2.0 copy.8
  95.5 1.9 collective-permute-start
  97.4 2.0 copy.13
  99.4 1.2 copy.9
  100.6 1.9 bitcast_add_fusion.2
  102.6 4.6 %collective-permute-start.4 = (f32[512,192]{0,1:T(8,128)}, f32[512,192]{0,1:T(8,128)}, u32[]{:S(2)}, u32[]{:S(2)}) collective-permute-start(f32[512,192]{0,1:T(8,128)} %bitcast_add_fusion.2), channel_id=1, source_target_pairs={{0,384},{128,0},{256,128},{384,256},{1,385},{129,1},{257,129},{385... | collective-permute-start | bytes 1179656 | tf_op jit(solution)/shard_map/ppermute | solution.py:20
  107.1 1.8 bitcast_add_fusion.5
  109.0 1.9 collective-permute-start.1
  110.9 2.0 copy.14
  112.9 1.2 copy.10
  114.1 1.9 bitcast_add_fusion.1
  116.0 4.6 %collective-permute-start.5 = (f32[512,192]{0,1:T(8,128)}, f32[512,192]{0,1:T(8,128)}, u32[]{:S(2)}, u32[]{:S(2)}) collective-permute-start(f32[512,192]{0,1:T(8,128)} %bitcast_add_fusion.1), channel_id=1, source_target_pairs={{0,384},{128,0},{256,128},{384,256},{1,385},{129,1},{257,129},{385... | collective-permute-start | bytes 1179656 | tf_op jit(solution)/shard_map/ppermute | solution.py:20
  120.6 1.8 bitcast_add_fusion.4
  122.4 1.9 collective-permute-start.2
  124.3 1.2 copy.11
  125.6 2.0 copy.15
  127.5 7.5 %collective-permute-done.2 = f32[512,192]{0,1:T(8,128)} collective-permute-done((f32[512,192]{0,1:T(8,128)}, f32[512,192]{0,1:T(8,128)}, u32[]{:S(2)}, u32[]{:S(2)}) %collective-permute-start.2) | collective-permute-done | bytes 393248 | tf_op jit(solution)/shard_map/ppermute | solution.py:20
  135.1 2.1 broadcast_select_fusion
  137.2 4.6 %collective-permute-start.6 = (f32[512,192]{0,1:T(8,128)}, f32[512,192]{0,1:T(8,128)}, u32[]{:S(2)}, u32[]{:S(2)}) collective-permute-start(f32[512,192]{0,1:T(8,128)} %broadcast_select_fusion), channel_id=1, source_target_pairs={{0,64},{64,0},{1,65},{65,1},{2,66},{66,2},{3,67},{67,3},{4,68},{68... | collective-permute-start | bytes 1179656 | tf_op jit(solution)/shard_map/ppermute | solution.py:45
  142.0 5.5 %collective-permute-done.6 = f32[512,192]{0,1:T(8,128)} collective-permute-done((f32[512,192]{0,1:T(8,128)}, f32[512,192]{0,1:T(8,128)}, u32[]{:S(2)}, u32[]{:S(2)}) %collective-permute-start.6) | collective-permute-done | bytes 393248 | tf_op jit(solution)/shard_map/ppermute | solution.py:45
  147.5 2.6 multiply_exponential_fusion
  150.2 2.0 copy.16
  152.2 1.2 multiply_reduce_fusion
  153.6 15.3 %all-reduce.2 = (f32[8]{0:T(128)S(1)}, f32[4,4]{1,0:T(4,128)S(1)}) all-reduce(f32[8]{0:T(128)S(1)} %get-tuple-element.32, f32[4,4]{1,0:T(4,128)S(1)} %fusion.9), channel_id=1, replica_groups=mesh['x'=4,'yh'=2,'z'=16,'yl'=2,'c'=2] {'c'}, use_global_device_ids=true, to_apply=%region_7.8 | all-reduce | flops 24 | bytes 192 | tf_op jit(solution)/shard_map/psum | solution.py:101
  168.9 3.8 %all-reduce.3 = (f32[8]{0:T(128)S(1)}, f32[4,4]{1,0:T(4,128)S(1)}) all-reduce(f32[8]{0:T(128)S(1)} %get-tuple-element.9, f32[4,4]{1,0:T(4,128)S(1)} %get-tuple-element.10), channel_id=1, replica_groups=mesh['x'=4,'yh'=2,'z'=16,'yl'=2,'c'=2] {'yl'}, use_global_device_ids=true, to_apply=%region_8.9 | all-reduce | flops 24 | bytes 192 | tf_op jit(solution)/shard_map/psum | solution.py:101
  172.7 5.3 %all-reduce.4 = (f32[8]{0:T(128)S(1)}, f32[4,4]{1,0:T(4,128)S(1)}) all-reduce(f32[8]{0:T(128)S(1)} %get-tuple-element.11, f32[4,4]{1,0:T(4,128)S(1)} %get-tuple-element.12), channel_id=1, replica_groups=mesh['x'=4,'yh'=2,'z'=16,'yl'=2,'c'=2] {'yh'}, use_global_device_ids=true, to_apply=%region_9.10 | all-reduce | flops 24 | bytes 192 | tf_op jit(solution)/shard_map/psum | solution.py:101
  177.9 6.0 %all-reduce.1 = (f32[8]{0:T(128)S(1)}, f32[4,4]{1,0:T(4,128)S(1)}) all-reduce(f32[8]{0:T(128)S(1)} %get-tuple-element.13, f32[4,4]{1,0:T(4,128)S(1)} %get-tuple-element.14), channel_id=1, replica_groups=mesh['x'=4,'yh'=2,'z'=16,'yl'=2,'c'=2] {'x'}, use_global_device_ids=true, to_apply=%region_10.11 | all-reduce | flops 24 | bytes 192 | tf_op jit(solution)/shard_map/psum | solution.py:101
  183.9 23.2 %all-reduce = (f32[8]{0:T(128)S(1)}, f32[4,4]{1,0:T(4,128)S(1)}) all-reduce(f32[8]{0:T(128)S(1)} %get-tuple-element.7, f32[4,4]{1,0:T(4,128)S(1)} %get-tuple-element.8), channel_id=1, replica_groups=mesh['x'=4,'yh'=2,'z'=16,'yl'=2,'c'=2] {'z'}, use_global_device_ids=true, to_apply=%region_11.12 | all-reduce | flops 24 | bytes 192 | tf_op jit(solution)/shard_map/psum | solution.py:101
  207.4 1.4 multiply_reduce_fusion.3
  210.3 1.2 copy.17
  212.3 2.0 copy.18
  214.3 1.6 divide_convert_fusion
  216.0 6.7 %all_gather.11 = bf16[512,384]{0,1:T(8,128)(2,1)S(1)} all-gather(bf16[512,192]{0,1:T(8,128)(2,1)S(1)} %divide_convert_fusion), channel_id=1, replica_groups=mesh['x'=4,'yh'=2,'z'=16,'yl'=2,'c'=2] {'yh'}, dimensions={1}, use_global_device_ids=true | all-gather | bytes 589824 | tf_op jit(solution)/shard_map/all_gather | solution.py:129
  222.7 3.3 collective-permute-start.7
  226.1 3.1 collective-permute-start.8
  229.9 2.6 collective-permute-done.7
  232.5 2.1 collective-permute-start.9
  234.6 1.7 fusion.3
  237.1 6.6 %collective-permute-done.9 = bf16[512,384]{0,1:T(8,128)(2,1)S(1)} collective-permute-done((bf16[512,384]{0,1:T(8,128)(2,1)}, bf16[512,384]{0,1:T(8,128)(2,1)S(1)}, u32[]{:S(2)}, u32[]{:S(2)}) %collective-permute-start.9) | collective-permute-done | bytes 393248 | tf_op jit(solution)/shard_map/ppermute | solution.py:20
  243.8 2.1 add_add_fusion
  245.9 70.8 %reduce-scatter.3.cloned.1.call-done = f32[32,1024]{1,0:T(8,128)} async-done(((f32[512,1024]{1,0:T(8,128)}), f32[32,1024]{1,0:T(8,128)}) %reduce-scatter.3.cloned.1.call-update) | async-done | bytes 131088 | tf_op jit(solution)/shard_map/reduce_scatter | solution.py:131
  317.4 35.9 %reduce-scatter.5.cloned.1.call-done = f32[8,1024]{1,0:T(8,128)} async-done(((f32[32,1024]{1,0:T(8,128)}), f32[8,1024]{1,0:T(8,128)}) %reduce-scatter.5.cloned.1.call-update) | async-done | bytes 32784 | tf_op jit(solution)/shard_map/reduce_scatter | solution.py:132
  (44 shorter events, 6.4 us)
Async XLA Ops:
  7.2 73.8 %copy-start = (bf16[1536,1024]{1,0:T(8,128)(2,1)S(1)}, bf16[1536,1024]{1,0:T(8,128)(2,1)}, u32[]{:S(2)}) copy-start(bf16[1536,1024]{1,0:T(8,128)(2,1)} %param.5) | copy-start | bytes 9437188
  7.2 73.8 %all-gather.2.cloned.1.call-start = ((), (), s32[]{:S(2)}) async-start(), calls=%async_computation.2 | async-start | bytes 1114112 | tf_op jit(solution)/shard_map/all_gather | solution.py:73
  20.0 296.8 %reduce-scatter.3.cloned.1.call-start = ((), (), s32[]{:S(2)}) async-start(), calls=%async_computation.3 | async-start | bytes 2228224 | tf_op jit(solution)/shard_map/reduce_scatter | solution.py:131
  89.2 11.4 %collective-permute-start.3 = (f32[512,192]{0,1:T(8,128)}, f32[512,192]{0,1:T(8,128)}, u32[]{:S(2)}, u32[]{:S(2)}) collective-permute-start(f32[512,192]{0,1:T(8,128)} %bitcast.8), channel_id=1, source_target_pairs={{0,384},{128,0},{256,128},{384,256},{1,385},{129,1},{257,129},{385... | collective-permute-start | bytes 1179656 | tf_op jit(solution)/shard_map/ppermute | solution.py:20
  95.5 11.7 %collective-permute-start = (f32[512,192]{0,1:T(8,128)}, f32[512,192]{0,1:T(8,128)}, u32[]{:S(2)}, u32[]{:S(2)}) collective-permute-start(f32[512,192]{0,1:T(8,128)} %bitcast.4), channel_id=1, source_target_pairs={{0,128},{128,256},{256,384},{384,0},{1,129},{129,257},{257,385},{3... | collective-permute-start | bytes 1179656 | tf_op jit(solution)/shard_map/ppermute | solution.py:20
  102.6 11.5 %collective-permute-start.4 = (f32[512,192]{0,1:T(8,128)}, f32[512,192]{0,1:T(8,128)}, u32[]{:S(2)}, u32[]{:S(2)}) collective-permute-start(f32[512,192]{0,1:T(8,128)} %bitcast_add_fusion.2), channel_id=1, source_target_pairs={{0,384},{128,0},{256,128},{384,256},{1,385},{129,1},{257,129},{385... | collective-permute-start | bytes 1179656 | tf_op jit(solution)/shard_map/ppermute | solution.py:20
  109.0 11.6 %collective-permute-start.1 = (f32[512,192]{0,1:T(8,128)}, f32[512,192]{0,1:T(8,128)}, u32[]{:S(2)}, u32[]{:S(2)}) collective-permute-start(f32[512,192]{0,1:T(8,128)} %bitcast_add_fusion.5), channel_id=1, source_target_pairs={{0,128},{128,256},{256,384},{384,0},{1,129},{129,257},{257,385},{3... | collective-permute-start | bytes 1179656 | tf_op jit(solution)/shard_map/ppermute | solution.py:20
  114.1 27.8 %copy-start.3 = (s32[8]{0:T(128)S(1)}, s32[8]{0:T(128)}, u32[]{:S(2)}) copy-start(s32[8]{0:T(128)} %param.6) | copy-start | bytes 100
  116.0 11.5 %collective-permute-start.5 = (f32[512,192]{0,1:T(8,128)}, f32[512,192]{0,1:T(8,128)}, u32[]{:S(2)}, u32[]{:S(2)}) collective-permute-start(f32[512,192]{0,1:T(8,128)} %bitcast_add_fusion.1), channel_id=1, source_target_pairs={{0,384},{128,0},{256,128},{384,256},{1,385},{129,1},{257,129},{385... | collective-permute-start | bytes 1179656 | tf_op jit(solution)/shard_map/ppermute | solution.py:20
  122.4 12.7 %collective-permute-start.2 = (f32[512,192]{0,1:T(8,128)}, f32[512,192]{0,1:T(8,128)}, u32[]{:S(2)}, u32[]{:S(2)}) collective-permute-start(f32[512,192]{0,1:T(8,128)} %bitcast_add_fusion.4), channel_id=1, source_target_pairs={{0,128},{128,256},{256,384},{384,0},{1,129},{129,257},{257,385},{3... | collective-permute-start | bytes 1179656 | tf_op jit(solution)/shard_map/ppermute | solution.py:20
  137.2 10.3 %collective-permute-start.6 = (f32[512,192]{0,1:T(8,128)}, f32[512,192]{0,1:T(8,128)}, u32[]{:S(2)}, u32[]{:S(2)}) collective-permute-start(f32[512,192]{0,1:T(8,128)} %broadcast_select_fusion), channel_id=1, source_target_pairs={{0,64},{64,0},{1,65},{65,1},{2,66},{66,2},{3,67},{67,3},{4,68},{68... | collective-permute-start | bytes 1179656 | tf_op jit(solution)/shard_map/ppermute | solution.py:45
  207.4 2.9 copy-start.1
  222.7 9.8 %collective-permute-start.7 = (bf16[512,384]{0,1:T(8,128)(2,1)S(1)}, bf16[512,384]{0,1:T(8,128)(2,1)}, u32[]{:S(2)}, u32[]{:S(2)}) collective-permute-start(bf16[512,384]{0,1:T(8,128)(2,1)S(1)} %all_gather.11), channel_id=1, source_target_pairs={{0,128},{128,256},{256,384},{384,0},{1,129},{129,257},{257,385},{3... | collective-permute-start | bytes 1179656 | tf_op jit(solution)/shard_map/ppermute | solution.py:20
  226.1 10.3 %collective-permute-start.8 = (bf16[512,384]{0,1:T(8,128)(2,1)S(1)}, bf16[512,384]{0,1:T(8,128)(2,1)S(1)}, u32[]{:S(2)}, u32[]{:S(2)}) collective-permute-start(bf16[512,384]{0,1:T(8,128)(2,1)S(1)} %all_gather.11), channel_id=1, source_target_pairs={{0,384},{128,0},{256,128},{384,256},{1,385},{129,1},{257,129},{385... | collective-permute-start | bytes 1179656 | tf_op jit(solution)/shard_map/ppermute | solution.py:20
  232.5 11.3 %collective-permute-start.9 = (bf16[512,384]{0,1:T(8,128)(2,1)}, bf16[512,384]{0,1:T(8,128)(2,1)S(1)}, u32[]{:S(2)}, u32[]{:S(2)}) collective-permute-start(bf16[512,384]{0,1:T(8,128)(2,1)} %collective-permute-done.7), channel_id=1, source_target_pairs={{0,128},{128,256},{256,384},{384,0},{1,129},{129,257},{257,385},{3... | collective-permute-start | bytes 1179656 | tf_op jit(solution)/shard_map/ppermute | solution.py:20
  237.1 79.7 %copy-start.2 = (f32[4]{0:T(128)S(1)}, f32[4]{0:T(128)}, u32[]{:S(2)}) copy-start(f32[4]{0:T(128)} %copy-done.1) | copy-start | bytes 52
  237.1 79.7 %copy-start.4 = (f32[4]{0:T(128)S(1)}, f32[4]{0:T(128)}, u32[]{:S(2)}) copy-start(f32[4]{0:T(128)} %get-tuple-element.4) | copy-start | bytes 52
  245.9 107.4 %reduce-scatter.5.cloned.1.call-start = ((), (), s32[]{:S(2)}) async-start(), calls=%async_computation.4 | async-start | bytes 163840 | tf_op jit(solution)/shard_map/reduce_scatter | solution.py:132
Sparse Core Ops, SparseCore 0:
  20.1 60.8 all-gather.1
  246.0 70.7 reduce-scatter.2
  320.2 33.0 reduce-scatter.4

commit v3 on v2

--- a/solution.py
+++ b/solution.py
@@ -20,25 +20,27 @@
     return lax.ppermute(v, axis, [(i, (i + k) % n) for i in range(n)])
 
 
-def _ring_reduce_scatter(x, axis, n):
+def _ring_matmul_reduce_scatter(lhs, weight, axis, n):
     me = lax.axis_index(axis)
-    blocks = jnp.stack(jnp.split(x, n, axis=1))
-    half = blocks.shape[-1] // 2
-    fwd, bwd = blocks[..., :half], blocks[..., half:]
+    rows = weight.shape[0] // n
+    half = rows // 2
 
-    def block(arr, k):
-        return lax.dynamic_index_in_dim(arr, k % n, 0, keepdims=False)
+    def term(k, offset):
+        w = lax.dynamic_slice_in_dim(weight, (k % n) * rows + offset, half, axis=0)
+        return lax.dot_general(
+            lhs, w, (((1,), (1,)), ((), ())), preferred_element_type=jnp.float32
+        )
 
-    acc_f = block(fwd, me - 1)
-    acc_b = block(bwd, me + 1)
+    acc_f = term(me - 1, 0)
+    acc_b = term(me + 1, half)
     for step in range(1, n):
-        acc_f = _shift(acc_f, axis, n, 1) + block(fwd, me - 1 - step)
-        acc_b = _shift(acc_b, axis, n, -1) + block(bwd, me + 1 + step)
+        acc_f = _shift(acc_f, axis, n, 1) + term(me - 1 - step, 0)
+        acc_b = _shift(acc_b, axis, n, -1) + term(me + 1 + step, half)
     return jnp.concatenate([acc_f, acc_b], axis=1)
 
 
-def _pair_reduce_scatter(x, axis):
-    lo, hi = jnp.split(x, 2, axis=1)
+def _pair_reduce_scatter(x, axis, dim):
+    lo, hi = jnp.split(x, 2, axis=dim)
     first = lax.axis_index(axis) == 0
     keep = jnp.where(first, lo, hi)
     send = jnp.where(first, hi, lo)
@@ -71,17 +73,11 @@
     half = NSEQ // 2
     gathered = lax.all_gather(hidden, ("yl", "c"), axis=0, tiled=True)
     gathered = lax.all_gather(gathered, "z", axis=0, tiled=True)
-    partial_logits = lax.dot_general(
-        gathered,
-        head_weight,
-        (((1,), (1,)), ((), ())),
-        preferred_element_type=jnp.float32,
-    )
-    total_rows = partial_logits.shape[0]
+    total_rows = gathered.shape[0]
     seq_len = total_rows // NSEQ
     n_x = lax.axis_size("x")
-    logits = _ring_reduce_scatter(partial_logits, "x", n_x)
-    logits = _pair_reduce_scatter(logits, "yh")
+    logits = _ring_matmul_reduce_scatter(gathered, head_weight, "x", n_x)
+    logits = _pair_reduce_scatter(logits, "yh", 1)
     columns = logits.shape[1]
     soft = jax.nn.softplus(logits)
     act = jnp.log1p(soft)
@@ -129,7 +125,8 @@
     dlogit = lax.all_gather(dlogit, "yh", axis=1, tiled=True)
     partial_grad = _ring_gather_matmul(dlogit, head_weight, "x", n_x)
     hidden_grad = lax.psum_scatter(partial_grad, "z", scatter_dimension=0, tiled=True)
-    hidden_grad = lax.psum_scatter(hidden_grad, ("yl", "c"), scatter_dimension=0, tiled=True)
+    hidden_grad = _pair_reduce_scatter(hidden_grad, "yl", 0)
+    hidden_grad = _pair_reduce_scatter(hidden_grad, "c", 0)
     return (hidden_grad, loss)
 
 

time: 361 us -> 343 us (0.950)
  waiting for transfers between devices: 190 us -> 161 us
  starting transfers between devices: 32.5 us -> 49.5 us
  local copies, waits for them, and re-layouts: 23.4 us -> 6.96 us
  matrix products: 8.92 us -> 19.9 us
  other arithmetic: 17.9 us -> 12.1 us
  blocking collectives: 73 us -> 77.2 us
    reduce_scatter x1 -> x0, waiting for transfers between devices: 35.9 us -> none  [local(): lax.psum_scatter(hidden_grad, ('yl', 'c'), scatter_dimension=0, tiled=True)]
    ppermute x1 -> x3, starting transfers between devices: 4.63 us -> 21.1 us  [_pair_reduce_scatter(): return keep + lax.ppermute(send, axis, [(0, 1), (1, 0)])]
    dynamic_slice x9 -> x0, local copies, waits for them, and re-layouts: 15.6 us -> none  [block(): return lax.dynamic_index_in_dim(arr, k % n, 0, keepdims=False)]
    dot_general x1 -> x8, matrix products: 3.05 us -> 14.1 us  [term(): lax.dot_general(lhs, w, (((1,), (1,)), ((), ())), preferred_element_type=...]
    ppermute x9, waiting for transfers between devices: 16.8 us -> 21.2 us  [_shift(): return lax.ppermute(v, axis, [(i, (i + k) % n) for i in range(n)])]
    add x4, other arithmetic: 7.48 us -> 3.1 us  [the longest x2 1.51 us: _pair_reduce_scatter(): return keep + lax.ppermute(send, axis, [(0, 1), (1, 0)])]
    psum x5, blocking collectives: 53.5 us -> 57.8 us  [local(): stats = lax.psum(stats, axis)]
    ppermute x1 -> x3, waiting for transfers between devices: 5.53 us -> 8.09 us  [_pair_reduce_scatter(): return keep + lax.ppermute(send, axis, [(0, 1), (1, 0)])]
  transfers between devices with their start and end apart: 13 -> 14, of which waited for: 7 -> 13; matrix products, arithmetic and copies ran while one was open for 6% -> 4% of each run, Pallas kernels for 0% -> 0%
where the time goes in v3:
time: 343 us; the launch traced here: 342 us
  waiting for transfers between devices  161 us (47%)
  blocking collectives  77.2 us (23%)
  starting transfers between devices  49.5 us (14%)
  matrix products  19.9 us (6%)
  between operations  14.5 us (4%)
  other arithmetic  12.1 us (4%)
  local copies, waits for them, and re-layouts  6.96 us (2%)
    reduce_scatter x1, waiting for transfers between devices, local(): lax.psum_scatter(partial_grad, 'z', scatter_dimension=0, tiled=True)  71.1 us
    all_gather x1, waiting for transfers between devices, local(): gathered = lax.all_gather(gathered, 'z', axis=0, tiled=True)  60.9 us
    psum x5, blocking collectives, local(): stats = lax.psum(stats, axis)  57.8 us
    ppermute x9, starting transfers between devices, _shift(): return lax.ppermute(v, axis, [(i, (i + k) % n) for i in range(n)])  28.4 us
    ppermute x9, waiting for transfers between devices, _shift(): return lax.ppermute(v, axis, [(i, (i + k) % n) for i in range(n)])  21.2 us
    ppermute x3, starting transfers between devices, _pair_reduce_scatter(): return keep + lax.ppermute(send, axis, [(0, 1), (1, 0)])  21.1 us
    dot_general x8, matrix products, term(): lax.dot_general(lhs, w, (((1,), (1,)), ((), ())), preferred_element_type=...  14.1 us
    all_gather x1, blocking collectives, local(): gathered = lax.all_gather(hidden, ('yl', 'c'), axis=0, tiled=True)  12.7 us
  transfers between devices with their start and end apart: 14, of which 13 were waited for; matrix products, arithmetic and copies ran while one was open for 4% of the time, Pallas kernels for 0%

profile of v3, /device:TPU:1, one launch (start us, length us, event | category | flops | bytes accessed | tf_op | source)
XLA Modules:
  0.0 341.6 jit_solution(3033280193039469991)
XLA Ops:
  7.2 12.7 %all_gather.9 = bf16[32,1024]{1,0:T(8,128)(2,1)} all-gather(bf16[8,1024]{1,0:T(8,128)(2,1)} %param.4), channel_id=1, replica_groups=mesh['x'=4,'yh'=2,'z'=16,'yl'=2,'c'=2] {'yl','c'}, dimensions={0}, use_global_device_ids=true | all-gather | bytes 81920 | tf_op jit(solution)/shard_map/all_gather | solution.py:74
  20.1 60.9 %all-gather.2.cloned.1.call-done = bf16[512,1024]{1,0:T(8,128)(2,1)} async-done(((bf16[32,1024]{1,0:T(8,128)(2,1)}), bf16[512,1024]{1,0:T(8,128)(2,1)}) %all-gather.2.cloned.1.call-update) | async-done | bytes 1048592 | tf_op jit(solution)/shard_map/all_gather | solution.py:75
  81.0 2.5 convolution_bitcast_fusion.7
  83.5 3.1 collective-permute-start
  86.6 2.5 convolution_bitcast_fusion.3
  89.1 3.4 collective-permute-start.3
  92.5 0.9 collective-permute-done
  93.4 1.7 fusion.1
  95.1 1.9 collective-permute-start.1
  97.9 1.8 fusion
  99.7 4.6 %collective-permute-start.4 = (f32[512,192]{0,1:T(8,128)S(1)}, f32[512,192]{0,1:T(8,128)S(1)}, u32[]{:S(2)}, u32[]{:S(2)}) collective-permute-start(f32[512,192]{0,1:T(8,128)S(1)} %fusion), channel_id=1, source_target_pairs={{0,384},{128,0},{256,128},{384,256},{1,385},{129,1},{257,129},{385... | collective-permute-start | bytes 1179656 | tf_op jit(solution)/shard_map/ppermute | solution.py:20
  105.3 2.8 collective-permute-done.1
  109.0 2.0 collective-permute-start.2
  111.0 1.5 collective-permute-done.4
  113.3 4.9 %collective-permute-start.5 = (f32[512,192]{0,1:T(8,128)}, f32[512,192]{0,1:T(8,128)}, u32[]{:S(2)}, u32[]{:S(2)}) collective-permute-start(f32[512,192]{0,1:T(8,128)} %add.216), channel_id=1, source_target_pairs={{0,384},{128,0},{256,128},{384,256},{1,385},{129,1},{257,129},{385... | collective-permute-start | bytes 1179656 | tf_op jit(solution)/shard_map/ppermute | solution.py:20
  118.3 1.7 convolution_bitcast_fusion.4
  120.0 2.7 collective-permute-done.2
  122.7 3.4 %collective-permute-done.5 = f32[512,192]{0,1:T(8,128)} collective-permute-done((f32[512,192]{0,1:T(8,128)}, f32[512,192]{0,1:T(8,128)}, u32[]{:S(2)}, u32[]{:S(2)}) %collective-permute-start.5) | collective-permute-done | bytes 393248 | tf_op jit(solution)/shard_map/ppermute | solution.py:20
  126.1 2.8 broadcast_select_fusion
  128.9 4.6 %collective-permute-start.6 = (f32[512,192]{0,1:T(8,128)}, f32[512,192]{0,1:T(8,128)}, u32[]{:S(2)}, u32[]{:S(2)}) collective-permute-start(f32[512,192]{0,1:T(8,128)} %get-tuple-element.25), channel_id=1, source_target_pairs={{0,64},{64,0},{1,65},{65,1},{2,66},{66,2},{3,67},{67,3},{4,68},{68... | collective-permute-start | bytes 1179656 | tf_op jit(solution)/shard_map/ppermute | solution.py:47
  133.7 5.5 %collective-permute-done.6 = f32[512,192]{0,1:T(8,128)} collective-permute-done((f32[512,192]{0,1:T(8,128)}, f32[512,192]{0,1:T(8,128)}, u32[]{:S(2)}, u32[]{:S(2)}) %collective-permute-start.6) | collective-permute-done | bytes 393248 | tf_op jit(solution)/shard_map/ppermute | solution.py:47
  139.3 2.6 multiply_exponential_fusion
  141.9 2.0 copy.8
  143.9 1.2 multiply_reduce_fusion
  145.4 16.9 %all-reduce.2 = (f32[8]{0:T(128)S(1)}, f32[4,4]{1,0:T(4,128)S(1)}) all-reduce(f32[8]{0:T(128)S(1)} %get-tuple-element.18, f32[4,4]{1,0:T(4,128)S(1)} %fusion.19), channel_id=1, replica_groups=mesh['x'=4,'yh'=2,'z'=16,'yl'=2,'c'=2] {'c'}, use_global_device_ids=true, to_apply=%region_7.8 | all-reduce | flops 24 | bytes 192 | tf_op jit(solution)/shard_map/psum | solution.py:97
  162.3 3.8 %all-reduce.3 = (f32[8]{0:T(128)S(1)}, f32[4,4]{1,0:T(4,128)S(1)}) all-reduce(f32[8]{0:T(128)S(1)} %get-tuple-element.9, f32[4,4]{1,0:T(4,128)S(1)} %get-tuple-element.10), channel_id=1, replica_groups=mesh['x'=4,'yh'=2,'z'=16,'yl'=2,'c'=2] {'yl'}, use_global_device_ids=true, to_apply=%region_8.9 | all-reduce | flops 24 | bytes 192 | tf_op jit(solution)/shard_map/psum | solution.py:97
  166.0 5.3 %all-reduce.4 = (f32[8]{0:T(128)S(1)}, f32[4,4]{1,0:T(4,128)S(1)}) all-reduce(f32[8]{0:T(128)S(1)} %get-tuple-element.11, f32[4,4]{1,0:T(4,128)S(1)} %get-tuple-element.12), channel_id=1, replica_groups=mesh['x'=4,'yh'=2,'z'=16,'yl'=2,'c'=2] {'yh'}, use_global_device_ids=true, to_apply=%region_9.10 | all-reduce | flops 24 | bytes 192 | tf_op jit(solution)/shard_map/psum | solution.py:97
  171.3 9.4 %all-reduce.1 = (f32[8]{0:T(128)S(1)}, f32[4,4]{1,0:T(4,128)S(1)}) all-reduce(f32[8]{0:T(128)S(1)} %get-tuple-element.13, f32[4,4]{1,0:T(4,128)S(1)} %get-tuple-element.14), channel_id=1, replica_groups=mesh['x'=4,'yh'=2,'z'=16,'yl'=2,'c'=2] {'x'}, use_global_device_ids=true, to_apply=%region_10.11 | all-reduce | flops 24 | bytes 192 | tf_op jit(solution)/shard_map/psum | solution.py:97
  180.7 22.5 %all-reduce = (f32[8]{0:T(128)S(1)}, f32[4,4]{1,0:T(4,128)S(1)}) all-reduce(f32[8]{0:T(128)S(1)} %get-tuple-element.7, f32[4,4]{1,0:T(4,128)S(1)} %get-tuple-element.8), channel_id=1, replica_groups=mesh['x'=4,'yh'=2,'z'=16,'yl'=2,'c'=2] {'z'}, use_global_device_ids=true, to_apply=%region_11.12 | all-reduce | flops 24 | bytes 192 | tf_op jit(solution)/shard_map/psum | solution.py:97
  203.4 1.4 multiply_reduce_fusion.3
  205.5 0.8 mul.194
  206.3 1.2 copy.9
  208.4 2.0 copy.10
  210.3 1.6 divide_convert_fusion
  212.0 6.7 %all_gather.11 = bf16[512,384]{0,1:T(8,128)(2,1)S(1)} all-gather(bf16[512,192]{0,1:T(8,128)(2,1)S(1)} %divide_convert_fusion), channel_id=1, replica_groups=mesh['x'=4,'yh'=2,'z'=16,'yl'=2,'c'=2] {'yh'}, dimensions={1}, use_global_device_ids=true | all-gather | bytes 589824 | tf_op jit(solution)/shard_map/all_gather | solution.py:125
  218.7 1.9 collective-permute-start.7
  220.6 4.6 %collective-permute-start.8 = (bf16[512,384]{0,1:T(8,128)(2,1)S(1)}, bf16[512,384]{0,1:T(8,128)(2,1)S(1)}, u32[]{:S(2)}, u32[]{:S(2)}) collective-permute-start(bf16[512,384]{0,1:T(8,128)(2,1)S(1)} %all_gather.11), channel_id=1, source_target_pairs={{0,384},{128,0},{256,128},{384,256},{1,385},{129,1},{257,129},{385... | collective-permute-start | bytes 1179656 | tf_op jit(solution)/shard_map/ppermute | solution.py:20
  225.9 2.6 collective-permute-done.7
  228.5 1.9 collective-permute-start.9
  230.4 1.7 fusion.5
  232.9 6.6 %collective-permute-done.9 = bf16[512,384]{0,1:T(8,128)(2,1)S(1)} collective-permute-done((bf16[512,384]{0,1:T(8,128)(2,1)}, bf16[512,384]{0,1:T(8,128)(2,1)S(1)}, u32[]{:S(2)}, u32[]{:S(2)}) %collective-permute-start.9) | collective-permute-done | bytes 393248 | tf_op jit(solution)/shard_map/ppermute | solution.py:20
  239.5 2.1 add_add_fusion
  241.6 71.1 %reduce-scatter.2.cloned.1.call-done = f32[32,1024]{1,0:T(8,128)} async-done(((f32[512,1024]{1,0:T(8,128)}), f32[32,1024]{1,0:T(8,128)}) %reduce-scatter.2.cloned.1.call-update) | async-done | bytes 131088 | tf_op jit(solution)/shard_map/reduce_scatter | solution.py:127
  312.7 0.9 slice_select_fusion
  313.6 2.7 collective-permute-start.10
  316.2 2.3 collective-permute-done.10
  318.6 0.9 select_add_fusion.1
  319.5 13.8 %collective-permute-start.11 = (f32[8,1024]{1,0:T(8,128)S(1)}, f32[8,1024]{1,0:T(8,128)S(1)}, u32[]{:S(2)}, u32[]{:S(2)}) collective-permute-start(f32[8,1024]{1,0:T(8,128)S(1)} %slice_select_fusion.1), channel_id=1, source_target_pairs={{0,1},{1,0},{2,3},{3,2},{4,5},{5,4},{6,7},{7,6},{8,9},{9,8},{10,11... | collective-permute-start | bytes 98312 | tf_op jit(solution)/shard_map/ppermute | solution.py:47
  (42 shorter events, 8.6 us)
Async XLA Ops:
  7.2 73.8 %copy-start = (bf16[1536,1024]{1,0:T(8,128)(2,1)S(1)}, bf16[1536,1024]{1,0:T(8,128)(2,1)}, u32[]{:S(2)}) copy-start(bf16[1536,1024]{1,0:T(8,128)(2,1)} %param.5) | copy-start | bytes 9437188
  7.2 73.8 %all-gather.2.cloned.1.call-start = ((), (), s32[]{:S(2)}) async-start(), calls=%async_computation.1 | async-start | bytes 1114112 | tf_op jit(solution)/shard_map/all_gather | solution.py:75
  20.0 292.7 %reduce-scatter.2.cloned.1.call-start = ((), (), s32[]{:S(2)}) async-start(), calls=%async_computation.2 | async-start | bytes 2228224 | tf_op jit(solution)/shard_map/reduce_scatter | solution.py:127
  83.5 9.9 %collective-permute-start = (f32[512,192]{0,1:T(8,128)}, f32[512,192]{0,1:T(8,128)S(1)}, u32[]{:S(2)}, u32[]{:S(2)}) collective-permute-start(f32[512,192]{0,1:T(8,128)} %convolution_bitcast_fusion.7), channel_id=1, source_target_pairs={{0,128},{128,256},{256,384},{384,0},{1,129},{129,257},{257,385},{3... | collective-permute-start | bytes 1179656 | tf_op jit(solution)/shard_map/ppermute | solution.py:20
  89.1 8.8 %collective-permute-start.3 = (f32[512,192]{0,1:T(8,128)}, f32[512,192]{0,1:T(8,128)}, u32[]{:S(2)}, u32[]{:S(2)}) collective-permute-start(f32[512,192]{0,1:T(8,128)} %convolution_bitcast_fusion.3), channel_id=1, source_target_pairs={{0,384},{128,0},{256,128},{384,256},{1,385},{129,1},{257,129},{385... | collective-permute-start | bytes 1179656 | tf_op jit(solution)/shard_map/ppermute | solution.py:20
  92.5 11.8 %copy-start.1 = (bf16[512,1024]{1,0:T(8,128)(2,1)S(1)}, bf16[512,1024]{1,0:T(8,128)(2,1)}, u32[]{:S(2)}) copy-start(bf16[512,1024]{1,0:T(8,128)(2,1)} %all-gather.2.cloned.1.call-done) | copy-start | bytes 3145732
  95.1 13.1 %collective-permute-start.1 = (f32[512,192]{0,1:T(8,128)S(1)}, f32[512,192]{0,1:T(8,128)S(1)}, u32[]{:S(2)}, u32[]{:S(2)}) collective-permute-start(f32[512,192]{0,1:T(8,128)S(1)} %fusion.1), channel_id=1, source_target_pairs={{0,128},{128,256},{256,384},{384,0},{1,129},{129,257},{257,385},{3... | collective-permute-start | bytes 1179656 | tf_op jit(solution)/shard_map/ppermute | solution.py:20
  99.7 12.8 %collective-permute-start.4 = (f32[512,192]{0,1:T(8,128)S(1)}, f32[512,192]{0,1:T(8,128)S(1)}, u32[]{:S(2)}, u32[]{:S(2)}) collective-permute-start(f32[512,192]{0,1:T(8,128)S(1)} %fusion), channel_id=1, source_target_pairs={{0,384},{128,0},{256,128},{384,256},{1,385},{129,1},{257,129},{385... | collective-permute-start | bytes 1179656 | tf_op jit(solution)/shard_map/ppermute | solution.py:20
  109.0 24.6 %copy-start.4 = (s32[8]{0:T(128)S(1)}, s32[8]{0:T(128)}, u32[]{:S(2)}) copy-start(s32[8]{0:T(128)} %param.6) | copy-start | bytes 100
  109.0 13.7 %collective-permute-start.2 = (f32[512,192]{0,1:T(8,128)}, f32[512,192]{0,1:T(8,128)}, u32[]{:S(2)}, u32[]{:S(2)}) collective-permute-start(f32[512,192]{0,1:T(8,128)} %add.199), channel_id=1, source_target_pairs={{0,128},{128,256},{256,384},{384,0},{1,129},{129,257},{257,385},{3... | collective-permute-start | bytes 1179656 | tf_op jit(solution)/shard_map/ppermute | solution.py:20
  113.3 12.8 %collective-permute-start.5 = (f32[512,192]{0,1:T(8,128)}, f32[512,192]{0,1:T(8,128)}, u32[]{:S(2)}, u32[]{:S(2)}) collective-permute-start(f32[512,192]{0,1:T(8,128)} %add.216), channel_id=1, source_target_pairs={{0,384},{128,0},{256,128},{384,256},{1,385},{129,1},{257,129},{385... | collective-permute-start | bytes 1179656 | tf_op jit(solution)/shard_map/ppermute | solution.py:20
  128.9 10.3 %collective-permute-start.6 = (f32[512,192]{0,1:T(8,128)}, f32[512,192]{0,1:T(8,128)}, u32[]{:S(2)}, u32[]{:S(2)}) collective-permute-start(f32[512,192]{0,1:T(8,128)} %get-tuple-element.25), channel_id=1, source_target_pairs={{0,64},{64,0},{1,65},{65,1},{2,66},{66,2},{3,67},{67,3},{4,68},{68... | collective-permute-start | bytes 1179656 | tf_op jit(solution)/shard_map/ppermute | solution.py:47
  203.4 1.4 copy-start.2
  218.7 9.8 %collective-permute-start.7 = (bf16[512,384]{0,1:T(8,128)(2,1)S(1)}, bf16[512,384]{0,1:T(8,128)(2,1)}, u32[]{:S(2)}, u32[]{:S(2)}) collective-permute-start(bf16[512,384]{0,1:T(8,128)(2,1)S(1)} %all_gather.11), channel_id=1, source_target_pairs={{0,128},{128,256},{256,384},{384,0},{1,129},{129,257},{257,385},{3... | collective-permute-start | bytes 1179656 | tf_op jit(solution)/shard_map/ppermute | solution.py:20
  220.6 11.5 %collective-permute-start.8 = (bf16[512,384]{0,1:T(8,128)(2,1)S(1)}, bf16[512,384]{0,1:T(8,128)(2,1)S(1)}, u32[]{:S(2)}, u32[]{:S(2)}) collective-permute-start(bf16[512,384]{0,1:T(8,128)(2,1)S(1)} %all_gather.11), channel_id=1, source_target_pairs={{0,384},{128,0},{256,128},{384,256},{1,385},{129,1},{257,129},{385... | collective-permute-start | bytes 1179656 | tf_op jit(solution)/shard_map/ppermute | solution.py:20
  228.5 11.0 %collective-permute-start.9 = (bf16[512,384]{0,1:T(8,128)(2,1)}, bf16[512,384]{0,1:T(8,128)(2,1)S(1)}, u32[]{:S(2)}, u32[]{:S(2)}) collective-permute-start(bf16[512,384]{0,1:T(8,128)(2,1)} %collective-permute-done.7), channel_id=1, source_target_pairs={{0,128},{128,256},{256,384},{384,0},{1,129},{129,257},{257,385},{3... | collective-permute-start | bytes 1179656 | tf_op jit(solution)/shard_map/ppermute | solution.py:20
  232.9 100.4 %copy-start.3 = (f32[4]{0:T(128)S(1)}, f32[4]{0:T(128)}, u32[]{:S(2)}) copy-start(f32[4]{0:T(128)} %copy-done.2) | copy-start | bytes 52
  232.9 100.4 %copy-start.5 = (f32[4]{0:T(128)S(1)}, f32[4]{0:T(128)}, u32[]{:S(2)}) copy-start(f32[4]{0:T(128)} %get-tuple-element.4) | copy-start | bytes 52
  313.6 5.0 %collective-permute-start.10 = (f32[16,1024]{1,0:T(8,128)S(1)}, f32[16,1024]{1,0:T(8,128)S(1)}, u32[]{:S(2)}, u32[]{:S(2)}) collective-permute-start(f32[16,1024]{1,0:T(8,128)S(1)} %slice_select_fusion), channel_id=1, source_target_pairs={{0,2},{2,0},{1,3},{3,1},{4,6},{6,4},{5,7},{7,5},{8,10},{10,8},{9,1... | collective-permute-start | bytes 196616 | tf_op jit(solution)/shard_map/ppermute | solution.py:47
  319.5 14.6 %collective-permute-start.11 = (f32[8,1024]{1,0:T(8,128)S(1)}, f32[8,1024]{1,0:T(8,128)S(1)}, u32[]{:S(2)}, u32[]{:S(2)}) collective-permute-start(f32[8,1024]{1,0:T(8,128)S(1)} %slice_select_fusion.1), channel_id=1, source_target_pairs={{0,1},{1,0},{2,3},{3,2},{4,5},{5,4},{6,7},{7,6},{8,9},{9,8},{10,11... | collective-permute-start | bytes 98312 | tf_op jit(solution)/shard_map/ppermute | solution.py:47
Sparse Core Ops, SparseCore 0:
  20.1 60.8 all-gather.1
  241.7 70.8 reduce-scatter.1

commit v4 on v3

--- a/solution.py
+++ b/solution.py
@@ -16,27 +16,36 @@
 VOC = ("z", "yl", "c")
 
 
+def _members(axes):
+    axes = axes if isinstance(axes, tuple) else (axes,)
+    n = 1
+    for a in axes:
+        n *= lax.axis_size(a)
+    return n
+
+
+def _all_gather_a2a(x, axes):
+    n = _members(axes)
+    copies = jnp.broadcast_to(x[None], (n,) + x.shape)
+    out = lax.all_to_all(copies, axes, 0, 0, tiled=True)
+    return out.reshape((n * x.shape[0],) + x.shape[1:])
+
+
+def _reduce_scatter_a2a(x, axes):
+    n = _members(axes)
+    rows, cols = x.shape
+    blocks = x.reshape(rows, n, cols // n).transpose(1, 0, 2)
+    return jnp.sum(lax.all_to_all(blocks, axes, 0, 0, tiled=True), axis=0)
+
+
+def _all_reduce_a2a(x, axes):
+    n = _members(axes)
+    copies = jnp.broadcast_to(x[None], (n,) + x.shape)
+    return jnp.sum(lax.all_to_all(copies, axes, 0, 0, tiled=True), axis=0)
+
+
 def _shift(v, axis, n, k):
     return lax.ppermute(v, axis, [(i, (i + k) % n) for i in range(n)])
-
-
-def _ring_matmul_reduce_scatter(lhs, weight, axis, n):
-    me = lax.axis_index(axis)
-    rows = weight.shape[0] // n
-    half = rows // 2
-
-    def term(k, offset):
-        w = lax.dynamic_slice_in_dim(weight, (k % n) * rows + offset, half, axis=0)
-        return lax.dot_general(
-            lhs, w, (((1,), (1,)), ((), ())), preferred_element_type=jnp.float32
-        )
-
-    acc_f = term(me - 1, 0)
-    acc_b = term(me + 1, half)
-    for step in range(1, n):
-        acc_f = _shift(acc_f, axis, n, 1) + term(me - 1 - step, 0)
-        acc_b = _shift(acc_b, axis, n, -1) + term(me + 1 + step, half)
-    return jnp.concatenate([acc_f, acc_b], axis=1)
 
 
 def _pair_reduce_scatter(x, axis, dim):
@@ -72,12 +81,17 @@
 def local(hidden, head_weight, lengths, pairing):
     half = NSEQ // 2
     gathered = lax.all_gather(hidden, ("yl", "c"), axis=0, tiled=True)
-    gathered = lax.all_gather(gathered, "z", axis=0, tiled=True)
+    gathered = _all_gather_a2a(gathered, "z")
     total_rows = gathered.shape[0]
     seq_len = total_rows // NSEQ
     n_x = lax.axis_size("x")
-    logits = _ring_matmul_reduce_scatter(gathered, head_weight, "x", n_x)
-    logits = _pair_reduce_scatter(logits, "yh", 1)
+    partial_logits = lax.dot_general(
+        gathered,
+        head_weight,
+        (((1,), (1,)), ((), ())),
+        preferred_element_type=jnp.float32,
+    )
+    logits = _reduce_scatter_a2a(partial_logits, SEC)
     columns = logits.shape[1]
     soft = jax.nn.softplus(logits)
     act = jnp.log1p(soft)
@@ -92,10 +106,11 @@
         queries, documents, (((1,), (1,)), ((), ())), precision=lax.Precision.HIGHEST
     )
     norms_part = jnp.sum(pooled * pooled, axis=1)
-    stats = (dots_part, norms_part)
-    for axis in ("c", "yl", "yh", "x", "z"):
-        stats = lax.psum(stats, axis)
-    dots, norms = stats
+    stats = jnp.concatenate([dots_part.reshape(-1), norms_part])
+    for axes in (("yl", "c"), SEC, "z"):
+        stats = _all_reduce_a2a(stats, axes)
+    dots = stats[: half * half].reshape(half, half)
+    norms = stats[half * half :]
     inv = lax.rsqrt(norms + eps_norm)
     inv_q = inv[:half]
     inv_d = inv[half:]

time: 343 us -> 311 us (0.907)
  waiting for transfers between devices: 161 us -> 113 us
  blocking collectives: 77.2 us -> 94.1 us
  matrix products: 19.9 us -> 11.4 us
  local copies, waits for them, and re-layouts: 6.96 us -> 11.4 us
  other arithmetic: 12.1 us -> 16.2 us
    all_to_all x0 -> x3, blocking collectives: none -> 75.1 us  [the longest x1 54.9 us: _all_gather_a2a(): out = lax.all_to_all(copies, axes, 0, 0, tiled=True)]
    all_gather x1 -> x0, waiting for transfers between devices: 60.9 us -> none  [local(): gathered = lax.all_gather(gathered, 'z', axis=0, tiled=True)]
    psum x5 -> x0, blocking collectives: 57.8 us -> none  [local(): stats = lax.psum(stats, axis)]
    all_to_all x0 -> x2, waiting for transfers between devices: none -> 45.2 us  [the longest x1 38.2 us: _reduce_scatter_a2a(): return jnp.sum(lax.all_to_all(blocks, axes, 0, 0, tiled=True), axis=0)]
    all_to_all x0 -> x2, starting transfers between devices: none -> 23.7 us  [the longest x1 16.9 us: _all_reduce_a2a(): return jnp.sum(lax.all_to_all(copies, axes, 0, 0, tiled=True), axis=0)]
    ppermute x9 -> x3, starting transfers between devices: 28.4 us -> 8.39 us  [_shift(): return lax.ppermute(v, axis, [(i, (i + k) % n) for i in range(n)])]
    reduce_scatter x1, waiting for transfers between devices: 71.1 us -> 57.7 us  [local(): lax.psum_scatter(partial_grad, 'z', scatter_dimension=0, tiled=True)]
    ppermute x9 -> x3, waiting for transfers between devices: 21.2 us -> 8.04 us  [_shift(): return lax.ppermute(v, axis, [(i, (i + k) % n) for i in range(n)])]
  transfers between devices with their start and end apart: 14 -> 8, of which waited for: 13 -> 7; matrix products, arithmetic and copies ran while one was open for 4% -> 3% of each run, Pallas kernels for 0% -> 0%
where the time goes in v4:
time: 311 us; the launch traced here: 310 us
  waiting for transfers between devices  113 us (36%)
  blocking collectives  94.1 us (30%)
  starting transfers between devices  48.8 us (16%)
  other arithmetic  16.2 us (5%)
  between operations  14.3 us (5%)
  local copies, waits for them, and re-layouts  11.4 us (4%)
  matrix products  11.4 us (4%)
    reduce_scatter x1, waiting for transfers between devices, local(): lax.psum_scatter(partial_grad, 'z', scatter_dimension=0, tiled=True)  57.7 us
    all_to_all x1, blocking collectives, _all_gather_a2a(): out = lax.all_to_all(copies, axes, 0, 0, tiled=True)  54.9 us
    all_to_all x1, waiting for transfers between devices, _reduce_scatter_a2a(): return jnp.sum(lax.all_to_all(blocks, axes, 0, 0, tiled=True), axis=0)  38.2 us
    all_to_all x2, blocking collectives, _all_reduce_a2a(): return jnp.sum(lax.all_to_all(copies, axes, 0, 0, tiled=True), axis=0)  20.3 us
    all_to_all x1, starting transfers between devices, _all_reduce_a2a(): return jnp.sum(lax.all_to_all(copies, axes, 0, 0, tiled=True), axis=0)  16.9 us
    ppermute x2, starting transfers between devices, _pair_reduce_scatter(): return keep + lax.ppermute(send, axis, [(0, 1), (1, 0)])  16.7 us
    all_gather x1, blocking collectives, local(): gathered = lax.all_gather(hidden, ('yl', 'c'), axis=0, tiled=True)  12.3 us
    ppermute x3, starting transfers between devices, _shift(): return lax.ppermute(v, axis, [(i, (i + k) % n) for i in range(n)])  8.39 us
  transfers between devices with their start and end apart: 8, of which 7 were waited for; matrix products, arithmetic and copies ran while one was open for 3% of the time, Pallas kernels for 0%

profile of v4, /device:TPU:1, one launch (start us, length us, event | category | flops | bytes accessed | tf_op | source)
XLA Modules:
  0.0 309.7 jit_solution(3227274133266953542)
XLA Ops:
  7.2 12.3 %all_gather.6 = bf16[32,1024]{1,0:T(8,128)(2,1)S(1)} all-gather(bf16[8,1024]{1,0:T(8,128)(2,1)} %param.4), channel_id=1, replica_groups=mesh['x'=4,'yh'=2,'z'=16,'yl'=2,'c'=2] {'yl','c'}, dimensions={0}, use_global_device_ids=true | all-gather | bytes 81920 | tf_op jit(solution)/shard_map/all_gather | solution.py:83
  19.6 54.9 %all_to_all.28 = bf16[16,32,1024]{2,1,0:T(8,128)(2,1)S(1)} all-to-all(bf16[16,32,1024]{2,1,0:T(8,128)(2,1)S(1)} %broadcast_in_dim.8), channel_id=1, replica_groups=mesh['x'=4,'yh'=2,'z'=16,'yl'=2,'c'=2] {'z'}, dimensions={0} | all-to-all | bytes 2097152 | tf_op jit(solution)/shard_map/all_to_all | solution.py:30
  74.5 3.6 %convolution_bitcast_fusion = f32[8,512,192]{1,2,0:T(8,128)} fusion(bf16[512,1024,1]{1,0,2:T(8,128)(2,1)S(1)} %bitcast.26, bf16[8,192,1024]{2,1,0:T(8,128)(2,1)S(1)} %bitcast.23), kind=kOutput, calls=%fused_computation.1 | convolution fusion | flops 1610612736 | bytes 7340032 | tf_op jit(solution)/shard_map/dot_general | solution.py:88
  78.1 6.8 %all-to-all-start.1 = ((f32[8,512,192]{1,2,0:T(8,128)}), f32[8,512,192]{1,2,0:T(8,128)}, u32[]{:S(2)}, u32[]{:S(2)}) async-start(f32[8,512,192]{1,2,0:T(8,128)} %convolution_bitcast_fusion), calls=%async_computation.1 | async-start | bytes 6291456 | tf_op jit(solution)/shard_map/all_to_all | solution.py:38
  84.9 38.2 %all-to-all-done.1 = f32[8,512,192]{1,2,0:T(8,128)} async-done(((f32[8,512,192]{1,2,0:T(8,128)}), f32[8,512,192]{1,2,0:T(8,128)}, u32[]{:S(2)}, u32[]{:S(2)}) %all-to-all-start.1) | async-done | bytes 3145760 | tf_op jit(solution)/shard_map/all_to_all | solution.py:38
  123.2 2.3 reduce_sum.101
  125.4 1.0 copy.14
  126.4 1.6 fusion.11
  128.0 0.6 multiply_reduce_fusion
  128.7 0.7 fusion.14
  129.4 1.4 reshape.87
  130.7 0.8 pad_maximum_fusion.1
  131.5 10.4 %all_to_all.29 = f32[4,1,24]{2,1,0:T(1,128)} all-to-all(f32[4,1,24]{2,1,0:T(1,128)S(1)} %broadcast_in_dim.9), channel_id=1, replica_groups=mesh['x'=4,'yh'=2,'z'=16,'yl'=2,'c'=2] {'yl','c'}, dimensions={0} | all-to-all | bytes 768 | tf_op jit(solution)/shard_map/all_to_all | solution.py:44
  141.9 1.2 reduce_sum.105
  143.1 0.7 broadcast_in_dim.10
  143.7 9.9 %all_to_all.30 = f32[8,1,24]{2,1,0:T(1,128)} all-to-all(f32[8,1,24]{2,1,0:T(1,128)S(1)} %broadcast_in_dim.10), channel_id=1, replica_groups=mesh['x'=4,'yh'=2,'z'=16,'yl'=2,'c'=2] {'x','yh'}, dimensions={0} | all-to-all | bytes 1536 | tf_op jit(solution)/shard_map/all_to_all | solution.py:44
  153.6 1.2 reduce_sum.106
  154.8 1.3 broadcast_in_dim.11
  156.1 16.9 %all-to-all-start.4 = ((f32[16,1,24]{2,1,0:T(1,128)}), f32[16,1,24]{2,1,0:T(1,128)}, u32[]{:S(2)}, u32[]{:S(2)}) async-start(f32[16,1,24]{2,1,0:T(1,128)} %broadcast_in_dim.11), calls=%async_computation.4 | async-start | bytes 16384 | tf_op jit(solution)/shard_map/all_to_all | solution.py:44
  173.0 1.3 reshape.89
  174.4 0.8 div.57
  175.2 2.0 copy.19
  177.2 6.9 %all-to-all-done.4 = f32[16,1,24]{2,1,0:T(1,128)} async-done(((f32[16,1,24]{2,1,0:T(1,128)}), f32[16,1,24]{2,1,0:T(1,128)}, u32[]{:S(2)}, u32[]{:S(2)}) %all-to-all-start.4) | async-done | bytes 1568 | tf_op jit(solution)/shard_map/all_to_all | solution.py:44
  184.1 0.7 reduce_sum.107
  185.6 0.8 exponential_reduce_fusion
  186.4 1.5 multiply_reduce_fusion.2
  188.1 0.9 convolution_add_fusion.1
  188.9 0.9 convolution_add_fusion
  189.9 0.8 mul.168
  190.7 2.0 copy.18
  192.7 1.6 divide_convert_fusion
  194.3 6.7 %all_gather.7 = bf16[512,384]{0,1:T(8,128)(2,1)S(1)} all-gather(bf16[512,192]{0,1:T(8,128)(2,1)S(1)} %divide_convert_fusion), channel_id=1, replica_groups=mesh['x'=4,'yh'=2,'z'=16,'yl'=2,'c'=2] {'yh'}, dimensions={1}, use_global_device_ids=true | all-gather | bytes 589824 | tf_op jit(solution)/shard_map/all_gather | solution.py:140
  201.0 2.0 collective-permute-start
  203.2 4.5 %collective-permute-start.1 = (bf16[512,384]{0,1:T(8,128)(2,1)S(1)}, bf16[512,384]{0,1:T(8,128)(2,1)S(1)}, u32[]{:S(2)}, u32[]{:S(2)}) collective-permute-start(bf16[512,384]{0,1:T(8,128)(2,1)S(1)} %all_gather.7), channel_id=1, source_target_pairs={{0,384},{128,0},{256,128},{384,256},{1,385},{129,1},{257,129},{385... | collective-permute-start | bytes 1179656 | tf_op jit(solution)/shard_map/ppermute | solution.py:48
  207.6 0.7 fusion.5
  208.3 2.5 collective-permute-done
  210.9 1.9 collective-permute-start.2
  212.8 1.7 fusion.3
  214.5 0.7 fusion.1
  215.3 5.5 %collective-permute-done.2 = bf16[512,384]{0,1:T(8,128)(2,1)S(1)} collective-permute-done((bf16[512,384]{0,1:T(8,128)(2,1)}, bf16[512,384]{0,1:T(8,128)(2,1)S(1)}, u32[]{:S(2)}, u32[]{:S(2)}) %collective-permute-start.2) | collective-permute-done | bytes 393248 | tf_op jit(solution)/shard_map/ppermute | solution.py:48
  220.8 2.1 add_add_fusion
  222.9 57.7 %reduce-scatter.2.cloned.1.call-done = f32[32,1024]{1,0:T(8,128)} async-done(((f32[512,1024]{1,0:T(8,128)}), f32[32,1024]{1,0:T(8,128)}) %reduce-scatter.2.cloned.1.call-update) | async-done | bytes 131088 | tf_op jit(solution)/shard_map/reduce_scatter | solution.py:142
  280.6 0.9 slice_select_fusion
  281.5 3.0 collective-permute-start.3
  284.5 2.3 collective-permute-done.3
  286.8 0.9 select_add_fusion
  287.7 13.7 %collective-permute-start.4 = (f32[8,1024]{1,0:T(8,128)S(1)}, f32[8,1024]{1,0:T(8,128)S(1)}, u32[]{:S(2)}, u32[]{:S(2)}) collective-permute-start(f32[8,1024]{1,0:T(8,128)S(1)} %slice_select_fusion.1), channel_id=1, source_target_pairs={{0,1},{1,0},{2,3},{3,2},{4,5},{5,4},{6,7},{7,6},{8,9},{9,8},{10,11... | collective-permute-start | bytes 98312 | tf_op jit(solution)/shard_map/ppermute | solution.py:56
  302.2 0.6 select_add_fusion.1
  (28 shorter events, 2.0 us)
Async XLA Ops:
  7.2 67.3 %copy-start = (bf16[1536,1024]{1,0:T(8,128)(2,1)S(1)}, bf16[1536,1024]{1,0:T(8,128)(2,1)}, u32[]{:S(2)}) copy-start(bf16[1536,1024]{1,0:T(8,128)(2,1)} %param.5) | copy-start | bytes 9437188
  78.1 6.8 %copy-start.4 = (s32[8]{0:T(128)S(1)}, s32[8]{0:T(128)}, u32[]{:S(2)}) copy-start(s32[8]{0:T(128)} %param.6) | copy-start | bytes 100
  78.1 45.1 %all-to-all-start.1 = ((f32[8,512,192]{1,2,0:T(8,128)}), f32[8,512,192]{1,2,0:T(8,128)}, u32[]{:S(2)}, u32[]{:S(2)}) async-start(f32[8,512,192]{1,2,0:T(8,128)} %convolution_bitcast_fusion), calls=%async_computation.1 | async-start | bytes 6291456 | tf_op jit(solution)/shard_map/all_to_all | solution.py:38
  84.9 41.5 %copy-start.1 = (f32[8,64]{1,0:T(8,128)}, f32[8,64]{1,0:T(8,128)S(1)}, u32[]{:S(2)}) copy-start(f32[8,64]{1,0:T(8,128)S(1)} %fusion.12) | copy-start | bytes 6148
  156.1 28.0 %all-to-all-start.4 = ((f32[16,1,24]{2,1,0:T(1,128)}), f32[16,1,24]{2,1,0:T(1,128)}, u32[]{:S(2)}, u32[]{:S(2)}) async-start(f32[16,1,24]{2,1,0:T(1,128)} %broadcast_in_dim.11), calls=%async_computation.4 | async-start | bytes 16384 | tf_op jit(solution)/shard_map/all_to_all | solution.py:44
  173.0 107.6 %reduce-scatter.2.cloned.1.call-start = ((), (), s32[]{:S(2)}) async-start(), calls=%async_computation.6 | async-start | bytes 2228224 | tf_op jit(solution)/shard_map/reduce_scatter | solution.py:142
  186.4 1.5 copy-start.2
  201.0 9.8 %collective-permute-start = (bf16[512,384]{0,1:T(8,128)(2,1)S(1)}, bf16[512,384]{0,1:T(8,128)(2,1)}, u32[]{:S(2)}, u32[]{:S(2)}) collective-permute-start(bf16[512,384]{0,1:T(8,128)(2,1)S(1)} %all_gather.7), channel_id=1, source_target_pairs={{0,128},{128,256},{256,384},{384,0},{1,129},{129,257},{257,385},{3... | collective-permute-start | bytes 1179656 | tf_op jit(solution)/shard_map/ppermute | solution.py:48
  203.2 11.4 %collective-permute-start.1 = (bf16[512,384]{0,1:T(8,128)(2,1)S(1)}, bf16[512,384]{0,1:T(8,128)(2,1)S(1)}, u32[]{:S(2)}, u32[]{:S(2)}) collective-permute-start(bf16[512,384]{0,1:T(8,128)(2,1)S(1)} %all_gather.7), channel_id=1, source_target_pairs={{0,384},{128,0},{256,128},{384,256},{1,385},{129,1},{257,129},{385... | collective-permute-start | bytes 1179656 | tf_op jit(solution)/shard_map/ppermute | solution.py:48
  210.9 9.9 %collective-permute-start.2 = (bf16[512,384]{0,1:T(8,128)(2,1)}, bf16[512,384]{0,1:T(8,128)(2,1)S(1)}, u32[]{:S(2)}, u32[]{:S(2)}) collective-permute-start(bf16[512,384]{0,1:T(8,128)(2,1)} %collective-permute-done), channel_id=1, source_target_pairs={{0,128},{128,256},{256,384},{384,0},{1,129},{129,257},{257,385},{3... | collective-permute-start | bytes 1179656 | tf_op jit(solution)/shard_map/ppermute | solution.py:48
  215.3 86.1 %copy-start.3 = (f32[4]{0:T(128)S(1)}, f32[4]{0:T(128)}, u32[]{:S(2)}) copy-start(f32[4]{0:T(128)} %copy-done.2) | copy-start | bytes 52
  215.3 86.1 %copy-start.5 = (f32[4]{0:T(128)S(1)}, f32[4]{0:T(128)}, u32[]{:S(2)}) copy-start(f32[4]{0:T(128)} %get-tuple-element.4) | copy-start | bytes 52
  281.5 5.2 %collective-permute-start.3 = (f32[16,1024]{1,0:T(8,128)S(1)}, f32[16,1024]{1,0:T(8,128)S(1)}, u32[]{:S(2)}, u32[]{:S(2)}) collective-permute-start(f32[16,1024]{1,0:T(8,128)S(1)} %slice_select_fusion), channel_id=1, source_target_pairs={{0,2},{2,0},{1,3},{3,1},{4,6},{6,4},{5,7},{7,5},{8,10},{10,8},{9,1... | collective-permute-start | bytes 196616 | tf_op jit(solution)/shard_map/ppermute | solution.py:56
  287.7 14.6 %collective-permute-start.4 = (f32[8,1024]{1,0:T(8,128)S(1)}, f32[8,1024]{1,0:T(8,128)S(1)}, u32[]{:S(2)}, u32[]{:S(2)}) collective-permute-start(f32[8,1024]{1,0:T(8,128)S(1)} %slice_select_fusion.1), channel_id=1, source_target_pairs={{0,1},{1,0},{2,3},{3,2},{4,5},{5,4},{6,7},{7,6},{8,9},{9,8},{10,11... | collective-permute-start | bytes 98312 | tf_op jit(solution)/shard_map/ppermute | solution.py:56
Sparse Core Ops, SparseCore 0:
  223.0 57.5 reduce-scatter.1

commit v5 on v4

--- a/solution.py
+++ b/solution.py
@@ -13,7 +13,8 @@
 eps_norm = 1e-06
 
 SEC = ("x", "yh")
-VOC = ("z", "yl", "c")
+Z = ("zh", "zl")
+VOC = Z + ("yl", "c")
 
 
 def _members(axes):
@@ -81,7 +82,11 @@
 def local(hidden, head_weight, lengths, pairing):
     half = NSEQ // 2
     gathered = lax.all_gather(hidden, ("yl", "c"), axis=0, tiled=True)
-    gathered = _all_gather_a2a(gathered, "z")
+    gathered = _all_gather_a2a(gathered, "zh")
+    n_zh = lax.axis_size("zh")
+    gathered = _all_gather_a2a(gathered, "zl")
+    gathered = gathered.reshape(-1, n_zh, gathered.shape[0] // (n_zh * lax.axis_size("zl")), gathered.shape[1])
+    gathered = gathered.transpose(1, 0, 2, 3).reshape(-1, gathered.shape[-1])
     total_rows = gathered.shape[0]
     seq_len = total_rows // NSEQ
     n_x = lax.axis_size("x")
@@ -107,7 +112,7 @@
     )
     norms_part = jnp.sum(pooled * pooled, axis=1)
     stats = jnp.concatenate([dots_part.reshape(-1), norms_part])
-    for axes in (("yl", "c"), SEC, "z"):
+    for axes in (("yl", "c"), SEC, Z):
         stats = _all_reduce_a2a(stats, axes)
     dots = stats[: half * half].reshape(half, half)
     norms = stats[half * half :]
@@ -139,7 +144,7 @@
     dlogit = (dact * jax.nn.sigmoid(logits) / (1.0 + soft)).astype(jnp.bfloat16)
     dlogit = lax.all_gather(dlogit, "yh", axis=1, tiled=True)
     partial_grad = _ring_gather_matmul(dlogit, head_weight, "x", n_x)
-    hidden_grad = lax.psum_scatter(partial_grad, "z", scatter_dimension=0, tiled=True)
+    hidden_grad = lax.psum_scatter(partial_grad, Z, scatter_dimension=0, tiled=True)
     hidden_grad = _pair_reduce_scatter(hidden_grad, "yl", 0)
     hidden_grad = _pair_reduce_scatter(hidden_grad, "c", 0)
     return (hidden_grad, loss)
@@ -148,7 +153,7 @@
 def solution(mesh):
     n_sec, n_voc = mesh.devices.shape
     fine = Mesh(
-        mesh.devices.reshape(n_sec // 2, 2, n_voc // 4, 2, 2), SEC + VOC
+        mesh.devices.reshape(n_sec // 2, 2, n_voc // 16, 4, 2, 2), SEC + VOC
     )
     in_specs = (P(VOC, SEC), P(VOC, SEC), P(), P())
     out_specs = (P(VOC, SEC), P())

time: 311 us -> 303 us (0.974)
  starting transfers between devices: 48.8 us -> 36.2 us
  waiting for transfers between devices: 113 us -> 119 us
    all_to_all x1, starting transfers between devices: 16.9 us -> 4.14 us  [_all_reduce_a2a(): return jnp.sum(lax.all_to_all(copies, axes, 0, 0, tiled=True), axis=0)]
    all_to_all x1, waiting for transfers between devices: 38.2 us -> 44 us  [_reduce_scatter_a2a(): return jnp.sum(lax.all_to_all(blocks, axes, 0, 0, tiled=True), axis=0)]
    all_to_all x1 -> x2, blocking collectives: 54.9 us -> 57.2 us  [_all_gather_a2a(): out = lax.all_to_all(copies, axes, 0, 0, tiled=True)]
where the time goes in v5:
time: 303 us; the launch traced here: 302 us
  waiting for transfers between devices  119 us (39%)
  blocking collectives  93.9 us (31%)
  starting transfers between devices  36.2 us (12%)
  other arithmetic  16.2 us (5%)
  between operations  14.3 us (5%)
  local copies, waits for them, and re-layouts  11.6 us (4%)
  matrix products  11.4 us (4%)
    reduce_scatter x1, waiting for transfers between devices, local(): lax.psum_scatter(partial_grad, Z, scatter_dimension=0, tiled=True)  57.3 us
    all_to_all x2, blocking collectives, _all_gather_a2a(): out = lax.all_to_all(copies, axes, 0, 0, tiled=True)  57.2 us
    all_to_all x1, waiting for transfers between devices, _reduce_scatter_a2a(): return jnp.sum(lax.all_to_all(blocks, axes, 0, 0, tiled=True), axis=0)  44 us
    all_to_all x2, blocking collectives, _all_reduce_a2a(): return jnp.sum(lax.all_to_all(copies, axes, 0, 0, tiled=True), axis=0)  17.7 us
    ppermute x2, starting transfers between devices, _pair_reduce_scatter(): return keep + lax.ppermute(send, axis, [(0, 1), (1, 0)])  16.9 us
    all_gather x1, blocking collectives, local(): gathered = lax.all_gather(hidden, ('yl', 'c'), axis=0, tiled=True)  12.3 us
    ppermute x3, starting transfers between devices, _shift(): return lax.ppermute(v, axis, [(i, (i + k) % n) for i in range(n)])  8.39 us
    ppermute x3, waiting for transfers between devices, _shift(): return lax.ppermute(v, axis, [(i, (i + k) % n) for i in range(n)])  8.04 us
  transfers between devices with their start and end apart: 8, of which 7 were waited for; matrix products, arithmetic and copies ran while one was open for 3% of the time, Pallas kernels for 0%

profile of v5, /device:TPU:1, one launch (start us, length us, event | category | flops | bytes accessed | tf_op | source)
XLA Modules:
  0.0 302.4 jit_solution(18238564717988387947)
XLA Ops:
  7.2 12.3 %all_gather.6 = bf16[32,1024]{1,0:T(8,128)(2,1)S(1)} all-gather(bf16[8,1024]{1,0:T(8,128)(2,1)} %param.4), channel_id=1, replica_groups=mesh['x'=4,'yh'=2,'zh'=4,'zl'=4,'yl'=2,'c'=2] {'yl','c'}, dimensions={0}, use_global_device_ids=true | all-gather | bytes 81920 | tf_op jit(solution)/shard_map/all_gather | solution.py:84
  19.5 23.6 %all_to_all.33 = bf16[4,32,1024]{2,1,0:T(8,128)(2,1)S(1)} all-to-all(bf16[4,32,1024]{2,1,0:T(8,128)(2,1)S(1)} %broadcast_in_dim.12), channel_id=1, replica_groups=mesh['x'=4,'yh'=2,'zh'=4,'zl'=4,'yl'=2,'c'=2] {'zh'}, dimensions={0} | all-to-all | bytes 524288 | tf_op jit(solution)/shard_map/all_to_all | solution.py:31
  43.2 33.6 %all_to_all.34 = bf16[4,128,1024]{2,1,0:T(8,128)(2,1)S(1)} all-to-all(bf16[4,128,1024]{2,1,0:T(8,128)(2,1)S(1)} %broadcast_in_dim.14), channel_id=1, replica_groups=mesh['x'=4,'yh'=2,'zh'=4,'zl'=4,'yl'=2,'c'=2] {'zl'}, dimensions={0} | all-to-all | bytes 2097152 | tf_op jit(solution)/shard_map/all_to_all | solution.py:31
  76.9 3.6 %convolution_bitcast_fusion = f32[8,512,192]{1,2,0:T(8,128)} fusion(bf16[512,1024,1]{1,0,2:T(8,128)(2,1)S(1)} %bitcast.32, bf16[8,192,1024]{2,1,0:T(8,128)(2,1)S(1)} %bitcast.27), kind=kOutput, calls=%fused_computation.1 | convolution fusion | flops 1610612736 | bytes 7340032 | tf_op jit(solution)/shard_map/dot_general | solution.py:93
  80.5 6.8 %all-to-all-start.2 = ((f32[8,512,192]{1,2,0:T(8,128)}), f32[8,512,192]{1,2,0:T(8,128)}, u32[]{:S(2)}, u32[]{:S(2)}) async-start(f32[8,512,192]{1,2,0:T(8,128)} %convolution_bitcast_fusion), calls=%async_computation.2 | async-start | bytes 6291456 | tf_op jit(solution)/shard_map/all_to_all | solution.py:39
  87.4 44.0 %all-to-all-done.2 = f32[8,512,192]{1,2,0:T(8,128)} async-done(((f32[8,512,192]{1,2,0:T(8,128)}), f32[8,512,192]{1,2,0:T(8,128)}, u32[]{:S(2)}, u32[]{:S(2)}) %all-to-all-start.2) | async-done | bytes 3145760 | tf_op jit(solution)/shard_map/all_to_all | solution.py:39
  131.4 2.3 reduce_sum.101
  133.6 1.0 copy.19
  134.6 1.6 fusion.11
  136.2 0.6 multiply_reduce_fusion
  136.9 0.7 fusion.14
  137.6 1.4 reshape.88
  138.9 0.8 pad_maximum_fusion.1
  139.7 8.2 %all_to_all.35 = f32[4,1,24]{2,1,0:T(1,128)} all-to-all(f32[4,1,24]{2,1,0:T(1,128)S(1)} %broadcast_in_dim.15), channel_id=1, replica_groups=mesh['x'=4,'yh'=2,'zh'=4,'zl'=4,'yl'=2,'c'=2] {'yl','c'}, dimensions={0} | all-to-all | bytes 768 | tf_op jit(solution)/shard_map/all_to_all | solution.py:45
  147.8 1.2 reduce_sum.105
  149.1 0.7 broadcast_in_dim.16
  149.7 9.5 %all_to_all.36 = f32[8,1,24]{2,1,0:T(1,128)} all-to-all(f32[8,1,24]{2,1,0:T(1,128)S(1)} %broadcast_in_dim.16), channel_id=1, replica_groups=mesh['x'=4,'yh'=2,'zh'=4,'zl'=4,'yl'=2,'c'=2] {'x','yh'}, dimensions={0} | all-to-all | bytes 1536 | tf_op jit(solution)/shard_map/all_to_all | solution.py:45
  159.3 1.2 reduce_sum.106
  160.5 1.3 broadcast_in_dim.17
  161.7 4.1 %all-to-all-start.5 = ((f32[16,1,24]{2,1,0:T(1,128)}), f32[16,1,24]{2,1,0:T(1,128)}, u32[]{:S(2)}, u32[]{:S(2)}) async-start(f32[16,1,24]{2,1,0:T(1,128)} %broadcast_in_dim.17), calls=%async_computation.5 | async-start | bytes 16384 | tf_op jit(solution)/shard_map/all_to_all | solution.py:45
  165.9 1.3 reshape.90
  167.3 0.8 div.57
  168.1 2.0 copy.24
  170.1 6.9 %all-to-all-done.5 = f32[16,1,24]{2,1,0:T(1,128)} async-done(((f32[16,1,24]{2,1,0:T(1,128)}), f32[16,1,24]{2,1,0:T(1,128)}, u32[]{:S(2)}, u32[]{:S(2)}) %all-to-all-start.5) | async-done | bytes 1568 | tf_op jit(solution)/shard_map/all_to_all | solution.py:45
  177.0 0.7 reduce_sum.107
  178.5 0.8 exponential_reduce_fusion
  179.3 1.5 multiply_reduce_fusion.2
  180.9 0.9 convolution_add_fusion.1
  181.8 0.9 convolution_add_fusion
  182.8 0.8 mul.168
  183.6 2.0 copy.23
  185.6 1.6 divide_convert_fusion
  187.2 6.7 %all_gather.7 = bf16[512,384]{0,1:T(8,128)(2,1)S(1)} all-gather(bf16[512,192]{0,1:T(8,128)(2,1)S(1)} %divide_convert_fusion), channel_id=1, replica_groups=mesh['x'=4,'yh'=2,'zh'=4,'zl'=4,'yl'=2,'c'=2] {'yh'}, dimensions={1}, use_global_device_ids=true | all-gather | bytes 589824 | tf_op jit(solution)/shard_map/all_gather | solution.py:145
  193.9 2.0 collective-permute-start
  196.1 4.4 %collective-permute-start.1 = (bf16[512,384]{0,1:T(8,128)(2,1)S(1)}, bf16[512,384]{0,1:T(8,128)(2,1)S(1)}, u32[]{:S(2)}, u32[]{:S(2)}) collective-permute-start(bf16[512,384]{0,1:T(8,128)(2,1)S(1)} %all_gather.7), channel_id=1, source_target_pairs={{0,384},{128,0},{256,128},{384,256},{1,385},{129,1},{257,129},{385... | collective-permute-start | bytes 1179656 | tf_op jit(solution)/shard_map/ppermute | solution.py:49
  200.5 0.7 fusion.5
  201.2 2.5 collective-permute-done
  203.8 1.9 collective-permute-start.2
  205.7 1.7 fusion.3
  207.4 0.7 fusion.1
  208.2 5.5 %collective-permute-done.2 = bf16[512,384]{0,1:T(8,128)(2,1)S(1)} collective-permute-done((bf16[512,384]{0,1:T(8,128)(2,1)}, bf16[512,384]{0,1:T(8,128)(2,1)S(1)}, u32[]{:S(2)}, u32[]{:S(2)}) %collective-permute-start.2) | collective-permute-done | bytes 393248 | tf_op jit(solution)/shard_map/ppermute | solution.py:49
  213.7 2.1 add_add_fusion
  215.8 57.3 %reduce-scatter.2.cloned.1.call-done = f32[32,1024]{1,0:T(8,128)} async-done(((f32[512,1024]{1,0:T(8,128)}), f32[32,1024]{1,0:T(8,128)}) %reduce-scatter.2.cloned.1.call-update) | async-done | bytes 131088 | tf_op jit(solution)/shard_map/reduce_scatter | solution.py:147
  273.1 0.9 slice_select_fusion
  274.0 3.0 collective-permute-start.3
  277.0 2.3 collective-permute-done.3
  279.3 0.9 select_add_fusion
  280.2 13.8 %collective-permute-start.4 = (f32[8,1024]{1,0:T(8,128)S(1)}, f32[8,1024]{1,0:T(8,128)S(1)}, u32[]{:S(2)}, u32[]{:S(2)}) collective-permute-start(f32[8,1024]{1,0:T(8,128)S(1)} %slice_select_fusion.1), channel_id=1, source_target_pairs={{0,1},{1,0},{2,3},{3,2},{4,5},{5,4},{6,7},{7,6},{8,9},{9,8},{10,11... | collective-permute-start | bytes 98312 | tf_op jit(solution)/shard_map/ppermute | solution.py:57
  (31 shorter events, 2.8 us)
Async XLA Ops:
  7.2 69.8 %copy-start = (bf16[1536,1024]{1,0:T(8,128)(2,1)S(1)}, bf16[1536,1024]{1,0:T(8,128)(2,1)}, u32[]{:S(2)}) copy-start(bf16[1536,1024]{1,0:T(8,128)(2,1)} %param.5) | copy-start | bytes 9437188
  80.5 6.8 %copy-start.4 = (s32[8]{0:T(128)S(1)}, s32[8]{0:T(128)}, u32[]{:S(2)}) copy-start(s32[8]{0:T(128)} %param.6) | copy-start | bytes 100
  80.5 50.8 %all-to-all-start.2 = ((f32[8,512,192]{1,2,0:T(8,128)}), f32[8,512,192]{1,2,0:T(8,128)}, u32[]{:S(2)}, u32[]{:S(2)}) async-start(f32[8,512,192]{1,2,0:T(8,128)} %convolution_bitcast_fusion), calls=%async_computation.2 | async-start | bytes 6291456 | tf_op jit(solution)/shard_map/all_to_all | solution.py:39
  87.4 47.2 %copy-start.1 = (f32[8,64]{1,0:T(8,128)}, f32[8,64]{1,0:T(8,128)S(1)}, u32[]{:S(2)}) copy-start(f32[8,64]{1,0:T(8,128)S(1)} %fusion.12) | copy-start | bytes 6148
  161.7 15.3 %all-to-all-start.5 = ((f32[16,1,24]{2,1,0:T(1,128)}), f32[16,1,24]{2,1,0:T(1,128)}, u32[]{:S(2)}, u32[]{:S(2)}) async-start(f32[16,1,24]{2,1,0:T(1,128)} %broadcast_in_dim.17), calls=%async_computation.5 | async-start | bytes 16384 | tf_op jit(solution)/shard_map/all_to_all | solution.py:45
  165.9 107.3 %reduce-scatter.2.cloned.1.call-start = ((), (), s32[]{:S(2)}) async-start(), calls=%async_computation.7 | async-start | bytes 2228224 | tf_op jit(solution)/shard_map/reduce_scatter | solution.py:147
  179.3 1.5 copy-start.2
  193.9 9.8 %collective-permute-start = (bf16[512,384]{0,1:T(8,128)(2,1)S(1)}, bf16[512,384]{0,1:T(8,128)(2,1)}, u32[]{:S(2)}, u32[]{:S(2)}) collective-permute-start(bf16[512,384]{0,1:T(8,128)(2,1)S(1)} %all_gather.7), channel_id=1, source_target_pairs={{0,128},{128,256},{256,384},{384,0},{1,129},{129,257},{257,385},{3... | collective-permute-start | bytes 1179656 | tf_op jit(solution)/shard_map/ppermute | solution.py:49
  196.1 11.4 %collective-permute-start.1 = (bf16[512,384]{0,1:T(8,128)(2,1)S(1)}, bf16[512,384]{0,1:T(8,128)(2,1)S(1)}, u32[]{:S(2)}, u32[]{:S(2)}) collective-permute-start(bf16[512,384]{0,1:T(8,128)(2,1)S(1)} %all_gather.7), channel_id=1, source_target_pairs={{0,384},{128,0},{256,128},{384,256},{1,385},{129,1},{257,129},{385... | collective-permute-start | bytes 1179656 | tf_op jit(solution)/shard_map/ppermute | solution.py:49
  203.8 9.9 %collective-permute-start.2 = (bf16[512,384]{0,1:T(8,128)(2,1)}, bf16[512,384]{0,1:T(8,128)(2,1)S(1)}, u32[]{:S(2)}, u32[]{:S(2)}) collective-permute-start(bf16[512,384]{0,1:T(8,128)(2,1)} %collective-permute-done), channel_id=1, source_target_pairs={{0,128},{128,256},{256,384},{384,0},{1,129},{129,257},{257,385},{3... | collective-permute-start | bytes 1179656 | tf_op jit(solution)/shard_map/ppermute | solution.py:49
  208.2 85.9 %copy-start.3 = (f32[4]{0:T(128)S(1)}, f32[4]{0:T(128)}, u32[]{:S(2)}) copy-start(f32[4]{0:T(128)} %copy-done.2) | copy-start | bytes 52
  208.2 85.9 %copy-start.5 = (f32[4]{0:T(128)S(1)}, f32[4]{0:T(128)}, u32[]{:S(2)}) copy-start(f32[4]{0:T(128)} %get-tuple-element.4) | copy-start | bytes 52
  274.0 5.3 %collective-permute-start.3 = (f32[16,1024]{1,0:T(8,128)S(1)}, f32[16,1024]{1,0:T(8,128)S(1)}, u32[]{:S(2)}, u32[]{:S(2)}) collective-permute-start(f32[16,1024]{1,0:T(8,128)S(1)} %slice_select_fusion), channel_id=1, source_target_pairs={{0,2},{2,0},{1,3},{3,1},{4,6},{6,4},{5,7},{7,5},{8,10},{10,8},{9,1... | collective-permute-start | bytes 196616 | tf_op jit(solution)/shard_map/ppermute | solution.py:57
  280.2 14.7 %collective-permute-start.4 = (f32[8,1024]{1,0:T(8,128)S(1)}, f32[8,1024]{1,0:T(8,128)S(1)}, u32[]{:S(2)}, u32[]{:S(2)}) collective-permute-start(f32[8,1024]{1,0:T(8,128)S(1)} %slice_select_fusion.1), channel_id=1, source_target_pairs={{0,1},{1,0},{2,3},{3,2},{4,5},{5,4},{6,7},{7,6},{8,9},{9,8},{10,11... | collective-permute-start | bytes 98312 | tf_op jit(solution)/shard_map/ppermute | solution.py:57
Sparse Core Ops, SparseCore 0:
  215.9 57.1 reduce-scatter.1

commit v6 on v5

--- a/solution.py
+++ b/solution.py
@@ -81,12 +81,12 @@
 
 def local(hidden, head_weight, lengths, pairing):
     half = NSEQ // 2
-    gathered = lax.all_gather(hidden, ("yl", "c"), axis=0, tiled=True)
-    gathered = _all_gather_a2a(gathered, "zh")
+    near = ("zl", "yl", "c")
+    gathered = _all_gather_a2a(hidden, "zh")
     n_zh = lax.axis_size("zh")
-    gathered = _all_gather_a2a(gathered, "zl")
-    gathered = gathered.reshape(-1, n_zh, gathered.shape[0] // (n_zh * lax.axis_size("zl")), gathered.shape[1])
-    gathered = gathered.transpose(1, 0, 2, 3).reshape(-1, gathered.shape[-1])
+    gathered = _all_gather_a2a(gathered, near)
+    gathered = gathered.reshape(_members(near), n_zh, hidden.shape[0], hidden.shape[1])
+    gathered = gathered.transpose(1, 0, 2, 3).reshape(-1, hidden.shape[1])
     total_rows = gathered.shape[0]
     seq_len = total_rows // NSEQ
     n_x = lax.axis_size("x")
@@ -112,7 +112,7 @@
     )
     norms_part = jnp.sum(pooled * pooled, axis=1)
     stats = jnp.concatenate([dots_part.reshape(-1), norms_part])
-    for axes in (("yl", "c"), SEC, Z):
+    for axes in (VOC, SEC):
         stats = _all_reduce_a2a(stats, axes)
     dots = stats[: half * half].reshape(half, half)
     norms = stats[half * half :]

time: 303 us -> 290 us (0.957)
  blocking collectives: 93.9 us -> 84.3 us
  waiting for transfers between devices: 119 us -> 115 us
    all_gather x1 -> x0, blocking collectives: 12.3 us -> none  [local(): gathered = lax.all_gather(hidden, ('yl', 'c'), axis=0, tiled=True)]
    all_to_all x1, waiting for transfers between devices: 6.94 us -> 2.35 us  [_all_reduce_a2a(): return jnp.sum(lax.all_to_all(copies, axes, 0, 0, tiled=True), axis=0)]
    all_to_all x2 -> x1, blocking collectives: 17.7 us -> 18.3 us  [_all_reduce_a2a(): return jnp.sum(lax.all_to_all(copies, axes, 0, 0, tiled=True), axis=0)]
where the time goes in v6:
time: 290 us; the launch traced here: 289 us
  waiting for transfers between devices  115 us (40%)
  blocking collectives  84.3 us (29%)
  starting transfers between devices  36.8 us (13%)
  other arithmetic  15.2 us (5%)
  between operations  14.3 us (5%)
  local copies, waits for them, and re-layouts  11.7 us (4%)
  matrix products  11.4 us (4%)
    all_to_all x2, blocking collectives, _all_gather_a2a(): out = lax.all_to_all(copies, axes, 0, 0, tiled=True)  59.3 us
    reduce_scatter x1, waiting for transfers between devices, local(): lax.psum_scatter(partial_grad, Z, scatter_dimension=0, tiled=True)  55.5 us
    all_to_all x1, waiting for transfers between devices, _reduce_scatter_a2a(): return jnp.sum(lax.all_to_all(blocks, axes, 0, 0, tiled=True), axis=0)  45.6 us
    all_to_all x1, blocking collectives, _all_reduce_a2a(): return jnp.sum(lax.all_to_all(copies, axes, 0, 0, tiled=True), axis=0)  18.3 us
    ppermute x2, starting transfers between devices, _pair_reduce_scatter(): return keep + lax.ppermute(send, axis, [(0, 1), (1, 0)])  16.7 us
    ppermute x3, waiting for transfers between devices, _shift(): return lax.ppermute(v, axis, [(i, (i + k) % n) for i in range(n)])  9.15 us
    ppermute x3, starting transfers between devices, _shift(): return lax.ppermute(v, axis, [(i, (i + k) % n) for i in range(n)])  8.39 us
    all_gather x1, blocking collectives, local(): dlogit = lax.all_gather(dlogit, 'yh', axis=1, tiled=True)  6.7 us
  transfers between devices with their start and end apart: 8, of which 7 were waited for; matrix products, arithmetic and copies ran while one was open for 3% of the time, Pallas kernels for 0%

profile of v6, /device:TPU:1, one launch (start us, length us, event | category | flops | bytes accessed | tf_op | source)
XLA Modules:
  0.0 288.8 jit_solution(5273631624534268052)
XLA Ops:
  7.2 0.9 broadcast_in_dim.10
  8.1 28.1 %all_to_all.27 = bf16[4,8,1024]{2,1,0:T(8,128)(2,1)S(1)} all-to-all(bf16[4,8,1024]{2,1,0:T(8,128)(2,1)S(1)} %broadcast_in_dim.10), channel_id=1, replica_groups=mesh['x'=4,'yh'=2,'zh'=4,'zl'=4,'yl'=2,'c'=2] {'zh'}, dimensions={0} | all-to-all | bytes 131072 | tf_op jit(solution)/shard_map/all_to_all | solution.py:31
  36.2 31.3 %all_to_all.28 = bf16[16,32,1024]{2,1,0:T(8,128)(2,1)S(1)} all-to-all(bf16[16,32,1024]{2,1,0:T(8,128)(2,1)S(1)} %broadcast_in_dim.12), channel_id=1, replica_groups=mesh['x'=4,'yh'=2,'zh'=4,'zl'=4,'yl'=2,'c'=2] {'zl','yl','c'}, dimensions={0} | all-to-all | bytes 2097152 | tf_op jit(solution)/shard_map/all_to_all | solution.py:31
  67.6 3.6 %convolution_bitcast_fusion = f32[8,512,192]{1,2,0:T(8,128)} fusion(bf16[512,1024,1]{1,0,2:T(8,128)(2,1)S(1)} %bitcast.29, bf16[8,192,1024]{2,1,0:T(8,128)(2,1)S(1)} %bitcast.25), kind=kOutput, calls=%fused_computation.1 | convolution fusion | flops 1610612736 | bytes 7340032 | tf_op jit(solution)/shard_map/dot_general | solution.py:93
  71.2 6.5 %all-to-all-start.2 = ((f32[8,512,192]{1,2,0:T(8,128)}), f32[8,512,192]{1,2,0:T(8,128)}, u32[]{:S(2)}, u32[]{:S(2)}) async-start(f32[8,512,192]{1,2,0:T(8,128)} %convolution_bitcast_fusion), calls=%async_computation.2 | async-start | bytes 6291456 | tf_op jit(solution)/shard_map/all_to_all | solution.py:39
  77.8 45.6 %all-to-all-done.2 = f32[8,512,192]{1,2,0:T(8,128)} async-done(((f32[8,512,192]{1,2,0:T(8,128)}), f32[8,512,192]{1,2,0:T(8,128)}, u32[]{:S(2)}, u32[]{:S(2)}) %all-to-all-start.2) | async-done | bytes 3145760 | tf_op jit(solution)/shard_map/all_to_all | solution.py:39
  123.4 2.3 reduce_sum.92
  125.7 1.0 copy.19
  126.7 1.6 fusion.11
  128.3 0.6 multiply_reduce_fusion
  128.9 0.7 fusion.14
  129.6 1.4 reshape.82
  131.0 0.8 pad_maximum_fusion.1
  131.8 18.3 %all_to_all.29 = f32[64,1,24]{2,1,0:T(1,128)} all-to-all(f32[64,1,24]{2,1,0:T(1,128)S(1)} %broadcast_in_dim.13), channel_id=1, replica_groups=mesh['x'=4,'yh'=2,'zh'=4,'zl'=4,'yl'=2,'c'=2] {'zh','zl','yl','c'}, dimensions={0} | all-to-all | bytes 12288 | tf_op jit(solution)/shard_map/all_to_all | solution.py:45
  150.0 1.4 reduce_sum.96
  151.4 1.2 broadcast_in_dim.14
  152.6 5.2 %all-to-all-start.4 = ((f32[8,1,24]{2,1,0:T(1,128)}), f32[8,1,24]{2,1,0:T(1,128)}, u32[]{:S(2)}, u32[]{:S(2)}) async-start(f32[8,1,24]{2,1,0:T(1,128)} %broadcast_in_dim.14), calls=%async_computation.4 | async-start | bytes 8192 | tf_op jit(solution)/shard_map/all_to_all | solution.py:45
  157.8 1.3 reshape.84
  159.2 0.8 div.57
  160.0 2.0 copy.23
  162.0 2.3 all-to-all-done.4
  164.3 0.7 reduce_sum.97
  165.1 0.6 broadcast_multiply_fusion.2
  165.7 0.8 exponential_reduce_fusion
  166.6 1.5 multiply_reduce_fusion.2
  168.2 0.9 convolution_add_fusion.1
  169.1 0.9 convolution_add_fusion
  170.1 0.8 mul.168
  170.9 2.0 copy.22
  172.9 1.6 divide_convert_fusion
  174.5 6.7 %all_gather.3 = bf16[512,384]{0,1:T(8,128)(2,1)S(1)} all-gather(bf16[512,192]{0,1:T(8,128)(2,1)S(1)} %divide_convert_fusion), channel_id=1, replica_groups=mesh['x'=4,'yh'=2,'zh'=4,'zl'=4,'yl'=2,'c'=2] {'yh'}, dimensions={1}, use_global_device_ids=true | all-gather | bytes 589824 | tf_op jit(solution)/shard_map/all_gather | solution.py:145
  181.2 2.0 collective-permute-start
  183.3 4.5 %collective-permute-start.1 = (bf16[512,384]{0,1:T(8,128)(2,1)S(1)}, bf16[512,384]{0,1:T(8,128)(2,1)S(1)}, u32[]{:S(2)}, u32[]{:S(2)}) collective-permute-start(bf16[512,384]{0,1:T(8,128)(2,1)S(1)} %all_gather.3), channel_id=1, source_target_pairs={{0,384},{128,0},{256,128},{384,256},{1,385},{129,1},{257,129},{385... | collective-permute-start | bytes 1179656 | tf_op jit(solution)/shard_map/ppermute | solution.py:49
  187.8 0.7 fusion.5
  188.5 3.6 %collective-permute-done = bf16[512,384]{0,1:T(8,128)(2,1)} collective-permute-done((bf16[512,384]{0,1:T(8,128)(2,1)S(1)}, bf16[512,384]{0,1:T(8,128)(2,1)}, u32[]{:S(2)}, u32[]{:S(2)}) %collective-permute-start) | collective-permute-done | bytes 393248 | tf_op jit(solution)/shard_map/ppermute | solution.py:49
  192.1 1.9 collective-permute-start.2
  194.1 1.7 fusion.3
  195.8 0.7 fusion.1
  196.6 5.5 %collective-permute-done.2 = bf16[512,384]{0,1:T(8,128)(2,1)S(1)} collective-permute-done((bf16[512,384]{0,1:T(8,128)(2,1)}, bf16[512,384]{0,1:T(8,128)(2,1)S(1)}, u32[]{:S(2)}, u32[]{:S(2)}) %collective-permute-start.2) | collective-permute-done | bytes 393248 | tf_op jit(solution)/shard_map/ppermute | solution.py:49
  202.1 2.1 add_add_fusion
  204.2 55.5 %reduce-scatter.2.cloned.1.call-done = f32[32,1024]{1,0:T(8,128)} async-done(((f32[512,1024]{1,0:T(8,128)}), f32[32,1024]{1,0:T(8,128)}) %reduce-scatter.2.cloned.1.call-update) | async-done | bytes 131088 | tf_op jit(solution)/shard_map/reduce_scatter | solution.py:147
  259.7 0.9 slice_select_fusion
  260.6 3.0 %collective-permute-start.3 = (f32[16,1024]{1,0:T(8,128)S(1)}, f32[16,1024]{1,0:T(8,128)S(1)}, u32[]{:S(2)}, u32[]{:S(2)}) collective-permute-start(f32[16,1024]{1,0:T(8,128)S(1)} %slice_select_fusion), channel_id=1, source_target_pairs={{0,2},{2,0},{1,3},{3,1},{4,6},{6,4},{5,7},{7,5},{8,10},{10,8},{9,1... | collective-permute-start | bytes 196616 | tf_op jit(solution)/shard_map/ppermute | solution.py:57
  263.6 2.3 collective-permute-done.3
  265.9 0.9 select_add_fusion
  266.8 13.7 %collective-permute-start.4 = (f32[8,1024]{1,0:T(8,128)S(1)}, f32[8,1024]{1,0:T(8,128)S(1)}, u32[]{:S(2)}, u32[]{:S(2)}) collective-permute-start(f32[8,1024]{1,0:T(8,128)S(1)} %slice_select_fusion.1), channel_id=1, source_target_pairs={{0,1},{1,0},{2,3},{3,2},{4,5},{5,4},{6,7},{7,6},{8,9},{9,8},{10,11... | collective-permute-start | bytes 98312 | tf_op jit(solution)/shard_map/ppermute | solution.py:57
  280.5 0.6 subtract_reduce_fusion
  281.4 0.6 select_add_fusion.1
  (27 shorter events, 0.9 us)
Async XLA Ops:
  7.2 60.4 %copy-start = (bf16[1536,1024]{1,0:T(8,128)(2,1)S(1)}, bf16[1536,1024]{1,0:T(8,128)(2,1)}, u32[]{:S(2)}) copy-start(bf16[1536,1024]{1,0:T(8,128)(2,1)} %param.5) | copy-start | bytes 9437188
  71.2 6.5 %copy-start.4 = (s32[8]{0:T(128)S(1)}, s32[8]{0:T(128)}, u32[]{:S(2)}) copy-start(s32[8]{0:T(128)} %param.6) | copy-start | bytes 100
  71.2 52.2 %all-to-all-start.2 = ((f32[8,512,192]{1,2,0:T(8,128)}), f32[8,512,192]{1,2,0:T(8,128)}, u32[]{:S(2)}, u32[]{:S(2)}) async-start(f32[8,512,192]{1,2,0:T(8,128)} %convolution_bitcast_fusion), calls=%async_computation.2 | async-start | bytes 6291456 | tf_op jit(solution)/shard_map/all_to_all | solution.py:39
  77.8 48.9 %copy-start.1 = (f32[8,64]{1,0:T(8,128)}, f32[8,64]{1,0:T(8,128)S(1)}, u32[]{:S(2)}) copy-start(f32[8,64]{1,0:T(8,128)S(1)} %fusion.12) | copy-start | bytes 6148
  152.6 11.7 %all-to-all-start.4 = ((f32[8,1,24]{2,1,0:T(1,128)}), f32[8,1,24]{2,1,0:T(1,128)}, u32[]{:S(2)}, u32[]{:S(2)}) async-start(f32[8,1,24]{2,1,0:T(1,128)} %broadcast_in_dim.14), calls=%async_computation.4 | async-start | bytes 8192 | tf_op jit(solution)/shard_map/all_to_all | solution.py:45
  157.8 101.9 %reduce-scatter.2.cloned.1.call-start = ((), (), s32[]{:S(2)}) async-start(), calls=%async_computation.6 | async-start | bytes 2228224 | tf_op jit(solution)/shard_map/reduce_scatter | solution.py:147
  166.6 1.5 copy-start.2
  181.2 10.9 %collective-permute-start = (bf16[512,384]{0,1:T(8,128)(2,1)S(1)}, bf16[512,384]{0,1:T(8,128)(2,1)}, u32[]{:S(2)}, u32[]{:S(2)}) collective-permute-start(bf16[512,384]{0,1:T(8,128)(2,1)S(1)} %all_gather.3), channel_id=1, source_target_pairs={{0,128},{128,256},{256,384},{384,0},{1,129},{129,257},{257,385},{3... | collective-permute-start | bytes 1179656 | tf_op jit(solution)/shard_map/ppermute | solution.py:49
  183.3 12.5 %collective-permute-start.1 = (bf16[512,384]{0,1:T(8,128)(2,1)S(1)}, bf16[512,384]{0,1:T(8,128)(2,1)S(1)}, u32[]{:S(2)}, u32[]{:S(2)}) collective-permute-start(bf16[512,384]{0,1:T(8,128)(2,1)S(1)} %all_gather.3), channel_id=1, source_target_pairs={{0,384},{128,0},{256,128},{384,256},{1,385},{129,1},{257,129},{385... | collective-permute-start | bytes 1179656 | tf_op jit(solution)/shard_map/ppermute | solution.py:49
  192.1 9.9 %collective-permute-start.2 = (bf16[512,384]{0,1:T(8,128)(2,1)}, bf16[512,384]{0,1:T(8,128)(2,1)S(1)}, u32[]{:S(2)}, u32[]{:S(2)}) collective-permute-start(bf16[512,384]{0,1:T(8,128)(2,1)} %collective-permute-done), channel_id=1, source_target_pairs={{0,128},{128,256},{256,384},{384,0},{1,129},{129,257},{257,385},{3... | collective-permute-start | bytes 1179656 | tf_op jit(solution)/shard_map/ppermute | solution.py:49
  196.5 84.0 %copy-start.3 = (f32[4]{0:T(128)S(1)}, f32[4]{0:T(128)}, u32[]{:S(2)}) copy-start(f32[4]{0:T(128)} %copy-done.2) | copy-start | bytes 52
  196.5 84.0 %copy-start.5 = (f32[4]{0:T(128)S(1)}, f32[4]{0:T(128)}, u32[]{:S(2)}) copy-start(f32[4]{0:T(128)} %get-tuple-element.4) | copy-start | bytes 52
  260.6 5.3 %collective-permute-start.3 = (f32[16,1024]{1,0:T(8,128)S(1)}, f32[16,1024]{1,0:T(8,128)S(1)}, u32[]{:S(2)}, u32[]{:S(2)}) collective-permute-start(f32[16,1024]{1,0:T(8,128)S(1)} %slice_select_fusion), channel_id=1, source_target_pairs={{0,2},{2,0},{1,3},{3,1},{4,6},{6,4},{5,7},{7,5},{8,10},{10,8},{9,1... | collective-permute-start | bytes 196616 | tf_op jit(solution)/shard_map/ppermute | solution.py:57
  266.8 14.6 %collective-permute-start.4 = (f32[8,1024]{1,0:T(8,128)S(1)}, f32[8,1024]{1,0:T(8,128)S(1)}, u32[]{:S(2)}, u32[]{:S(2)}) collective-permute-start(f32[8,1024]{1,0:T(8,128)S(1)} %slice_select_fusion.1), channel_id=1, source_target_pairs={{0,1},{1,0},{2,3},{3,2},{4,5},{5,4},{6,7},{7,6},{8,9},{9,8},{10,11... | collective-permute-start | bytes 98312 | tf_op jit(solution)/shard_map/ppermute | solution.py:57
Sparse Core Ops, SparseCore 0:
  204.3 55.3 reduce-scatter.1

commit v7 on v6

--- a/solution.py
+++ b/solution.py
@@ -142,11 +142,17 @@
     dpooled = jnp.concatenate([dpool_q, dpool_d], axis=0)
     dact = (dpooled[:, None, :] * expo / totals[:, None, :]).reshape(total_rows, columns)
     dlogit = (dact * jax.nn.sigmoid(logits) / (1.0 + soft)).astype(jnp.bfloat16)
-    dlogit = lax.all_gather(dlogit, "yh", axis=1, tiled=True)
-    partial_grad = _ring_gather_matmul(dlogit, head_weight, "x", n_x)
-    hidden_grad = lax.psum_scatter(partial_grad, Z, scatter_dimension=0, tiled=True)
-    hidden_grad = _pair_reduce_scatter(hidden_grad, "yl", 0)
-    hidden_grad = _pair_reduce_scatter(hidden_grad, "c", 0)
+    n_sec = _members(SEC)
+    dlogit = _all_gather_a2a(dlogit[None], SEC)
+    weight = head_weight.reshape(n_sec, columns, head_weight.shape[1])
+    partial_grad = lax.dot_general(
+        dlogit, weight, (((0, 2), (0, 1)), ((), ())), preferred_element_type=jnp.float32
+    )
+    n_near = _members(near)
+    rows = hidden.shape[0]
+    grad = partial_grad.reshape(n_zh, n_near, rows, partial_grad.shape[1]).transpose(1, 0, 2, 3)
+    grad = jnp.sum(lax.all_to_all(grad, near, 0, 0, tiled=True), axis=0)
+    hidden_grad = jnp.sum(lax.all_to_all(grad, "zh", 0, 0, tiled=True), axis=0)
     return (hidden_grad, loss)
 
 

time: 290 us -> 278 us (0.959)
  blocking collectives: 84.3 us -> 156 us
  waiting for transfers between devices: 115 us -> 62 us
  starting transfers between devices: 36.8 us -> 15 us
  between operations: 14.3 us -> 0.76 us
  local copies, waits for them, and re-layouts: 11.7 us -> 17.2 us
    reduce_scatter x1 -> x0, waiting for transfers between devices: 55.5 us -> none  [local(): lax.psum_scatter(partial_grad, Z, scatter_dimension=0, tiled=True)]
    all_to_all x0 -> x1, blocking collectives: none -> 53.7 us  [local(): grad = jnp.sum(lax.all_to_all(grad, near, 0, 0, tiled=True), axis=0)]
    ppermute x5 -> x0, starting transfers between devices: 25.1 us -> none  [the longest x2 16.7 us: _pair_reduce_scatter(): return keep + lax.ppermute(send, axis, [(0, 1), (1, 0)])]
    all_to_all x2 -> x3, blocking collectives: 59.3 us -> 84.1 us  [_all_gather_a2a(): out = lax.all_to_all(copies, axes, 0, 0, tiled=True)]
    all_to_all x0 -> x1, waiting for transfers between devices: none -> 13.9 us  [local(): hidden_grad = jnp.sum(lax.all_to_all(grad, 'zh', 0, 0, tiled=True), axis=0)]
    ppermute x5 -> x0, waiting for transfers between devices: 11.7 us -> none  [the longest x3 9.15 us: _shift(): return lax.ppermute(v, axis, [(i, (i + k) % n) for i in range(n)])]
    all_gather x1 -> x0, blocking collectives: 6.7 us -> none  [local(): dlogit = lax.all_gather(dlogit, 'yh', axis=1, tiled=True)]
    all_to_all x0 -> x1, local copies, waits for them, and re-layouts: none -> 4.4 us  [_all_gather_a2a(): out = lax.all_to_all(copies, axes, 0, 0, tiled=True)]
  transfers between devices with their start and end apart: 8 -> 3, of which waited for: 7 -> 3; matrix products, arithmetic and copies ran while one was open for 3% -> 2% of each run, Pallas kernels for 0% -> 0%
where the time goes in v7:
time: 278 us; the launch traced here: 277 us
  blocking collectives  156 us (56%)
  waiting for transfers between devices  62 us (22%)
  local copies, waits for them, and re-layouts  17.2 us (6%)
  other arithmetic  16.3 us (6%)
  starting transfers between devices  15 us (5%)
  matrix products  9.59 us (3%)
    all_to_all x3, blocking collectives, _all_gather_a2a(): out = lax.all_to_all(copies, axes, 0, 0, tiled=True)  84.1 us
    all_to_all x1, blocking collectives, local(): grad = jnp.sum(lax.all_to_all(grad, near, 0, 0, tiled=True), axis=0)  53.7 us
    all_to_all x1, waiting for transfers between devices, _reduce_scatter_a2a(): return jnp.sum(lax.all_to_all(blocks, axes, 0, 0, tiled=True), axis=0)  45.6 us
    all_to_all x1, blocking collectives, _all_reduce_a2a(): return jnp.sum(lax.all_to_all(copies, axes, 0, 0, tiled=True), axis=0)  18.3 us
    all_to_all x1, waiting for transfers between devices, local(): hidden_grad = jnp.sum(lax.all_to_all(grad, 'zh', 0, 0, tiled=True), axis=0)  13.9 us
    all_to_all x1, starting transfers between devices, _reduce_scatter_a2a(): return jnp.sum(lax.all_to_all(blocks, axes, 0, 0, tiled=True), axis=0)  6.49 us
  transfers between devices with their start and end apart: 3, of which 3 were waited for; matrix products, arithmetic and copies ran while one was open for 2% of the time, Pallas kernels for 0%

profile of v7, /device:TPU:1, one launch (start us, length us, event | category | flops | bytes accessed | tf_op | source)
XLA Modules:
  0.0 276.8 jit_solution(10887105773157480883)
XLA Ops:
  0.6 0.9 broadcast_in_dim.12
  1.5 28.1 %all_to_all.42 = bf16[4,8,1024]{2,1,0:T(8,128)(2,1)S(1)} all-to-all(bf16[4,8,1024]{2,1,0:T(8,128)(2,1)S(1)} %broadcast_in_dim.12), channel_id=1, replica_groups=mesh['x'=4,'yh'=2,'zh'=4,'zl'=4,'yl'=2,'c'=2] {'zh'}, dimensions={0} | all-to-all | bytes 131072 | tf_op jit(solution)/shard_map/all_to_all | solution.py:31
  29.6 0.1 broadcast_in_dim.14
  29.7 31.3 %all_to_all.43 = bf16[16,32,1024]{2,1,0:T(8,128)(2,1)S(1)} all-to-all(bf16[16,32,1024]{2,1,0:T(8,128)(2,1)S(1)} %broadcast_in_dim.14), channel_id=1, replica_groups=mesh['x'=4,'yh'=2,'zh'=4,'zl'=4,'yl'=2,'c'=2] {'zl','yl','c'}, dimensions={0} | all-to-all | bytes 2097152 | tf_op jit(solution)/shard_map/all_to_all | solution.py:31
  61.0 0.1 copy.28
  61.1 3.6 %convolution_bitcast_fusion = f32[8,512,192]{1,2,0:T(8,128)} fusion(bf16[512,1024,1]{1,0,2:T(8,128)(2,1)S(1)} %bitcast.42, bf16[8,192,1024]{2,1,0:T(8,128)(2,1)S(1)} %bitcast.37), kind=kOutput, calls=%fused_computation.2 | convolution fusion | flops 1610612736 | bytes 7340032 | tf_op jit(solution)/shard_map/dot_general | solution.py:93
  64.7 6.5 %all-to-all-start.2 = ((f32[8,512,192]{1,2,0:T(8,128)}), f32[8,512,192]{1,2,0:T(8,128)}, u32[]{:S(2)}, u32[]{:S(2)}) async-start(f32[8,512,192]{1,2,0:T(8,128)} %convolution_bitcast_fusion), calls=%async_computation.2 | async-start | bytes 6291456 | tf_op jit(solution)/shard_map/all_to_all | solution.py:39
  71.2 0.1 fusion.10
  71.2 45.6 %all-to-all-done.2 = f32[8,512,192]{1,2,0:T(8,128)} async-done(((f32[8,512,192]{1,2,0:T(8,128)}), f32[8,512,192]{1,2,0:T(8,128)}, u32[]{:S(2)}, u32[]{:S(2)}) %all-to-all-start.2) | async-done | bytes 3145760 | tf_op jit(solution)/shard_map/all_to_all | solution.py:39
  116.9 2.3 reduce_sum.110
  119.1 1.0 copy.29
  120.1 1.6 fusion.9
  121.7 0.6 multiply_reduce_fusion
  122.4 0.7 fusion.12
  123.1 1.4 reshape.134
  124.4 0.8 pad_maximum_fusion.1
  125.2 18.3 %all_to_all.44 = f32[64,1,24]{2,1,0:T(1,128)} all-to-all(f32[64,1,24]{2,1,0:T(1,128)S(1)} %broadcast_in_dim.15), channel_id=1, replica_groups=mesh['x'=4,'yh'=2,'zh'=4,'zl'=4,'yl'=2,'c'=2] {'zh','zl','yl','c'}, dimensions={0} | all-to-all | bytes 12288 | tf_op jit(solution)/shard_map/all_to_all | solution.py:45
  143.5 1.4 reduce_sum.114
  144.8 1.2 broadcast_in_dim.16
  146.1 5.2 %all-to-all-start.4 = ((f32[8,1,24]{2,1,0:T(1,128)}), f32[8,1,24]{2,1,0:T(1,128)}, u32[]{:S(2)}, u32[]{:S(2)}) async-start(f32[8,1,24]{2,1,0:T(1,128)} %broadcast_in_dim.16), calls=%async_computation.4 | async-start | bytes 8192 | tf_op jit(solution)/shard_map/all_to_all | solution.py:45
  151.2 1.3 reshape.137
  152.6 0.8 div.69
  153.4 2.0 copy.33
  155.4 2.4 all-to-all-done.4
  157.8 0.7 reduce_sum.115
  158.5 0.1 add_rsqrt_fusion
  158.5 0.6 broadcast_multiply_fusion.2
  159.1 0.7 reshape.135
  159.8 0.9 exponential_reduce_fusion
  160.7 1.4 multiply_reduce_fusion.2
  162.1 0.7 multiply_multiply_fusion.5
  162.8 0.1 slice_multiply_fusion.1
  162.9 0.9 convolution_add_fusion.1
  163.8 0.9 convolution_add_fusion
  164.7 0.8 mul.168
  165.6 2.0 copy.32
  167.6 1.6 divide_convert_fusion
  169.2 0.1 broadcast_in_dim.17
  169.3 24.7 %all_to_all.45 = bf16[8,1,512,192]{2,3,1,0:T(8,128)(2,1)} all-to-all(bf16[8,1,512,192]{2,3,1,0:T(8,128)(2,1)S(1)} %broadcast_in_dim.17), channel_id=1, replica_groups=mesh['x'=4,'yh'=2,'zh'=4,'zl'=4,'yl'=2,'c'=2] {'x','yh'}, dimensions={0} | all-to-all | bytes 3145728 | tf_op jit(solution)/shard_map/all_to_all | solution.py:31
  194.1 4.4 %copy.34 = bf16[8,1,512,192]{3,0,2,1:T(8,128)(2,1)} copy(bf16[8,1,512,192]{2,3,1,0:T(8,128)(2,1)} %all_to_all.45) | data formatting | bytes 3145728 | tf_op jit(solution)/shard_map/all_to_all | solution.py:31
  198.5 3.5 %fusion.2 = f32[16,4,8,1024]{3,2,0,1:T(8,128)S(1)} fusion(bf16[8,192,1024,1,1]{2,1,0,4,3:T(8,128)(2,1)S(1)} %bitcast.36, bf16[4,16,8,8,192]{4,3,2,1,0:T(8,128)(2,1)} %bitcast.39), kind=kOutput, calls=%fused_computation.3 | convolution fusion | flops 1610612736 | bytes 6815744 | tf_op jit(solution)/shard_map/dot_general | solution.py:148
  202.0 0.2 copy.36
  202.2 53.7 %all_to_all.46 = f32[16,4,8,1024]{3,2,1,0:T(8,128)} all-to-all(f32[16,4,8,1024]{3,2,1,0:T(8,128)S(1)} %copy.36), channel_id=1, replica_groups=mesh['x'=4,'yh'=2,'zh'=4,'zl'=4,'yl'=2,'c'=2] {'zl','yl','c'}, dimensions={0} | all-to-all | bytes 4194304 | tf_op jit(solution)/shard_map/all_to_all | solution.py:154
  255.9 2.4 reduce_sum.119
  258.3 3.3 %all-to-all-start.7 = ((f32[4,8,1024]{2,1,0:T(8,128)}), f32[4,8,1024]{2,1,0:T(8,128)S(1)}, u32[]{:S(2)}, u32[]{:S(2)}) async-start(f32[4,8,1024]{2,1,0:T(8,128)} %reduce_sum.119), calls=%async_computation.7 | async-start | bytes 262144 | tf_op jit(solution)/shard_map/all_to_all | solution.py:155
  261.6 0.6 subtract_reduce_fusion
  262.2 13.9 %all-to-all-done.7 = f32[4,8,1024]{2,1,0:T(8,128)S(1)} async-done(((f32[4,8,1024]{2,1,0:T(8,128)}), f32[4,8,1024]{2,1,0:T(8,128)S(1)}, u32[]{:S(2)}, u32[]{:S(2)}) %all-to-all-start.7) | async-done | bytes 131104 | tf_op jit(solution)/shard_map/all_to_all | solution.py:155
  276.2 0.6 reduce_sum.120
  (19 shorter events, 0.1 us)
Async XLA Ops:
  0.6 60.4 %copy-start = (bf16[1536,1024]{1,0:T(8,128)(2,1)S(1)}, bf16[1536,1024]{1,0:T(8,128)(2,1)}, u32[]{:S(2)}) copy-start(bf16[1536,1024]{1,0:T(8,128)(2,1)} %param.5) | copy-start | bytes 9437188
  64.7 6.5 %copy-start.6 = (s32[8]{0:T(128)S(1)}, s32[8]{0:T(128)}, u32[]{:S(2)}) copy-start(s32[8]{0:T(128)} %param.6) | copy-start | bytes 100
  64.7 52.2 %all-to-all-start.2 = ((f32[8,512,192]{1,2,0:T(8,128)}), f32[8,512,192]{1,2,0:T(8,128)}, u32[]{:S(2)}, u32[]{:S(2)}) async-start(f32[8,512,192]{1,2,0:T(8,128)} %convolution_bitcast_fusion), calls=%async_computation.2 | async-start | bytes 6291456 | tf_op jit(solution)/shard_map/all_to_all | solution.py:39
  71.2 48.9 %copy-start.1 = (f32[8,64]{1,0:T(8,128)}, f32[8,64]{1,0:T(8,128)S(1)}, u32[]{:S(2)}) copy-start(f32[8,64]{1,0:T(8,128)S(1)} %fusion.10) | copy-start | bytes 6148
  146.1 11.7 %all-to-all-start.4 = ((f32[8,1,24]{2,1,0:T(1,128)}), f32[8,1,24]{2,1,0:T(1,128)}, u32[]{:S(2)}, u32[]{:S(2)}) async-start(f32[8,1,24]{2,1,0:T(1,128)} %broadcast_in_dim.16), calls=%async_computation.4 | async-start | bytes 8192 | tf_op jit(solution)/shard_map/all_to_all | solution.py:45
  153.4 14.2 %copy-start.2 = (f32[512]{0:T(512)S(1)}, f32[512]{0:T(512)}, u32[]{:S(2)}) copy-start(f32[512]{0:T(512)} %reshape.137) | copy-start | bytes 6148
  158.5 0.7 copy-start.3
  160.7 1.4 copy-start.4
  255.9 5.7 %copy-start.5 = (f32[4]{0:T(128)S(1)}, f32[4]{0:T(128)}, u32[]{:S(2)}) copy-start(f32[4]{0:T(128)} %copy-done.4) | copy-start | bytes 52
  255.9 5.7 %copy-start.7 = (f32[4]{0:T(128)S(1)}, f32[4]{0:T(128)}, u32[]{:S(2)}) copy-start(f32[4]{0:T(128)} %get-tuple-element.4) | copy-start | bytes 52
  258.3 17.9 %all-to-all-start.7 = ((f32[4,8,1024]{2,1,0:T(8,128)}), f32[4,8,1024]{2,1,0:T(8,128)S(1)}, u32[]{:S(2)}, u32[]{:S(2)}) async-start(f32[4,8,1024]{2,1,0:T(8,128)} %reduce_sum.119), calls=%async_computation.7 | async-start | bytes 262144 | tf_op jit(solution)/shard_map/all_to_all | solution.py:155

commit v8 on v7

--- a/solution.py
+++ b/solution.py
@@ -148,10 +148,13 @@
     partial_grad = lax.dot_general(
         dlogit, weight, (((0, 2), (0, 1)), ((), ())), preferred_element_type=jnp.float32
     )
-    n_near = _members(near)
+    n_zl, n_yl, n_c = (lax.axis_size(a) for a in near)
     rows = hidden.shape[0]
-    grad = partial_grad.reshape(n_zh, n_near, rows, partial_grad.shape[1]).transpose(1, 0, 2, 3)
-    grad = jnp.sum(lax.all_to_all(grad, near, 0, 0, tiled=True), axis=0)
+    width = partial_grad.shape[1]
+    grad = partial_grad.reshape(n_zh, n_zl, n_yl, n_c, rows, width).transpose(3, 0, 1, 2, 4, 5)
+    grad = jnp.sum(lax.all_to_all(grad, "c", 0, 0, tiled=True), axis=0)
+    grad = grad.transpose(1, 2, 0, 3, 4).reshape(n_zl * n_yl, n_zh, rows, width)
+    grad = jnp.sum(lax.all_to_all(grad, ("zl", "yl"), 0, 0, tiled=True), axis=0)
     hidden_grad = jnp.sum(lax.all_to_all(grad, "zh", 0, 0, tiled=True), axis=0)
     return (hidden_grad, loss)
 

time: 278 us -> 265 us (0.953)
  blocking collectives: 156 us -> 140 us
    all_to_all x1 -> x2, blocking collectives: 53.7 us -> 37.4 us  [the longest x1 28.6 us: local(): grad = jnp.sum(lax.all_to_all(grad, ('zl', 'yl'), 0, 0, tiled=True), axis=0)]
where the time goes in v8:
time: 265 us; the launch traced here: 262 us
  blocking collectives  140 us (53%)
  waiting for transfers between devices  59.6 us (22%)
  other arithmetic  18.7 us (7%)
  local copies, waits for them, and re-layouts  18.5 us (7%)
  starting transfers between devices  15 us (6%)
  matrix products  9.59 us (4%)
    all_to_all x3, blocking collectives, _all_gather_a2a(): out = lax.all_to_all(copies, axes, 0, 0, tiled=True)  84.1 us
    all_to_all x1, waiting for transfers between devices, _reduce_scatter_a2a(): return jnp.sum(lax.all_to_all(blocks, axes, 0, 0, tiled=True), axis=0)  45.6 us
    all_to_all x1, blocking collectives, local(): grad = jnp.sum(lax.all_to_all(grad, ('zl', 'yl'), 0, 0, tiled=True), axis=0)  28.6 us
    all_to_all x1, blocking collectives, _all_reduce_a2a(): return jnp.sum(lax.all_to_all(copies, axes, 0, 0, tiled=True), axis=0)  18.3 us
    all_to_all x1, waiting for transfers between devices, local(): hidden_grad = jnp.sum(lax.all_to_all(grad, 'zh', 0, 0, tiled=True), axis=0)  11.6 us
    all_to_all x1, blocking collectives, local(): grad = jnp.sum(lax.all_to_all(grad, 'c', 0, 0, tiled=True), axis=0)  8.79 us
    all_to_all x1, starting transfers between devices, _reduce_scatter_a2a(): return jnp.sum(lax.all_to_all(blocks, axes, 0, 0, tiled=True), axis=0)  6.49 us
  transfers between devices with their start and end apart: 3, of which 3 were waited for; matrix products, arithmetic and copies ran while one was open for 2% of the time, Pallas kernels for 0%

profile of v8, /device:TPU:1, one launch (start us, length us, event | category | flops | bytes accessed | tf_op | source)
XLA Modules:
  0.0 261.9 jit_solution(1192540732920995253)
XLA Ops:
  0.6 0.9 broadcast_in_dim.12
  1.5 28.1 %all_to_all.47 = bf16[4,8,1024]{2,1,0:T(8,128)(2,1)S(1)} all-to-all(bf16[4,8,1024]{2,1,0:T(8,128)(2,1)S(1)} %broadcast_in_dim.12), channel_id=1, replica_groups=mesh['x'=4,'yh'=2,'zh'=4,'zl'=4,'yl'=2,'c'=2] {'zh'}, dimensions={0} | all-to-all | bytes 131072 | tf_op jit(solution)/shard_map/all_to_all | solution.py:31
  29.6 0.1 broadcast_in_dim.14
  29.7 31.3 %all_to_all.48 = bf16[16,32,1024]{2,1,0:T(8,128)(2,1)S(1)} all-to-all(bf16[16,32,1024]{2,1,0:T(8,128)(2,1)S(1)} %broadcast_in_dim.14), channel_id=1, replica_groups=mesh['x'=4,'yh'=2,'zh'=4,'zl'=4,'yl'=2,'c'=2] {'zl','yl','c'}, dimensions={0} | all-to-all | bytes 2097152 | tf_op jit(solution)/shard_map/all_to_all | solution.py:31
  61.0 0.1 copy.37
  61.1 3.6 %convolution_bitcast_fusion = f32[8,512,192]{1,2,0:T(8,128)} fusion(bf16[512,1024,1]{1,0,2:T(8,128)(2,1)S(1)} %bitcast.46, bf16[8,192,1024]{2,1,0:T(8,128)(2,1)S(1)} %bitcast.40), kind=kOutput, calls=%fused_computation.2 | convolution fusion | flops 1610612736 | bytes 7340032 | tf_op jit(solution)/shard_map/dot_general | solution.py:93
  64.7 6.5 %all-to-all-start.2 = ((f32[8,512,192]{1,2,0:T(8,128)}), f32[8,512,192]{1,2,0:T(8,128)}, u32[]{:S(2)}, u32[]{:S(2)}) async-start(f32[8,512,192]{1,2,0:T(8,128)} %convolution_bitcast_fusion), calls=%async_computation.2 | async-start | bytes 6291456 | tf_op jit(solution)/shard_map/all_to_all | solution.py:39
  71.2 45.6 %all-to-all-done.2 = f32[8,512,192]{1,2,0:T(8,128)} async-done(((f32[8,512,192]{1,2,0:T(8,128)}), f32[8,512,192]{1,2,0:T(8,128)}, u32[]{:S(2)}, u32[]{:S(2)}) %all-to-all-start.2) | async-done | bytes 3145760 | tf_op jit(solution)/shard_map/all_to_all | solution.py:39
  116.9 2.3 reduce_sum.119
  119.1 1.0 copy.38
  120.1 1.6 fusion.9
  121.7 0.6 multiply_reduce_fusion
  122.4 0.7 fusion.12
  123.1 1.4 reshape.137
  124.4 0.8 pad_maximum_fusion.1
  125.2 18.3 %all_to_all.49 = f32[64,1,24]{2,1,0:T(1,128)} all-to-all(f32[64,1,24]{2,1,0:T(1,128)S(1)} %broadcast_in_dim.15), channel_id=1, replica_groups=mesh['x'=4,'yh'=2,'zh'=4,'zl'=4,'yl'=2,'c'=2] {'zh','zl','yl','c'}, dimensions={0} | all-to-all | bytes 12288 | tf_op jit(solution)/shard_map/all_to_all | solution.py:45
  143.5 1.4 reduce_sum.123
  144.8 1.2 broadcast_in_dim.16
  146.1 5.2 %all-to-all-start.4 = ((f32[8,1,24]{2,1,0:T(1,128)}), f32[8,1,24]{2,1,0:T(1,128)}, u32[]{:S(2)}, u32[]{:S(2)}) async-start(f32[8,1,24]{2,1,0:T(1,128)} %broadcast_in_dim.16), calls=%async_computation.4 | async-start | bytes 8192 | tf_op jit(solution)/shard_map/all_to_all | solution.py:45
  151.2 1.3 reshape.141
  152.6 0.8 div.69
  153.4 2.0 copy.42
  155.4 2.4 all-to-all-done.4
  157.8 0.7 reduce_sum.124
  158.5 0.6 broadcast_multiply_fusion.2
  159.1 0.7 reshape.138
  159.8 0.9 exponential_reduce_fusion
  160.7 1.4 multiply_reduce_fusion.2
  162.1 0.7 multiply_multiply_fusion.5
  162.9 0.9 convolution_add_fusion.1
  163.8 0.9 convolution_add_fusion
  164.7 0.8 mul.168
  165.6 2.0 copy.41
  167.6 1.6 divide_convert_fusion
  169.2 0.1 broadcast_in_dim.17
  169.3 24.7 %all_to_all.50 = bf16[8,1,512,192]{2,3,1,0:T(8,128)(2,1)} all-to-all(bf16[8,1,512,192]{2,3,1,0:T(8,128)(2,1)S(1)} %broadcast_in_dim.17), channel_id=1, replica_groups=mesh['x'=4,'yh'=2,'zh'=4,'zl'=4,'yl'=2,'c'=2] {'x','yh'}, dimensions={0} | all-to-all | bytes 3145728 | tf_op jit(solution)/shard_map/all_to_all | solution.py:31
  194.1 4.4 %copy.43 = bf16[8,1,512,192]{3,0,2,1:T(8,128)(2,1)} copy(bf16[8,1,512,192]{2,3,1,0:T(8,128)(2,1)} %all_to_all.50) | data formatting | bytes 3145728 | tf_op jit(solution)/shard_map/all_to_all | solution.py:31
  198.5 3.5 %fusion.2 = f32[2,4,4,2,8,1024]{5,4,0,3,2,1:T(8,128)S(1)} fusion(bf16[8,192,1024,1,1,1,1]{2,1,0,6,5,4,3:T(8,128)(2,1)S(1)} %bitcast.39, bf16[4,4,2,2,8,8,192]{6,5,4,3,2,1,0:T(8,128)(2,1)} %bitcast.43), kind=kOutput, calls=%fused_computation.3 | convolution fusion | flops 1610612736 | bytes 6815744 | tf_op jit(solution)/shard_map/dot_general | solution.py:148
  202.0 0.2 copy.45
  202.2 8.8 %all_to_all.51 = f32[2,4,4,2,8,1024]{5,4,3,2,1,0:T(8,128)} all-to-all(f32[2,4,4,2,8,1024]{5,4,3,2,1,0:T(8,128)S(1)} %copy.45), channel_id=1, replica_groups=mesh['x'=4,'yh'=2,'zh'=4,'zl'=4,'yl'=2,'c'=2] {'c'}, dimensions={0} | all-to-all | bytes 4194304 | tf_op jit(solution)/shard_map/all_to_all | solution.py:155
  211.0 2.8 %reduce_sum.128 = f32[4,4,2,8,1024]{4,3,2,1,0:T(8,128)} reduce(f32[2,4,4,2,8,1024]{5,4,3,2,1,0:T(8,128)} %all_to_all.51, f32[]{:T(128)} %constant.8.clone.1), dimensions={0}, to_apply=%region_8.9 | reduce | flops 262144 | bytes 3145732 | tf_op jit(solution)/shard_map/reduce_sum | solution.py:155
  213.8 1.3 copy.46
  215.2 28.6 %all_to_all.52 = f32[8,4,8,1024]{3,2,1,0:T(8,128)} all-to-all(f32[8,4,8,1024]{3,2,1,0:T(8,128)S(1)} %copy.46), channel_id=1, replica_groups=mesh['x'=4,'yh'=2,'zh'=4,'zl'=4,'yl'=2,'c'=2] {'zl','yl'}, dimensions={0} | all-to-all | bytes 2097152 | tf_op jit(solution)/shard_map/all_to_all | solution.py:157
  243.8 1.9 reduce_sum.129
  245.7 3.3 %all-to-all-start.8 = ((f32[4,8,1024]{2,1,0:T(8,128)}), f32[4,8,1024]{2,1,0:T(8,128)S(1)}, u32[]{:S(2)}, u32[]{:S(2)}) async-start(f32[4,8,1024]{2,1,0:T(8,128)} %reduce_sum.129), calls=%async_computation.8 | async-start | bytes 262144 | tf_op jit(solution)/shard_map/all_to_all | solution.py:158
  249.0 0.6 subtract_reduce_fusion
  249.7 11.6 %all-to-all-done.8 = f32[4,8,1024]{2,1,0:T(8,128)S(1)} async-done(((f32[4,8,1024]{2,1,0:T(8,128)}), f32[4,8,1024]{2,1,0:T(8,128)S(1)}, u32[]{:S(2)}, u32[]{:S(2)}) %all-to-all-start.8) | async-done | bytes 131104 | tf_op jit(solution)/shard_map/all_to_all | solution.py:158
  261.2 0.6 reduce_sum.130
  (22 shorter events, 0.3 us)
Async XLA Ops:
  0.6 60.4 %copy-start = (bf16[1536,1024]{1,0:T(8,128)(2,1)S(1)}, bf16[1536,1024]{1,0:T(8,128)(2,1)}, u32[]{:S(2)}) copy-start(bf16[1536,1024]{1,0:T(8,128)(2,1)} %param.5) | copy-start | bytes 9437188
  64.7 6.5 %copy-start.6 = (s32[8]{0:T(128)S(1)}, s32[8]{0:T(128)}, u32[]{:S(2)}) copy-start(s32[8]{0:T(128)} %param.6) | copy-start | bytes 100
  64.7 52.2 %all-to-all-start.2 = ((f32[8,512,192]{1,2,0:T(8,128)}), f32[8,512,192]{1,2,0:T(8,128)}, u32[]{:S(2)}, u32[]{:S(2)}) async-start(f32[8,512,192]{1,2,0:T(8,128)} %convolution_bitcast_fusion), calls=%async_computation.2 | async-start | bytes 6291456 | tf_op jit(solution)/shard_map/all_to_all | solution.py:39
  71.2 48.9 %copy-start.1 = (f32[8,64]{1,0:T(8,128)}, f32[8,64]{1,0:T(8,128)S(1)}, u32[]{:S(2)}) copy-start(f32[8,64]{1,0:T(8,128)S(1)} %fusion.10) | copy-start | bytes 6148
  146.1 11.7 %all-to-all-start.4 = ((f32[8,1,24]{2,1,0:T(1,128)}), f32[8,1,24]{2,1,0:T(1,128)}, u32[]{:S(2)}, u32[]{:S(2)}) async-start(f32[8,1,24]{2,1,0:T(1,128)} %broadcast_in_dim.16), calls=%async_computation.4 | async-start | bytes 8192 | tf_op jit(solution)/shard_map/all_to_all | solution.py:45
  153.4 14.2 %copy-start.2 = (f32[512]{0:T(512)S(1)}, f32[512]{0:T(512)}, u32[]{:S(2)}) copy-start(f32[512]{0:T(512)} %reshape.141) | copy-start | bytes 6148
  158.5 0.7 copy-start.3
  160.7 1.4 copy-start.4
  215.2 33.9 %copy-start.5 = (f32[4]{0:T(128)S(1)}, f32[4]{0:T(128)}, u32[]{:S(2)}) copy-start(f32[4]{0:T(128)} %copy-done.4) | copy-start | bytes 52
  215.2 33.9 %copy-start.7 = (f32[4]{0:T(128)S(1)}, f32[4]{0:T(128)}, u32[]{:S(2)}) copy-start(f32[4]{0:T(128)} %get-tuple-element.4) | copy-start | bytes 52
  245.7 15.5 %all-to-all-start.8 = ((f32[4,8,1024]{2,1,0:T(8,128)}), f32[4,8,1024]{2,1,0:T(8,128)S(1)}, u32[]{:S(2)}, u32[]{:S(2)}) async-start(f32[4,8,1024]{2,1,0:T(8,128)} %reduce_sum.129), calls=%async_computation.8 | async-start | bytes 262144 | tf_op jit(solution)/shard_map/all_to_all | solution.py:158

commit v9 on v8

--- a/solution.py
+++ b/solution.py
@@ -30,6 +30,11 @@
     copies = jnp.broadcast_to(x[None], (n,) + x.shape)
     out = lax.all_to_all(copies, axes, 0, 0, tiled=True)
     return out.reshape((n * x.shape[0],) + x.shape[1:])
+
+
+def _copies_a2a(x, axes):
+    n = _members(axes)
+    return lax.all_to_all(jnp.broadcast_to(x[None], (n,) + x.shape), axes, 0, 0, tiled=True)
 
 
 def _reduce_scatter_a2a(x, axes):
@@ -82,11 +87,11 @@
 def local(hidden, head_weight, lengths, pairing):
     half = NSEQ // 2
     near = ("zl", "yl", "c")
-    gathered = _all_gather_a2a(hidden, "zh")
     n_zh = lax.axis_size("zh")
-    gathered = _all_gather_a2a(gathered, near)
-    gathered = gathered.reshape(_members(near), n_zh, hidden.shape[0], hidden.shape[1])
-    gathered = gathered.transpose(1, 0, 2, 3).reshape(-1, hidden.shape[1])
+    gathered = _copies_a2a(hidden, "zh")
+    gathered = _copies_a2a(gathered, ("zl", "yl"))
+    gathered = _copies_a2a(gathered, "c")
+    gathered = gathered.transpose(2, 1, 0, 3, 4).reshape(-1, hidden.shape[1])
     total_rows = gathered.shape[0]
     seq_len = total_rows // NSEQ
     n_x = lax.axis_size("x")

time: 265 us -> 256 us (0.966)
  blocking collectives: 140 us -> 132 us
    all_to_all x3 -> x1, blocking collectives: 84.1 us -> 24.7 us  [_all_gather_a2a(): out = lax.all_to_all(copies, axes, 0, 0, tiled=True)]
    all_to_all x0 -> x3, blocking collectives: none -> 51.5 us  [_copies_a2a(): lax.all_to_all(jnp.broadcast_to(x[None], (n,) + x.shape), axes, 0, 0, til...]
where the time goes in v9:
time: 256 us; the launch traced here: 253 us
  blocking collectives  132 us (52%)
  waiting for transfers between devices  59 us (23%)
  other arithmetic  18.7 us (7%)
  local copies, waits for them, and re-layouts  18.6 us (7%)
  starting transfers between devices  14.1 us (6%)
  matrix products  9.59 us (4%)
    all_to_all x3, blocking collectives, _copies_a2a(): lax.all_to_all(jnp.broadcast_to(x[None], (n,) + x.shape), axes, 0, 0, til...  51.5 us
    all_to_all x1, waiting for transfers between devices, _reduce_scatter_a2a(): return jnp.sum(lax.all_to_all(blocks, axes, 0, 0, tiled=True), axis=0)  45 us
    all_to_all x1, blocking collectives, local(): grad = jnp.sum(lax.all_to_all(grad, ('zl', 'yl'), 0, 0, tiled=True), axis=0)  28.6 us
    all_to_all x1, blocking collectives, _all_gather_a2a(): out = lax.all_to_all(copies, axes, 0, 0, tiled=True)  24.7 us
    all_to_all x1, blocking collectives, _all_reduce_a2a(): return jnp.sum(lax.all_to_all(copies, axes, 0, 0, tiled=True), axis=0)  18.7 us
    all_to_all x1, waiting for transfers between devices, local(): hidden_grad = jnp.sum(lax.all_to_all(grad, 'zh', 0, 0, tiled=True), axis=0)  11.6 us
    all_to_all x1, blocking collectives, local(): grad = jnp.sum(lax.all_to_all(grad, 'c', 0, 0, tiled=True), axis=0)  8.79 us
    all_to_all x1, starting transfers between devices, _reduce_scatter_a2a(): return jnp.sum(lax.all_to_all(blocks, axes, 0, 0, tiled=True), axis=0)  6.48 us
  transfers between devices with their start and end apart: 3, of which 3 were waited for; matrix products, arithmetic and copies ran while one was open for 2% of the time, Pallas kernels for 0%

profile of v9, /device:TPU:1, one launch (start us, length us, event | category | flops | bytes accessed | tf_op | source)
XLA Modules:
  0.0 253.1 jit_solution(11741991473302375267)
XLA Ops:
  0.6 0.9 broadcast_in_dim.12
  1.5 28.1 %all_to_all.52 = bf16[4,8,1024]{2,1,0:T(8,128)(2,1)S(1)} all-to-all(bf16[4,8,1024]{2,1,0:T(8,128)(2,1)S(1)} %broadcast_in_dim.12), channel_id=1, replica_groups=mesh['x'=4,'yh'=2,'zh'=4,'zl'=4,'yl'=2,'c'=2] {'zh'}, dimensions={0} | all-to-all | bytes 131072 | tf_op jit(solution)/shard_map/all_to_all | solution.py:37
  29.6 17.1 %all_to_all.53 = bf16[8,4,8,1024]{3,2,1,0:T(8,128)(2,1)S(1)} all-to-all(bf16[8,4,8,1024]{3,2,1,0:T(8,128)(2,1)S(1)} %broadcast_in_dim.13), channel_id=1, replica_groups=mesh['x'=4,'yh'=2,'zh'=4,'zl'=4,'yl'=2,'c'=2] {'zl','yl'}, dimensions={0} | all-to-all | bytes 1048576 | tf_op jit(solution)/shard_map/all_to_all | solution.py:37
  46.8 0.1 broadcast_in_dim.14
  46.9 6.3 %all_to_all.54 = bf16[2,8,4,8,1024]{4,3,1,2,0:T(8,128)(2,1)S(1)} all-to-all(bf16[2,8,4,8,1024]{4,3,1,2,0:T(8,128)(2,1)S(1)} %broadcast_in_dim.14), channel_id=1, replica_groups=mesh['x'=4,'yh'=2,'zh'=4,'zl'=4,'yl'=2,'c'=2] {'c'}, dimensions={0} | all-to-all | bytes 2097152 | tf_op jit(solution)/shard_map/all_to_all | solution.py:37
  53.3 3.6 %convolution_bitcast_fusion = f32[8,512,192]{1,2,0:T(8,128)} fusion(bf16[512,1024,1]{1,0,2:T(8,128)(2,1)S(1)} %bitcast.43, bf16[8,192,1024]{2,1,0:T(8,128)(2,1)S(1)} %bitcast.37), kind=kOutput, calls=%fused_computation.2 | convolution fusion | flops 1610612736 | bytes 7340032 | tf_op jit(solution)/shard_map/dot_general | solution.py:98
  56.9 6.5 %all-to-all-start.3 = ((f32[8,512,192]{1,2,0:T(8,128)}), f32[8,512,192]{1,2,0:T(8,128)}, u32[]{:S(2)}, u32[]{:S(2)}) async-start(f32[8,512,192]{1,2,0:T(8,128)} %convolution_bitcast_fusion), calls=%async_computation.3 | async-start | bytes 6291456 | tf_op jit(solution)/shard_map/all_to_all | solution.py:44
  63.5 45.0 %all-to-all-done.3 = f32[8,512,192]{1,2,0:T(8,128)} async-done(((f32[8,512,192]{1,2,0:T(8,128)}), f32[8,512,192]{1,2,0:T(8,128)}, u32[]{:S(2)}, u32[]{:S(2)}) %all-to-all-start.3) | async-done | bytes 3145760 | tf_op jit(solution)/shard_map/all_to_all | solution.py:44
  108.5 2.3 reduce_sum.119
  110.7 1.0 copy.42
  111.7 1.6 fusion.9
  113.3 0.6 multiply_reduce_fusion
  113.9 0.7 fusion.12
  114.7 1.4 reshape.138
  116.0 0.8 pad_maximum_fusion.1
  116.8 18.7 %all_to_all.55 = f32[64,1,24]{2,1,0:T(1,128)} all-to-all(f32[64,1,24]{2,1,0:T(1,128)S(1)} %broadcast_in_dim.15), channel_id=1, replica_groups=mesh['x'=4,'yh'=2,'zh'=4,'zl'=4,'yl'=2,'c'=2] {'zh','zl','yl','c'}, dimensions={0} | all-to-all | bytes 12288 | tf_op jit(solution)/shard_map/all_to_all | solution.py:50
  135.5 1.4 reduce_sum.123
  136.9 1.2 broadcast_in_dim.16
  138.1 4.3 %all-to-all-start.5 = ((f32[8,1,24]{2,1,0:T(1,128)}), f32[8,1,24]{2,1,0:T(1,128)}, u32[]{:S(2)}, u32[]{:S(2)}) async-start(f32[8,1,24]{2,1,0:T(1,128)} %broadcast_in_dim.16), calls=%async_computation.5 | async-start | bytes 8192 | tf_op jit(solution)/shard_map/all_to_all | solution.py:50
  142.4 1.3 reshape.142
  143.8 0.8 div.69
  144.6 2.0 copy.46
  146.6 2.4 all-to-all-done.5
  149.0 0.7 reduce_sum.124
  149.7 0.6 broadcast_multiply_fusion.2
  150.3 0.7 reshape.139
  151.0 0.9 exponential_reduce_fusion
  151.9 1.4 multiply_reduce_fusion.2
  153.3 0.7 multiply_multiply_fusion.5
  154.1 0.9 convolution_add_fusion.1
  155.0 0.9 convolution_add_fusion
  155.9 0.8 mul.168
  156.8 2.0 copy.45
  158.8 1.6 divide_convert_fusion
  160.4 0.1 broadcast_in_dim.17
  160.5 24.7 %all_to_all.56 = bf16[8,1,512,192]{2,3,1,0:T(8,128)(2,1)} all-to-all(bf16[8,1,512,192]{2,3,1,0:T(8,128)(2,1)S(1)} %broadcast_in_dim.17), channel_id=1, replica_groups=mesh['x'=4,'yh'=2,'zh'=4,'zl'=4,'yl'=2,'c'=2] {'x','yh'}, dimensions={0} | all-to-all | bytes 3145728 | tf_op jit(solution)/shard_map/all_to_all | solution.py:31
  185.3 4.4 %copy.47 = bf16[8,1,512,192]{3,0,2,1:T(8,128)(2,1)} copy(bf16[8,1,512,192]{2,3,1,0:T(8,128)(2,1)} %all_to_all.56) | data formatting | bytes 3145728 | tf_op jit(solution)/shard_map/all_to_all | solution.py:31
  189.7 3.5 %fusion.2 = f32[2,4,4,2,8,1024]{5,4,0,3,2,1:T(8,128)S(1)} fusion(bf16[8,192,1024,1,1,1,1]{2,1,0,6,5,4,3:T(8,128)(2,1)S(1)} %bitcast.36, bf16[4,4,2,2,8,8,192]{6,5,4,3,2,1,0:T(8,128)(2,1)} %bitcast.40), kind=kOutput, calls=%fused_computation.3 | convolution fusion | flops 1610612736 | bytes 6815744 | tf_op jit(solution)/shard_map/dot_general | solution.py:153
  193.2 0.2 copy.49
  193.4 8.8 %all_to_all.57 = f32[2,4,4,2,8,1024]{5,4,3,2,1,0:T(8,128)} all-to-all(f32[2,4,4,2,8,1024]{5,4,3,2,1,0:T(8,128)S(1)} %copy.49), channel_id=1, replica_groups=mesh['x'=4,'yh'=2,'zh'=4,'zl'=4,'yl'=2,'c'=2] {'c'}, dimensions={0} | all-to-all | bytes 4194304 | tf_op jit(solution)/shard_map/all_to_all | solution.py:160
  202.2 2.8 %reduce_sum.128 = f32[4,4,2,8,1024]{4,3,2,1,0:T(8,128)} reduce(f32[2,4,4,2,8,1024]{5,4,3,2,1,0:T(8,128)} %all_to_all.57, f32[]{:T(128)} %constant.8.clone.1), dimensions={0}, to_apply=%region_8.9 | reduce | flops 262144 | bytes 3145732 | tf_op jit(solution)/shard_map/reduce_sum | solution.py:160
  205.0 1.3 copy.50
  206.4 28.6 %all_to_all.58 = f32[8,4,8,1024]{3,2,1,0:T(8,128)} all-to-all(f32[8,4,8,1024]{3,2,1,0:T(8,128)S(1)} %copy.50), channel_id=1, replica_groups=mesh['x'=4,'yh'=2,'zh'=4,'zl'=4,'yl'=2,'c'=2] {'zl','yl'}, dimensions={0} | all-to-all | bytes 2097152 | tf_op jit(solution)/shard_map/all_to_all | solution.py:162
  235.0 1.9 reduce_sum.129
  236.9 3.3 %all-to-all-start.9 = ((f32[4,8,1024]{2,1,0:T(8,128)}), f32[4,8,1024]{2,1,0:T(8,128)S(1)}, u32[]{:S(2)}, u32[]{:S(2)}) async-start(f32[4,8,1024]{2,1,0:T(8,128)} %reduce_sum.129), calls=%async_computation.9 | async-start | bytes 262144 | tf_op jit(solution)/shard_map/all_to_all | solution.py:163
  240.3 0.6 subtract_reduce_fusion
  240.9 11.6 %all-to-all-done.9 = f32[4,8,1024]{2,1,0:T(8,128)S(1)} async-done(((f32[4,8,1024]{2,1,0:T(8,128)}), f32[4,8,1024]{2,1,0:T(8,128)S(1)}, u32[]{:S(2)}, u32[]{:S(2)}) %all-to-all-start.9) | async-done | bytes 131104 | tf_op jit(solution)/shard_map/all_to_all | solution.py:163
  252.4 0.6 reduce_sum.130
  (25 shorter events, 0.5 us)
Async XLA Ops:
  0.6 52.7 %copy-start = (bf16[1536,1024]{1,0:T(8,128)(2,1)S(1)}, bf16[1536,1024]{1,0:T(8,128)(2,1)}, u32[]{:S(2)}) copy-start(bf16[1536,1024]{1,0:T(8,128)(2,1)} %param.5) | copy-start | bytes 9437188
  56.9 6.5 %copy-start.6 = (s32[8]{0:T(128)S(1)}, s32[8]{0:T(128)}, u32[]{:S(2)}) copy-start(s32[8]{0:T(128)} %param.6) | copy-start | bytes 100
  56.9 51.6 %all-to-all-start.3 = ((f32[8,512,192]{1,2,0:T(8,128)}), f32[8,512,192]{1,2,0:T(8,128)}, u32[]{:S(2)}, u32[]{:S(2)}) async-start(f32[8,512,192]{1,2,0:T(8,128)} %convolution_bitcast_fusion), calls=%async_computation.3 | async-start | bytes 6291456 | tf_op jit(solution)/shard_map/all_to_all | solution.py:44
  63.5 48.3 %copy-start.1 = (f32[8,64]{1,0:T(8,128)}, f32[8,64]{1,0:T(8,128)S(1)}, u32[]{:S(2)}) copy-start(f32[8,64]{1,0:T(8,128)S(1)} %fusion.10) | copy-start | bytes 6148
  138.1 10.9 %all-to-all-start.5 = ((f32[8,1,24]{2,1,0:T(1,128)}), f32[8,1,24]{2,1,0:T(1,128)}, u32[]{:S(2)}, u32[]{:S(2)}) async-start(f32[8,1,24]{2,1,0:T(1,128)} %broadcast_in_dim.16), calls=%async_computation.5 | async-start | bytes 8192 | tf_op jit(solution)/shard_map/all_to_all | solution.py:50
  144.6 14.2 %copy-start.2 = (f32[512]{0:T(512)S(1)}, f32[512]{0:T(512)}, u32[]{:S(2)}) copy-start(f32[512]{0:T(512)} %reshape.142) | copy-start | bytes 6148
  149.7 0.7 copy-start.3
  151.9 1.4 copy-start.4
  206.4 33.9 %copy-start.5 = (f32[4]{0:T(128)S(1)}, f32[4]{0:T(128)}, u32[]{:S(2)}) copy-start(f32[4]{0:T(128)} %copy-done.4) | copy-start | bytes 52
  206.4 33.9 %copy-start.7 = (f32[4]{0:T(128)S(1)}, f32[4]{0:T(128)}, u32[]{:S(2)}) copy-start(f32[4]{0:T(128)} %get-tuple-element.4) | copy-start | bytes 52
  236.9 15.5 %all-to-all-start.9 = ((f32[4,8,1024]{2,1,0:T(8,128)}), f32[4,8,1024]{2,1,0:T(8,128)S(1)}, u32[]{:S(2)}, u32[]{:S(2)}) async-start(f32[4,8,1024]{2,1,0:T(8,128)} %reduce_sum.129), calls=%async_computation.9 | async-start | bytes 262144 | tf_op jit(solution)/shard_map/all_to_all | solution.py:163

commit v10 on v9

--- a/solution.py
+++ b/solution.py
@@ -1,6 +1,7 @@
 import jax
 import jax.numpy as jnp
 from jax import lax
+from jax.experimental.layout import Layout, with_layout_constraint
 from jax.sharding import Mesh
 from jax.sharding import PartitionSpec as P
 
@@ -102,6 +103,7 @@
         preferred_element_type=jnp.float32,
     )
     logits = _reduce_scatter_a2a(partial_logits, SEC)
+    logits = with_layout_constraint(logits, Layout((0, 1)))
     columns = logits.shape[1]
     soft = jax.nn.softplus(logits)
     act = jnp.log1p(soft)
@@ -147,6 +149,7 @@
     dpooled = jnp.concatenate([dpool_q, dpool_d], axis=0)
     dact = (dpooled[:, None, :] * expo / totals[:, None, :]).reshape(total_rows, columns)
     dlogit = (dact * jax.nn.sigmoid(logits) / (1.0 + soft)).astype(jnp.bfloat16)
+    dlogit = with_layout_constraint(dlogit, Layout((0, 1)))
     n_sec = _members(SEC)
     dlogit = _all_gather_a2a(dlogit[None], SEC)
     weight = head_weight.reshape(n_sec, columns, head_weight.shape[1])

time: 256 us -> 243 us (0.949)
  local copies, waits for them, and re-layouts: 18.6 us -> 10.2 us
  other arithmetic: 18.7 us -> 13.4 us
  waiting for transfers between devices: 59 us -> 62.9 us
    all_to_all x1, waiting for transfers between devices: 2.39 us -> 6.35 us  [_all_reduce_a2a(): return jnp.sum(lax.all_to_all(copies, axes, 0, 0, tiled=True), axis=0)]
    mul x2 -> x0, local copies, waits for them, and re-layouts: 2.81 us -> none  [local(): dpooled[:, None, :] * expo / totals[:, None, :]]
    div x2 -> x0, local copies, waits for them, and re-layouts: 2.81 us -> none  [local(): dpooled[:, None, :] * expo / totals[:, None, :]]
  transfers between devices with their start and end apart: 3 -> 3, of which waited for: 3 -> 3; matrix products, arithmetic and copies ran while one was open for 2% -> 0% of each run, Pallas kernels for 0% -> 0%
where the time goes in v10:
time: 243 us; the launch traced here: 240 us
  blocking collectives  131 us (54%)
  waiting for transfers between devices  62.9 us (26%)
  starting transfers between devices  14.7 us (6%)
  other arithmetic  13.4 us (6%)
  local copies, waits for them, and re-layouts  10.2 us (4%)
  matrix products  7.68 us (3%)
    all_to_all x3, blocking collectives, _copies_a2a(): lax.all_to_all(jnp.broadcast_to(x[None], (n,) + x.shape), axes, 0, 0, til...  51.5 us
    all_to_all x1, waiting for transfers between devices, _reduce_scatter_a2a(): return jnp.sum(lax.all_to_all(blocks, axes, 0, 0, tiled=True), axis=0)  45 us
    all_to_all x1, blocking collectives, local(): grad = jnp.sum(lax.all_to_all(grad, ('zl', 'yl'), 0, 0, tiled=True), axis=0)  28.6 us
    all_to_all x1, blocking collectives, _all_gather_a2a(): out = lax.all_to_all(copies, axes, 0, 0, tiled=True)  22.9 us
    all_to_all x1, blocking collectives, _all_reduce_a2a(): return jnp.sum(lax.all_to_all(copies, axes, 0, 0, tiled=True), axis=0)  18.1 us
    all_to_all x1, waiting for transfers between devices, local(): hidden_grad = jnp.sum(lax.all_to_all(grad, 'zh', 0, 0, tiled=True), axis=0)  11.6 us
    all_to_all x1, blocking collectives, local(): grad = jnp.sum(lax.all_to_all(grad, 'c', 0, 0, tiled=True), axis=0)  9.62 us
    all_to_all x1, starting transfers between devices, _reduce_scatter_a2a(): return jnp.sum(lax.all_to_all(blocks, axes, 0, 0, tiled=True), axis=0)  6.48 us
  transfers between devices with their start and end apart: 3, of which 3 were waited for; matrix products, arithmetic and copies ran while one was open for 0% of the time, Pallas kernels for 0%

profile of v10, /device:TPU:1, one launch (start us, length us, event | category | flops | bytes accessed | tf_op | source)
XLA Modules:
  0.0 240.3 jit_solution(17719722438502047277)
XLA Ops:
  0.6 0.9 broadcast_in_dim.12
  1.5 28.1 %all_to_all.52 = bf16[4,8,1024]{2,1,0:T(8,128)(2,1)S(1)} all-to-all(bf16[4,8,1024]{2,1,0:T(8,128)(2,1)S(1)} %broadcast_in_dim.12), channel_id=1, replica_groups=mesh['x'=4,'yh'=2,'zh'=4,'zl'=4,'yl'=2,'c'=2] {'zh'}, dimensions={0} | all-to-all | bytes 131072 | tf_op jit(solution)/shard_map/all_to_all | solution.py:38
  29.6 17.1 %all_to_all.53 = bf16[8,4,8,1024]{3,2,1,0:T(8,128)(2,1)S(1)} all-to-all(bf16[8,4,8,1024]{3,2,1,0:T(8,128)(2,1)S(1)} %broadcast_in_dim.13), channel_id=1, replica_groups=mesh['x'=4,'yh'=2,'zh'=4,'zl'=4,'yl'=2,'c'=2] {'zl','yl'}, dimensions={0} | all-to-all | bytes 1048576 | tf_op jit(solution)/shard_map/all_to_all | solution.py:38
  46.8 0.1 broadcast_in_dim.14
  46.9 6.3 %all_to_all.54 = bf16[2,8,4,8,1024]{4,3,1,2,0:T(8,128)(2,1)S(1)} all-to-all(bf16[2,8,4,8,1024]{4,3,1,2,0:T(8,128)(2,1)S(1)} %broadcast_in_dim.14), channel_id=1, replica_groups=mesh['x'=4,'yh'=2,'zh'=4,'zl'=4,'yl'=2,'c'=2] {'c'}, dimensions={0} | all-to-all | bytes 2097152 | tf_op jit(solution)/shard_map/all_to_all | solution.py:38
  53.2 0.1 copy.31
  53.3 3.6 %convolution_bitcast_fusion = f32[8,512,192]{1,2,0:T(8,128)} fusion(bf16[512,1024,1]{1,0,2:T(8,128)(2,1)S(1)} %bitcast.50, bf16[8,192,1024]{2,1,0:T(8,128)(2,1)S(1)} %bitcast.46), kind=kOutput, calls=%fused_computation.2 | convolution fusion | flops 1610612736 | bytes 7340032 | tf_op jit(solution)/shard_map/dot_general | solution.py:99
  56.9 6.5 %all-to-all-start.3 = ((f32[8,512,192]{1,2,0:T(8,128)}), f32[8,512,192]{1,2,0:T(8,128)}, u32[]{:S(2)}, u32[]{:S(2)}) async-start(f32[8,512,192]{1,2,0:T(8,128)} %convolution_bitcast_fusion), calls=%async_computation.3 | async-start | bytes 6291456 | tf_op jit(solution)/shard_map/all_to_all | solution.py:45
  63.4 0.1 fusion.8
  63.5 45.0 %all-to-all-done.3 = f32[8,512,192]{1,2,0:T(8,128)} async-done(((f32[8,512,192]{1,2,0:T(8,128)}), f32[8,512,192]{1,2,0:T(8,128)}, u32[]{:S(2)}, u32[]{:S(2)}) %all-to-all-start.3) | async-done | bytes 3145760 | tf_op jit(solution)/shard_map/all_to_all | solution.py:45
  108.5 2.3 reduce_sum.117
  110.7 1.0 copy.32
  111.7 1.6 multiply_reduce_fusion
  113.3 0.1 multiply_reduce_fusion.1
  113.4 0.1 fusion.10
  113.6 0.1 reshape.97
  113.6 0.1 pad_maximum_fusion.1
  113.8 18.1 %all_to_all.55 = f32[64,1,24]{2,1,0:T(1,128)S(1)} all-to-all(f32[64,1,24]{2,1,0:T(1,128)S(1)} %broadcast_in_dim.15), channel_id=1, replica_groups=mesh['x'=4,'yh'=2,'zh'=4,'zl'=4,'yl'=2,'c'=2] {'zh','zl','yl','c'}, dimensions={0} | all-to-all | bytes 12288 | tf_op jit(solution)/shard_map/all_to_all | solution.py:51
  131.8 0.1 reduce_sum.120
  131.9 0.6 broadcast_in_dim.16
  132.5 4.9 %all-to-all-start.5 = ((f32[8,1,24]{2,1,0:T(1,128)}), f32[8,1,24]{2,1,0:T(1,128)S(1)}, u32[]{:S(2)}, u32[]{:S(2)}) async-start(f32[8,1,24]{2,1,0:T(1,128)} %broadcast_in_dim.16), calls=%async_computation.5 | async-start | bytes 8192 | tf_op jit(solution)/shard_map/all_to_all | solution.py:51
  137.4 0.1 reshape.101
  137.5 6.4 %all-to-all-done.5 = f32[8,1,24]{2,1,0:T(1,128)S(1)} async-done(((f32[8,1,24]{2,1,0:T(1,128)}), f32[8,1,24]{2,1,0:T(1,128)S(1)}, u32[]{:S(2)}, u32[]{:S(2)}) %all-to-all-start.5) | async-done | bytes 800 | tf_op jit(solution)/shard_map/all_to_all | solution.py:51
  143.8 0.1 add_rsqrt_fusion
  143.9 0.1 broadcast_multiply_fusion.2
  144.0 0.1 reshape.98
  144.1 0.2 exponential_reduce_fusion
  144.3 0.2 multiply_reduce_fusion.3
  144.5 0.1 multiply_multiply_fusion.5
  144.6 0.1 slice_multiply_fusion.1
  144.6 0.2 convolution_add_fusion.1
  144.8 0.3 convolution_add_fusion
  145.1 2.4 %fusion.7 = bf16[512,192]{1,0:T(8,128)(2,1)} fusion(f32[512,192]{1,0:T(8,128)} %copy.32, f32[8,192]{1,0:T(8,128)S(1)} %multiply_reduce_fusion, f32[512]{0:T(512)S(1)} %reshape.101, f32[8,192]{1,0:T(8,128)S(1)} %pad_maximum_fusion), kind=kLoop, calls=%fused_computation.13 | loop fusion | flops 1671168 | bytes 604160 | tf_op jit(solution)/shard_map/convert_element_type | solution.py:151
  147.6 1.1 copy.35
  148.6 0.1 broadcast_in_dim.17
  148.8 22.9 %all_to_all.56 = bf16[8,1,512,192]{2,3,1,0:T(8,128)(2,1)} all-to-all(bf16[8,1,512,192]{2,3,1,0:T(8,128)(2,1)S(1)} %broadcast_in_dim.17), channel_id=1, replica_groups=mesh['x'=4,'yh'=2,'zh'=4,'zl'=4,'yl'=2,'c'=2] {'x','yh'}, dimensions={0} | all-to-all | bytes 3145728 | tf_op jit(solution)/shard_map/all_to_all | solution.py:32
  171.7 4.4 %copy.36 = bf16[8,1,512,192]{3,0,2,1:T(8,128)(2,1)} copy(bf16[8,1,512,192]{2,3,1,0:T(8,128)(2,1)} %all_to_all.56) | data formatting | bytes 3145728 | tf_op jit(solution)/shard_map/all_to_all | solution.py:32
  176.1 3.5 %fusion.2 = f32[2,4,4,2,8,1024]{5,4,0,3,2,1:T(8,128)S(1)} fusion(bf16[8,192,1024,1,1,1,1]{2,1,0,6,5,4,3:T(8,128)(2,1)S(1)} %bitcast.45, bf16[4,4,2,2,8,8,192]{6,5,4,3,2,1,0:T(8,128)(2,1)} %bitcast.49), kind=kOutput, calls=%fused_computation.3 | convolution fusion | flops 1610612736 | bytes 6815744 | tf_op jit(solution)/shard_map/dot_general | solution.py:156
  179.6 0.2 copy.38
  179.8 9.6 %all_to_all.57 = f32[2,4,4,2,8,1024]{5,4,3,2,1,0:T(8,128)} all-to-all(f32[2,4,4,2,8,1024]{5,4,3,2,1,0:T(8,128)S(1)} %copy.38), channel_id=1, replica_groups=mesh['x'=4,'yh'=2,'zh'=4,'zl'=4,'yl'=2,'c'=2] {'c'}, dimensions={0} | all-to-all | bytes 4194304 | tf_op jit(solution)/shard_map/all_to_all | solution.py:163
  189.4 2.8 %reduce_sum.125 = f32[4,4,2,8,1024]{4,3,2,1,0:T(8,128)} reduce(f32[2,4,4,2,8,1024]{5,4,3,2,1,0:T(8,128)} %all_to_all.57, f32[]{:T(128)} %constant.8.clone.1), dimensions={0}, to_apply=%region_8.9 | reduce | flops 262144 | bytes 3145732 | tf_op jit(solution)/shard_map/reduce_sum | solution.py:163
  192.3 1.3 copy.39
  193.6 28.6 %all_to_all.58 = f32[8,4,8,1024]{3,2,1,0:T(8,128)} all-to-all(f32[8,4,8,1024]{3,2,1,0:T(8,128)S(1)} %copy.39), channel_id=1, replica_groups=mesh['x'=4,'yh'=2,'zh'=4,'zl'=4,'yl'=2,'c'=2] {'zl','yl'}, dimensions={0} | all-to-all | bytes 2097152 | tf_op jit(solution)/shard_map/all_to_all | solution.py:165
  222.2 1.9 reduce_sum.126
  224.1 3.3 %all-to-all-start.9 = ((f32[4,8,1024]{2,1,0:T(8,128)}), f32[4,8,1024]{2,1,0:T(8,128)S(1)}, u32[]{:S(2)}, u32[]{:S(2)}) async-start(f32[4,8,1024]{2,1,0:T(8,128)} %reduce_sum.126), calls=%async_computation.9 | async-start | bytes 262144 | tf_op jit(solution)/shard_map/all_to_all | solution.py:166
  227.5 0.6 subtract_reduce_fusion
  228.1 11.6 %all-to-all-done.9 = f32[4,8,1024]{2,1,0:T(8,128)S(1)} async-done(((f32[4,8,1024]{2,1,0:T(8,128)}), f32[4,8,1024]{2,1,0:T(8,128)S(1)}, u32[]{:S(2)}, u32[]{:S(2)}) %all-to-all-start.9) | async-done | bytes 131104 | tf_op jit(solution)/shard_map/all_to_all | solution.py:166
  239.7 0.6 reduce_sum.127
  (12 shorter events, 0.2 us)
Async XLA Ops:
  0.6 52.7 %copy-start = (bf16[1536,1024]{1,0:T(8,128)(2,1)S(1)}, bf16[1536,1024]{1,0:T(8,128)(2,1)}, u32[]{:S(2)}) copy-start(bf16[1536,1024]{1,0:T(8,128)(2,1)} %param.5) | copy-start | bytes 9437188
  56.9 6.5 %copy-start.1 = (s32[8]{0:T(128)S(1)}, s32[8]{0:T(128)}, u32[]{:S(2)}) copy-start(s32[8]{0:T(128)} %param.6) | copy-start | bytes 100
  56.9 51.6 %all-to-all-start.3 = ((f32[8,512,192]{1,2,0:T(8,128)}), f32[8,512,192]{1,2,0:T(8,128)}, u32[]{:S(2)}, u32[]{:S(2)}) async-start(f32[8,512,192]{1,2,0:T(8,128)} %convolution_bitcast_fusion), calls=%async_computation.3 | async-start | bytes 6291456 | tf_op jit(solution)/shard_map/all_to_all | solution.py:45
  63.5 80.8 %copy-start.2 = (s32[4]{0:T(128)S(1)}, s32[4]{0:T(128)}, u32[]{:S(2)}) copy-start(s32[4]{0:T(128)} %param.7) | copy-start | bytes 52
  132.5 11.3 %all-to-all-start.5 = ((f32[8,1,24]{2,1,0:T(1,128)}), f32[8,1,24]{2,1,0:T(1,128)S(1)}, u32[]{:S(2)}, u32[]{:S(2)}) async-start(f32[8,1,24]{2,1,0:T(1,128)} %broadcast_in_dim.16), calls=%async_computation.5 | async-start | bytes 8192 | tf_op jit(solution)/shard_map/all_to_all | solution.py:51
  224.1 15.5 %all-to-all-start.9 = ((f32[4,8,1024]{2,1,0:T(8,128)}), f32[4,8,1024]{2,1,0:T(8,128)S(1)}, u32[]{:S(2)}, u32[]{:S(2)}) async-start(f32[4,8,1024]{2,1,0:T(8,128)} %reduce_sum.126), calls=%async_computation.9 | async-start | bytes 262144 | tf_op jit(solution)/shard_map/all_to_all | solution.py:166

commit v11 on v10

--- a/solution.py
+++ b/solution.py
@@ -151,19 +151,20 @@
     dlogit = (dact * jax.nn.sigmoid(logits) / (1.0 + soft)).astype(jnp.bfloat16)
     dlogit = with_layout_constraint(dlogit, Layout((0, 1)))
     n_sec = _members(SEC)
-    dlogit = _all_gather_a2a(dlogit[None], SEC)
-    weight = head_weight.reshape(n_sec, columns, head_weight.shape[1])
-    partial_grad = lax.dot_general(
-        dlogit, weight, (((0, 2), (0, 1)), ((), ())), preferred_element_type=jnp.float32
+    copies = jnp.broadcast_to(dlogit.T[None], (n_sec,) + dlogit.T.shape)
+    copies = with_layout_constraint(copies, Layout((0, 1, 2)))
+    dlogit_t = lax.all_to_all(copies, SEC, 0, 0, tiled=True).reshape(-1, dlogit.shape[0])
+    grad_t = lax.dot_general(
+        head_weight, dlogit_t, (((0,), (0,)), ((), ())), preferred_element_type=jnp.float32
     )
     n_zl, n_yl, n_c = (lax.axis_size(a) for a in near)
     rows = hidden.shape[0]
-    width = partial_grad.shape[1]
-    grad = partial_grad.reshape(n_zh, n_zl, n_yl, n_c, rows, width).transpose(3, 0, 1, 2, 4, 5)
+    width = grad_t.shape[0]
+    grad = grad_t.reshape(width, n_zh, n_zl, n_yl, n_c, rows).transpose(4, 1, 2, 3, 0, 5)
     grad = jnp.sum(lax.all_to_all(grad, "c", 0, 0, tiled=True), axis=0)
-    grad = grad.transpose(1, 2, 0, 3, 4).reshape(n_zl * n_yl, n_zh, rows, width)
+    grad = grad.transpose(1, 2, 0, 3, 4).reshape(n_zl * n_yl, n_zh, width, rows)
     grad = jnp.sum(lax.all_to_all(grad, ("zl", "yl"), 0, 0, tiled=True), axis=0)
-    hidden_grad = jnp.sum(lax.all_to_all(grad, "zh", 0, 0, tiled=True), axis=0)
+    hidden_grad = jnp.sum(lax.all_to_all(grad, "zh", 0, 0, tiled=True), axis=0).T
     return (hidden_grad, loss)
 
 

time: 243 us -> 236 us (0.971)
  local copies, waits for them, and re-layouts: 10.2 us -> 5.81 us
    all_to_all x1 -> x0, local copies, waits for them, and re-layouts: 4.4 us -> none  [_all_gather_a2a(): out = lax.all_to_all(copies, axes, 0, 0, tiled=True)]
where the time goes in v11:
time: 236 us; the launch traced here: 234 us
  blocking collectives  130 us (55%)
  waiting for transfers between devices  62.9 us (27%)
  starting transfers between devices  14.7 us (6%)
  other arithmetic  13.4 us (6%)
  matrix products  6.03 us (3%)
  local copies, waits for them, and re-layouts  5.81 us (2%)
    all_to_all x3, blocking collectives, _copies_a2a(): lax.all_to_all(jnp.broadcast_to(x[None], (n,) + x.shape), axes, 0, 0, til...  51.5 us
    all_to_all x1, waiting for transfers between devices, _reduce_scatter_a2a(): return jnp.sum(lax.all_to_all(blocks, axes, 0, 0, tiled=True), axis=0)  45 us
    all_to_all x1, blocking collectives, local(): grad = jnp.sum(lax.all_to_all(grad, ('zl', 'yl'), 0, 0, tiled=True), axis=0)  28.6 us
    all_to_all x1, blocking collectives, local(): lax.all_to_all(copies, SEC, 0, 0, tiled=True).reshape(-1, dlogit.shape[0])  22.2 us
    all_to_all x1, blocking collectives, _all_reduce_a2a(): return jnp.sum(lax.all_to_all(copies, axes, 0, 0, tiled=True), axis=0)  18.1 us
    all_to_all x1, waiting for transfers between devices, local(): lax.all_to_all(grad, 'zh', 0, 0, tiled=True)  11.6 us
    all_to_all x1, blocking collectives, local(): grad = jnp.sum(lax.all_to_all(grad, 'c', 0, 0, tiled=True), axis=0)  9.63 us
    all_to_all x1, starting transfers between devices, _reduce_scatter_a2a(): return jnp.sum(lax.all_to_all(blocks, axes, 0, 0, tiled=True), axis=0)  6.48 us
  transfers between devices with their start and end apart: 3, of which 3 were waited for; matrix products, arithmetic and copies ran while one was open for 0% of the time, Pallas kernels for 0%

profile of v11, /device:TPU:1, one launch (start us, length us, event | category | flops | bytes accessed | tf_op | source)
XLA Modules:
  0.0 233.5 jit_solution(17750001766316647328)
XLA Ops:
  0.6 0.0 copy-start
  0.6 0.9 broadcast_in_dim.12
  1.5 28.1 %all_to_all.52 = bf16[4,8,1024]{2,1,0:T(8,128)(2,1)S(1)} all-to-all(bf16[4,8,1024]{2,1,0:T(8,128)(2,1)S(1)} %broadcast_in_dim.12), channel_id=1, replica_groups=mesh['x'=4,'yh'=2,'zh'=4,'zl'=4,'yl'=2,'c'=2] {'zh'}, dimensions={0} | all-to-all | bytes 131072 | tf_op jit(solution)/shard_map/all_to_all | solution.py:38
  29.6 17.1 %all_to_all.53 = bf16[8,4,8,1024]{3,2,1,0:T(8,128)(2,1)S(1)} all-to-all(bf16[8,4,8,1024]{3,2,1,0:T(8,128)(2,1)S(1)} %broadcast_in_dim.13), channel_id=1, replica_groups=mesh['x'=4,'yh'=2,'zh'=4,'zl'=4,'yl'=2,'c'=2] {'zl','yl'}, dimensions={0} | all-to-all | bytes 1048576 | tf_op jit(solution)/shard_map/all_to_all | solution.py:38
  46.8 0.1 broadcast_in_dim.14
  46.9 6.3 %all_to_all.54 = bf16[2,8,4,8,1024]{4,3,1,2,0:T(8,128)(2,1)S(1)} all-to-all(bf16[2,8,4,8,1024]{4,3,1,2,0:T(8,128)(2,1)S(1)} %broadcast_in_dim.14), channel_id=1, replica_groups=mesh['x'=4,'yh'=2,'zh'=4,'zl'=4,'yl'=2,'c'=2] {'c'}, dimensions={0} | all-to-all | bytes 2097152 | tf_op jit(solution)/shard_map/all_to_all | solution.py:38
  53.2 0.1 copy.22
  53.3 3.6 %convolution_bitcast_fusion = f32[8,512,192]{1,2,0:T(8,128)} fusion(bf16[512,1024,1]{1,0,2:T(8,128)(2,1)S(1)} %bitcast.47, bf16[8,192,1024]{2,1,0:T(8,128)(2,1)S(1)} %bitcast.41), kind=kOutput, calls=%fused_computation.1 | convolution fusion | flops 1610612736 | bytes 7340032 | tf_op jit(solution)/shard_map/dot_general | solution.py:99
  56.9 6.5 %all-to-all-start.3 = ((f32[8,512,192]{1,2,0:T(8,128)}), f32[8,512,192]{1,2,0:T(8,128)}, u32[]{:S(2)}, u32[]{:S(2)}) async-start(f32[8,512,192]{1,2,0:T(8,128)} %convolution_bitcast_fusion), calls=%async_computation.3 | async-start | bytes 6291456 | tf_op jit(solution)/shard_map/all_to_all | solution.py:45
  63.4 0.1 fusion.3
  63.5 45.0 %all-to-all-done.3 = f32[8,512,192]{1,2,0:T(8,128)} async-done(((f32[8,512,192]{1,2,0:T(8,128)}), f32[8,512,192]{1,2,0:T(8,128)}, u32[]{:S(2)}, u32[]{:S(2)}) %all-to-all-start.3) | async-done | bytes 3145760 | tf_op jit(solution)/shard_map/all_to_all | solution.py:45
  108.5 2.3 reduce_sum.117
  110.7 1.0 copy.23
  111.7 1.6 multiply_reduce_fusion
  113.3 0.1 multiply_reduce_fusion.1
  113.4 0.1 fusion.5
  113.6 0.1 reshape.95
  113.6 0.1 pad_maximum_fusion.1
  113.8 18.1 %all_to_all.55 = f32[64,1,24]{2,1,0:T(1,128)S(1)} all-to-all(f32[64,1,24]{2,1,0:T(1,128)S(1)} %broadcast_in_dim.15), channel_id=1, replica_groups=mesh['x'=4,'yh'=2,'zh'=4,'zl'=4,'yl'=2,'c'=2] {'zh','zl','yl','c'}, dimensions={0} | all-to-all | bytes 12288 | tf_op jit(solution)/shard_map/all_to_all | solution.py:51
  131.8 0.1 reduce_sum.120
  131.9 0.6 broadcast_in_dim.16
  132.5 4.9 %all-to-all-start.5 = ((f32[8,1,24]{2,1,0:T(1,128)}), f32[8,1,24]{2,1,0:T(1,128)S(1)}, u32[]{:S(2)}, u32[]{:S(2)}) async-start(f32[8,1,24]{2,1,0:T(1,128)} %broadcast_in_dim.16), calls=%async_computation.5 | async-start | bytes 8192 | tf_op jit(solution)/shard_map/all_to_all | solution.py:51
  137.4 0.1 reshape.100
  137.5 6.4 %all-to-all-done.5 = f32[8,1,24]{2,1,0:T(1,128)S(1)} async-done(((f32[8,1,24]{2,1,0:T(1,128)}), f32[8,1,24]{2,1,0:T(1,128)S(1)}, u32[]{:S(2)}, u32[]{:S(2)}) %all-to-all-start.5) | async-done | bytes 800 | tf_op jit(solution)/shard_map/all_to_all | solution.py:51
  143.8 0.1 add_rsqrt_fusion
  143.9 0.1 broadcast_multiply_fusion.2
  144.0 0.1 reshape.96
  144.1 0.2 exponential_reduce_fusion
  144.3 0.2 multiply_reduce_fusion.3
  144.5 0.1 multiply_multiply_fusion.5
  144.6 0.1 slice_multiply_fusion.1
  144.6 0.2 convolution_add_fusion.1
  144.8 0.3 convolution_add_fusion
  145.1 2.4 %fusion.2 = bf16[512,192]{1,0:T(8,128)(2,1)} fusion(f32[512,192]{1,0:T(8,128)} %copy.23, f32[8,192]{1,0:T(8,128)S(1)} %multiply_reduce_fusion, f32[512]{0:T(512)S(1)} %reshape.100, f32[8,192]{1,0:T(8,128)S(1)} %pad_maximum_fusion), kind=kLoop, calls=%fused_computation.11 | loop fusion | flops 1671168 | bytes 604160 | tf_op jit(solution)/shard_map/convert_element_type | solution.py:151
  147.6 1.1 copy.26
  148.6 0.1 broadcast_in_dim.17
  148.8 22.2 %all_to_all.56 = bf16[8,192,512]{2,1,0:T(8,128)(2,1)S(1)} all-to-all(bf16[8,192,512]{2,1,0:T(8,128)(2,1)S(1)} %broadcast_in_dim.17), channel_id=1, replica_groups=mesh['x'=4,'yh'=2,'zh'=4,'zl'=4,'yl'=2,'c'=2] {'x','yh'}, dimensions={0} | all-to-all | bytes 3145728 | tf_op jit(solution)/shard_map/all_to_all | solution.py:156
  171.0 1.8 fusion.17
  172.8 0.2 copy.33
  173.0 9.6 %all_to_all.57 = f32[2,4,4,2,1024,8]{4,5,3,2,1,0:T(8,128)} all-to-all(f32[2,4,4,2,1024,8]{4,5,3,2,1,0:T(8,128)S(1)} %bitcast.42), channel_id=1, replica_groups=mesh['x'=4,'yh'=2,'zh'=4,'zl'=4,'yl'=2,'c'=2] {'c'}, dimensions={0} | all-to-all | bytes 4194304 | tf_op jit(solution)/shard_map/all_to_all | solution.py:164
  182.7 2.8 %reduce_sum.125 = f32[4,4,2,1024,8]{3,4,2,1,0:T(8,128)} reduce(f32[2,4,4,2,1024,8]{4,5,3,2,1,0:T(8,128)} %all_to_all.57, f32[]{:T(128)} %constant.8.clone.1), dimensions={0}, to_apply=%region_8.9 | reduce | flops 262144 | bytes 3145732 | tf_op jit(solution)/shard_map/reduce_sum | solution.py:164
  185.5 1.3 copy.29
  186.8 28.6 %all_to_all.58 = f32[8,4,1024,8]{2,3,1,0:T(8,128)} all-to-all(f32[8,4,1024,8]{2,3,1,0:T(8,128)S(1)} %copy.29), channel_id=1, replica_groups=mesh['x'=4,'yh'=2,'zh'=4,'zl'=4,'yl'=2,'c'=2] {'zl','yl'}, dimensions={0} | all-to-all | bytes 2097152 | tf_op jit(solution)/shard_map/all_to_all | solution.py:166
  215.4 1.9 reduce_sum.126
  217.3 3.3 %all-to-all-start.9 = ((f32[4,1024,8]{1,2,0:T(8,128)}), f32[4,1024,8]{1,2,0:T(8,128)S(1)}, u32[]{:S(2)}, u32[]{:S(2)}) async-start(f32[4,1024,8]{1,2,0:T(8,128)} %reduce_sum.126), calls=%async_computation.9 | async-start | bytes 262144 | tf_op jit(solution)/shard_map/all_to_all | solution.py:167
  220.7 0.6 subtract_reduce_fusion
  221.3 11.6 %all-to-all-done.9 = f32[4,1024,8]{1,2,0:T(8,128)S(1)} async-done(((f32[4,1024,8]{1,2,0:T(8,128)}), f32[4,1024,8]{1,2,0:T(8,128)S(1)}, u32[]{:S(2)}, u32[]{:S(2)}) %all-to-all-start.9) | async-done | bytes 131104 | tf_op jit(solution)/shard_map/all_to_all | solution.py:167
  232.9 0.6 reduce_sum.127
  (11 shorter events, 0.2 us)
Async XLA Ops:
  0.6 52.7 %copy-start = (bf16[1536,1024]{1,0:T(8,128)(2,1)S(1)}, bf16[1536,1024]{1,0:T(8,128)(2,1)}, u32[]{:S(2)}) copy-start(bf16[1536,1024]{1,0:T(8,128)(2,1)} %param.5) | copy-start | bytes 9437188
  56.9 6.5 %copy-start.1 = (s32[8]{0:T(128)S(1)}, s32[8]{0:T(128)}, u32[]{:S(2)}) copy-start(s32[8]{0:T(128)} %param.6) | copy-start | bytes 100
  56.9 51.6 %all-to-all-start.3 = ((f32[8,512,192]{1,2,0:T(8,128)}), f32[8,512,192]{1,2,0:T(8,128)}, u32[]{:S(2)}, u32[]{:S(2)}) async-start(f32[8,512,192]{1,2,0:T(8,128)} %convolution_bitcast_fusion), calls=%async_computation.3 | async-start | bytes 6291456 | tf_op jit(solution)/shard_map/all_to_all | solution.py:45
  63.4 80.9 %copy-start.2 = (s32[4]{0:T(128)S(1)}, s32[4]{0:T(128)}, u32[]{:S(2)}) copy-start(s32[4]{0:T(128)} %param.7) | copy-start | bytes 52
  132.5 11.3 %all-to-all-start.5 = ((f32[8,1,24]{2,1,0:T(1,128)}), f32[8,1,24]{2,1,0:T(1,128)S(1)}, u32[]{:S(2)}, u32[]{:S(2)}) async-start(f32[8,1,24]{2,1,0:T(1,128)} %broadcast_in_dim.16), calls=%async_computation.5 | async-start | bytes 8192 | tf_op jit(solution)/shard_map/all_to_all | solution.py:51
  217.3 15.5 %all-to-all-start.9 = ((f32[4,1024,8]{1,2,0:T(8,128)}), f32[4,1024,8]{1,2,0:T(8,128)S(1)}, u32[]{:S(2)}, u32[]{:S(2)}) async-start(f32[4,1024,8]{1,2,0:T(8,128)} %reduce_sum.126), calls=%async_computation.9 | async-start | bytes 262144 | tf_op jit(solution)/shard_map/all_to_all | solution.py:167

commit v12 on v11

--- a/solution.py
+++ b/solution.py
@@ -162,8 +162,10 @@
     width = grad_t.shape[0]
     grad = grad_t.reshape(width, n_zh, n_zl, n_yl, n_c, rows).transpose(4, 1, 2, 3, 0, 5)
     grad = jnp.sum(lax.all_to_all(grad, "c", 0, 0, tiled=True), axis=0)
-    grad = grad.transpose(1, 2, 0, 3, 4).reshape(n_zl * n_yl, n_zh, width, rows)
-    grad = jnp.sum(lax.all_to_all(grad, ("zl", "yl"), 0, 0, tiled=True), axis=0)
+    grad = grad.transpose(2, 0, 1, 3, 4)
+    grad = jnp.sum(lax.all_to_all(grad, "yl", 0, 0, tiled=True), axis=0)
+    grad = grad.transpose(1, 0, 2, 3)
+    grad = jnp.sum(lax.all_to_all(grad, "zl", 0, 0, tiled=True), axis=0)
     hidden_grad = jnp.sum(lax.all_to_all(grad, "zh", 0, 0, tiled=True), axis=0).T
     return (hidden_grad, loss)
 

time: 236 us -> 244 us (1.034)
  blocking collectives: 130 us -> 135 us
    all_to_all x1 -> x2, blocking collectives: 28.6 us -> 33.2 us  [the longest x1 16.6 us: local(): grad = jnp.sum(lax.all_to_all(grad, 'zl', 0, 0, tiled=True), axis=0)]
where the time goes in v12:
time: 244 us; the launch traced here: 241 us
  blocking collectives  135 us (55%)
  waiting for transfers between devices  62.8 us (26%)
  other arithmetic  15.3 us (6%)
  starting transfers between devices  14.7 us (6%)
  local copies, waits for them, and re-layouts  6.89 us (3%)
  matrix products  6.03 us (2%)
    all_to_all x3, blocking collectives, _copies_a2a(): lax.all_to_all(jnp.broadcast_to(x[None], (n,) + x.shape), axes, 0, 0, til...  51.5 us
    all_to_all x1, waiting for transfers between devices, _reduce_scatter_a2a(): return jnp.sum(lax.all_to_all(blocks, axes, 0, 0, tiled=True), axis=0)  45 us
    all_to_all x1, blocking collectives, local(): lax.all_to_all(copies, SEC, 0, 0, tiled=True).reshape(-1, dlogit.shape[0])  22.2 us
    all_to_all x1, blocking collectives, _all_reduce_a2a(): return jnp.sum(lax.all_to_all(copies, axes, 0, 0, tiled=True), axis=0)  18.1 us
    all_to_all x1, blocking collectives, local(): grad = jnp.sum(lax.all_to_all(grad, 'zl', 0, 0, tiled=True), axis=0)  16.6 us
    all_to_all x1, blocking collectives, local(): grad = jnp.sum(lax.all_to_all(grad, 'yl', 0, 0, tiled=True), axis=0)  16.6 us
    all_to_all x1, waiting for transfers between devices, local(): lax.all_to_all(grad, 'zh', 0, 0, tiled=True)  11.5 us
    all_to_all x1, blocking collectives, local(): grad = jnp.sum(lax.all_to_all(grad, 'c', 0, 0, tiled=True), axis=0)  9.63 us
  transfers between devices with their start and end apart: 3, of which 3 were waited for; matrix products, arithmetic and copies ran while one was open for 0% of the time, Pallas kernels for 0%

profile of v12, /device:TPU:1, one launch (start us, length us, event | category | flops | bytes accessed | tf_op | source)
XLA Modules:
  0.0 241.0 jit_solution(18324243454912534220)
XLA Ops:
  0.6 0.9 broadcast_in_dim.12
  1.5 28.1 %all_to_all.57 = bf16[4,8,1024]{2,1,0:T(8,128)(2,1)S(1)} all-to-all(bf16[4,8,1024]{2,1,0:T(8,128)(2,1)S(1)} %broadcast_in_dim.12), channel_id=1, replica_groups=mesh['x'=4,'yh'=2,'zh'=4,'zl'=4,'yl'=2,'c'=2] {'zh'}, dimensions={0} | all-to-all | bytes 131072 | tf_op jit(solution)/shard_map/all_to_all | solution.py:38
  29.6 17.1 %all_to_all.58 = bf16[8,4,8,1024]{3,2,1,0:T(8,128)(2,1)S(1)} all-to-all(bf16[8,4,8,1024]{3,2,1,0:T(8,128)(2,1)S(1)} %broadcast_in_dim.13), channel_id=1, replica_groups=mesh['x'=4,'yh'=2,'zh'=4,'zl'=4,'yl'=2,'c'=2] {'zl','yl'}, dimensions={0} | all-to-all | bytes 1048576 | tf_op jit(solution)/shard_map/all_to_all | solution.py:38
  46.8 0.1 broadcast_in_dim.14
  46.9 6.3 %all_to_all.59 = bf16[2,8,4,8,1024]{4,3,1,2,0:T(8,128)(2,1)S(1)} all-to-all(bf16[2,8,4,8,1024]{4,3,1,2,0:T(8,128)(2,1)S(1)} %broadcast_in_dim.14), channel_id=1, replica_groups=mesh['x'=4,'yh'=2,'zh'=4,'zl'=4,'yl'=2,'c'=2] {'c'}, dimensions={0} | all-to-all | bytes 2097152 | tf_op jit(solution)/shard_map/all_to_all | solution.py:38
  53.2 0.1 copy.31
  53.3 3.6 %convolution_bitcast_fusion = f32[8,512,192]{1,2,0:T(8,128)} fusion(bf16[512,1024,1]{1,0,2:T(8,128)(2,1)S(1)} %bitcast.47, bf16[8,192,1024]{2,1,0:T(8,128)(2,1)S(1)} %bitcast.40), kind=kOutput, calls=%fused_computation.1 | convolution fusion | flops 1610612736 | bytes 7340032 | tf_op jit(solution)/shard_map/dot_general | solution.py:99
  56.9 6.5 %all-to-all-start.3 = ((f32[8,512,192]{1,2,0:T(8,128)}), f32[8,512,192]{1,2,0:T(8,128)}, u32[]{:S(2)}, u32[]{:S(2)}) async-start(f32[8,512,192]{1,2,0:T(8,128)} %convolution_bitcast_fusion), calls=%async_computation.3 | async-start | bytes 6291456 | tf_op jit(solution)/shard_map/all_to_all | solution.py:45
  63.5 45.0 %all-to-all-done.3 = f32[8,512,192]{1,2,0:T(8,128)} async-done(((f32[8,512,192]{1,2,0:T(8,128)}), f32[8,512,192]{1,2,0:T(8,128)}, u32[]{:S(2)}, u32[]{:S(2)}) %all-to-all-start.3) | async-done | bytes 3145760 | tf_op jit(solution)/shard_map/all_to_all | solution.py:45
  108.5 2.3 reduce_sum.126
  110.7 1.0 copy.32
  111.7 1.6 multiply_reduce_fusion
  113.3 0.1 multiply_reduce_fusion.1
  113.4 0.1 fusion.5
  113.6 0.1 reshape.92
  113.6 0.1 pad_maximum_fusion.1
  113.8 18.1 %all_to_all.60 = f32[64,1,24]{2,1,0:T(1,128)S(1)} all-to-all(f32[64,1,24]{2,1,0:T(1,128)S(1)} %broadcast_in_dim.15), channel_id=1, replica_groups=mesh['x'=4,'yh'=2,'zh'=4,'zl'=4,'yl'=2,'c'=2] {'zh','zl','yl','c'}, dimensions={0} | all-to-all | bytes 12288 | tf_op jit(solution)/shard_map/all_to_all | solution.py:51
  131.8 0.1 reduce_sum.129
  131.9 0.6 broadcast_in_dim.16
  132.5 4.9 %all-to-all-start.5 = ((f32[8,1,24]{2,1,0:T(1,128)}), f32[8,1,24]{2,1,0:T(1,128)S(1)}, u32[]{:S(2)}, u32[]{:S(2)}) async-start(f32[8,1,24]{2,1,0:T(1,128)} %broadcast_in_dim.16), calls=%async_computation.5 | async-start | bytes 8192 | tf_op jit(solution)/shard_map/all_to_all | solution.py:51
  137.4 0.1 reshape.96
  137.5 6.4 %all-to-all-done.5 = f32[8,1,24]{2,1,0:T(1,128)S(1)} async-done(((f32[8,1,24]{2,1,0:T(1,128)}), f32[8,1,24]{2,1,0:T(1,128)S(1)}, u32[]{:S(2)}, u32[]{:S(2)}) %all-to-all-start.5) | async-done | bytes 800 | tf_op jit(solution)/shard_map/all_to_all | solution.py:51
  143.8 0.1 add_rsqrt_fusion
  144.0 0.1 reshape.93
  144.1 0.2 exponential_reduce_fusion
  144.3 0.2 multiply_reduce_fusion.3
  144.5 0.1 multiply_multiply_fusion.5
  144.6 0.1 slice_multiply_fusion.1
  144.6 0.2 convolution_add_fusion.1
  144.8 0.3 convolution_add_fusion
  145.1 2.4 %fusion.2 = bf16[512,192]{1,0:T(8,128)(2,1)} fusion(f32[512,192]{1,0:T(8,128)} %copy.32, f32[8,192]{1,0:T(8,128)S(1)} %multiply_reduce_fusion, f32[512]{0:T(512)S(1)} %reshape.96, f32[8,192]{1,0:T(8,128)S(1)} %pad_maximum_fusion), kind=kLoop, calls=%fused_computation.11 | loop fusion | flops 1671168 | bytes 604160 | tf_op jit(solution)/shard_map/convert_element_type | solution.py:151
  147.6 1.1 copy.35
  148.6 0.1 broadcast_in_dim.17
  148.8 22.2 %all_to_all.61 = bf16[8,192,512]{2,1,0:T(8,128)(2,1)S(1)} all-to-all(bf16[8,192,512]{2,1,0:T(8,128)(2,1)S(1)} %broadcast_in_dim.17), channel_id=1, replica_groups=mesh['x'=4,'yh'=2,'zh'=4,'zl'=4,'yl'=2,'c'=2] {'x','yh'}, dimensions={0} | all-to-all | bytes 3145728 | tf_op jit(solution)/shard_map/all_to_all | solution.py:156
  171.0 1.8 fusion.17
  172.8 0.2 copy.43
  173.0 9.6 %all_to_all.62 = f32[2,4,4,2,1024,8]{4,5,3,2,1,0:T(8,128)} all-to-all(f32[2,4,4,2,1024,8]{4,5,3,2,1,0:T(8,128)S(1)} %bitcast.41), channel_id=1, replica_groups=mesh['x'=4,'yh'=2,'zh'=4,'zl'=4,'yl'=2,'c'=2] {'c'}, dimensions={0} | all-to-all | bytes 4194304 | tf_op jit(solution)/shard_map/all_to_all | solution.py:164
  182.7 2.8 %reduce_sum.134 = f32[4,4,2,1024,8]{3,4,2,1,0:T(8,128)} reduce(f32[2,4,4,2,1024,8]{4,5,3,2,1,0:T(8,128)} %all_to_all.62, f32[]{:T(128)} %constant.8.clone.1), dimensions={0}, to_apply=%region_8.9 | reduce | flops 262144 | bytes 3145732 | tf_op jit(solution)/shard_map/reduce_sum | solution.py:164
  185.5 1.3 copy.38
  186.8 16.6 %all_to_all.63 = f32[2,4,4,1024,8]{3,4,2,1,0:T(8,128)} all-to-all(f32[2,4,4,1024,8]{3,4,2,1,0:T(8,128)S(1)} %copy.38), channel_id=1, replica_groups=mesh['x'=4,'yh'=2,'zh'=4,'zl'=4,'yl'=2,'c'=2] {'yl'}, dimensions={0} | all-to-all | bytes 2097152 | tf_op jit(solution)/shard_map/all_to_all | solution.py:166
  203.4 2.2 reduce_sum.135
  205.6 1.1 copy.39
  206.6 16.6 %all_to_all.64 = f32[4,4,1024,8]{2,3,1,0:T(8,128)} all-to-all(f32[4,4,1024,8]{2,3,1,0:T(8,128)S(1)} %copy.39), channel_id=1, replica_groups=mesh['x'=4,'yh'=2,'zh'=4,'zl'=4,'yl'=2,'c'=2] {'zl'}, dimensions={0} | all-to-all | bytes 1048576 | tf_op jit(solution)/shard_map/all_to_all | solution.py:168
  223.3 1.7 reduce_sum.136
  225.0 3.3 %all-to-all-start.10 = ((f32[4,1024,8]{1,2,0:T(8,128)}), f32[4,1024,8]{1,2,0:T(8,128)S(1)}, u32[]{:S(2)}, u32[]{:S(2)}) async-start(f32[4,1024,8]{1,2,0:T(8,128)} %reduce_sum.136), calls=%async_computation.10 | async-start | bytes 262144 | tf_op jit(solution)/shard_map/all_to_all | solution.py:169
  228.3 0.6 subtract_reduce_fusion
  228.9 11.5 %all-to-all-done.10 = f32[4,1024,8]{1,2,0:T(8,128)S(1)} async-done(((f32[4,1024,8]{1,2,0:T(8,128)}), f32[4,1024,8]{1,2,0:T(8,128)S(1)}, u32[]{:S(2)}, u32[]{:S(2)}) %all-to-all-start.10) | async-done | bytes 131104 | tf_op jit(solution)/shard_map/all_to_all | solution.py:169
  240.4 0.6 reduce_sum.137
  (14 shorter events, 0.3 us)
Async XLA Ops:
  0.6 52.7 %copy-start = (bf16[1536,1024]{1,0:T(8,128)(2,1)S(1)}, bf16[1536,1024]{1,0:T(8,128)(2,1)}, u32[]{:S(2)}) copy-start(bf16[1536,1024]{1,0:T(8,128)(2,1)} %param.5) | copy-start | bytes 9437188
  56.9 6.5 %copy-start.1 = (s32[8]{0:T(128)S(1)}, s32[8]{0:T(128)}, u32[]{:S(2)}) copy-start(s32[8]{0:T(128)} %param.6) | copy-start | bytes 100
  56.9 51.6 %all-to-all-start.3 = ((f32[8,512,192]{1,2,0:T(8,128)}), f32[8,512,192]{1,2,0:T(8,128)}, u32[]{:S(2)}, u32[]{:S(2)}) async-start(f32[8,512,192]{1,2,0:T(8,128)} %convolution_bitcast_fusion), calls=%async_computation.3 | async-start | bytes 6291456 | tf_op jit(solution)/shard_map/all_to_all | solution.py:45
  63.4 80.9 %copy-start.2 = (s32[4]{0:T(128)S(1)}, s32[4]{0:T(128)}, u32[]{:S(2)}) copy-start(s32[4]{0:T(128)} %param.7) | copy-start | bytes 52
  132.5 11.3 %all-to-all-start.5 = ((f32[8,1,24]{2,1,0:T(1,128)}), f32[8,1,24]{2,1,0:T(1,128)S(1)}, u32[]{:S(2)}, u32[]{:S(2)}) async-start(f32[8,1,24]{2,1,0:T(1,128)} %broadcast_in_dim.16), calls=%async_computation.5 | async-start | bytes 8192 | tf_op jit(solution)/shard_map/all_to_all | solution.py:51
  225.0 15.4 %all-to-all-start.10 = ((f32[4,1024,8]{1,2,0:T(8,128)}), f32[4,1024,8]{1,2,0:T(8,128)S(1)}, u32[]{:S(2)}, u32[]{:S(2)}) async-start(f32[4,1024,8]{1,2,0:T(8,128)} %reduce_sum.136), calls=%async_computation.10 | async-start | bytes 262144 | tf_op jit(solution)/shard_map/all_to_all | solution.py:169

commit v13 on v11

--- a/solution.py
+++ b/solution.py
@@ -119,7 +119,7 @@
     )
     norms_part = jnp.sum(pooled * pooled, axis=1)
     stats = jnp.concatenate([dots_part.reshape(-1), norms_part])
-    for axes in (VOC, SEC):
+    for axes in (SEC, VOC):
         stats = _all_reduce_a2a(stats, axes)
     dots = stats[: half * half].reshape(half, half)
     norms = stats[half * half :]

time: 236 us -> 238 us (level)
  blocking collectives: 130 us -> 122 us
  waiting for transfers between devices: 62.9 us -> 69.7 us
    all_to_all x1, blocking collectives: 18.1 us -> 10.5 us  [_all_reduce_a2a(): return jnp.sum(lax.all_to_all(copies, axes, 0, 0, tiled=True), axis=0)]
    all_to_all x1, waiting for transfers between devices: 6.35 us -> 13.2 us  [_all_reduce_a2a(): return jnp.sum(lax.all_to_all(copies, axes, 0, 0, tiled=True), axis=0)]
where the time goes in v13:
time: 238 us; the launch traced here: 235 us
  blocking collectives  122 us (51%)
  waiting for transfers between devices  69.7 us (29%)
  starting transfers between devices  16.7 us (7%)
  other arithmetic  13.4 us (6%)
  matrix products  6.03 us (3%)
  local copies, waits for them, and re-layouts  5.83 us (2%)
    all_to_all x3, blocking collectives, _copies_a2a(): lax.all_to_all(jnp.broadcast_to(x[None], (n,) + x.shape), axes, 0, 0, til...  51.5 us
    all_to_all x1, waiting for transfers between devices, _reduce_scatter_a2a(): return jnp.sum(lax.all_to_all(blocks, axes, 0, 0, tiled=True), axis=0)  45 us
    all_to_all x1, blocking collectives, local(): grad = jnp.sum(lax.all_to_all(grad, ('zl', 'yl'), 0, 0, tiled=True), axis=0)  28.6 us
    all_to_all x1, blocking collectives, local(): lax.all_to_all(copies, SEC, 0, 0, tiled=True).reshape(-1, dlogit.shape[0])  23.7 us
    all_to_all x1, waiting for transfers between devices, _all_reduce_a2a(): return jnp.sum(lax.all_to_all(copies, axes, 0, 0, tiled=True), axis=0)  13.2 us
    all_to_all x1, waiting for transfers between devices, local(): lax.all_to_all(grad, 'zh', 0, 0, tiled=True)  11.6 us
    all_to_all x1, blocking collectives, _all_reduce_a2a(): return jnp.sum(lax.all_to_all(copies, axes, 0, 0, tiled=True), axis=0)  10.5 us
    all_to_all x1, blocking collectives, local(): grad = jnp.sum(lax.all_to_all(grad, 'c', 0, 0, tiled=True), axis=0)  8.13 us
  transfers between devices with their start and end apart: 3, of which 3 were waited for; matrix products, arithmetic and copies ran while one was open for 0% of the time, Pallas kernels for 0%

profile of v13, /device:TPU:1, one launch (start us, length us, event | category | flops | bytes accessed | tf_op | source)
XLA Modules:
  0.0 234.8 jit_solution(3762942423811020160)
XLA Ops:
  0.6 0.0 copy-start
  0.6 0.9 broadcast_in_dim.12
  1.5 28.1 %all_to_all.52 = bf16[4,8,1024]{2,1,0:T(8,128)(2,1)S(1)} all-to-all(bf16[4,8,1024]{2,1,0:T(8,128)(2,1)S(1)} %broadcast_in_dim.12), channel_id=1, replica_groups=mesh['x'=4,'yh'=2,'zh'=4,'zl'=4,'yl'=2,'c'=2] {'zh'}, dimensions={0} | all-to-all | bytes 131072 | tf_op jit(solution)/shard_map/all_to_all | solution.py:38
  29.6 17.1 %all_to_all.53 = bf16[8,4,8,1024]{3,2,1,0:T(8,128)(2,1)S(1)} all-to-all(bf16[8,4,8,1024]{3,2,1,0:T(8,128)(2,1)S(1)} %broadcast_in_dim.13), channel_id=1, replica_groups=mesh['x'=4,'yh'=2,'zh'=4,'zl'=4,'yl'=2,'c'=2] {'zl','yl'}, dimensions={0} | all-to-all | bytes 1048576 | tf_op jit(solution)/shard_map/all_to_all | solution.py:38
  46.8 0.1 broadcast_in_dim.14
  46.9 6.3 %all_to_all.54 = bf16[2,8,4,8,1024]{4,3,1,2,0:T(8,128)(2,1)S(1)} all-to-all(bf16[2,8,4,8,1024]{4,3,1,2,0:T(8,128)(2,1)S(1)} %broadcast_in_dim.14), channel_id=1, replica_groups=mesh['x'=4,'yh'=2,'zh'=4,'zl'=4,'yl'=2,'c'=2] {'c'}, dimensions={0} | all-to-all | bytes 2097152 | tf_op jit(solution)/shard_map/all_to_all | solution.py:38
  53.2 0.1 copy.22
  53.3 3.6 %convolution_bitcast_fusion = f32[8,512,192]{1,2,0:T(8,128)} fusion(bf16[512,1024,1]{1,0,2:T(8,128)(2,1)S(1)} %bitcast.47, bf16[8,192,1024]{2,1,0:T(8,128)(2,1)S(1)} %bitcast.41), kind=kOutput, calls=%fused_computation.1 | convolution fusion | flops 1610612736 | bytes 7340032 | tf_op jit(solution)/shard_map/dot_general | solution.py:99
  56.9 6.5 %all-to-all-start.3 = ((f32[8,512,192]{1,2,0:T(8,128)}), f32[8,512,192]{1,2,0:T(8,128)}, u32[]{:S(2)}, u32[]{:S(2)}) async-start(f32[8,512,192]{1,2,0:T(8,128)} %convolution_bitcast_fusion), calls=%async_computation.3 | async-start | bytes 6291456 | tf_op jit(solution)/shard_map/all_to_all | solution.py:45
  63.4 0.1 fusion.3
  63.5 45.0 %all-to-all-done.3 = f32[8,512,192]{1,2,0:T(8,128)} async-done(((f32[8,512,192]{1,2,0:T(8,128)}), f32[8,512,192]{1,2,0:T(8,128)}, u32[]{:S(2)}, u32[]{:S(2)}) %all-to-all-start.3) | async-done | bytes 3145760 | tf_op jit(solution)/shard_map/all_to_all | solution.py:45
  108.5 2.3 reduce_sum.117
  110.7 1.0 copy.23
  111.7 1.6 multiply_reduce_fusion
  113.3 0.1 multiply_reduce_fusion.1
  113.4 0.1 fusion.5
  113.6 0.1 reshape.95
  113.6 0.1 pad_maximum_fusion.1
  113.7 10.5 %all_to_all.55 = f32[8,1,24]{2,1,0:T(1,128)S(1)} all-to-all(f32[8,1,24]{2,1,0:T(1,128)S(1)} %broadcast_in_dim.15), channel_id=1, replica_groups=mesh['x'=4,'yh'=2,'zh'=4,'zl'=4,'yl'=2,'c'=2] {'x','yh'}, dimensions={0} | all-to-all | bytes 1536 | tf_op jit(solution)/shard_map/all_to_all | solution.py:51
  124.3 0.6 broadcast_in_dim.16
  124.9 6.9 %all-to-all-start.5 = ((f32[64,1,24]{2,1,0:T(1,128)}), f32[64,1,24]{2,1,0:T(1,128)S(1)}, u32[]{:S(2)}, u32[]{:S(2)}) async-start(f32[64,1,24]{2,1,0:T(1,128)} %broadcast_in_dim.16), calls=%async_computation.5 | async-start | bytes 65536 | tf_op jit(solution)/shard_map/all_to_all | solution.py:51
  131.9 0.1 reshape.100
  131.9 13.2 %all-to-all-done.5 = f32[64,1,24]{2,1,0:T(1,128)S(1)} async-done(((f32[64,1,24]{2,1,0:T(1,128)}), f32[64,1,24]{2,1,0:T(1,128)S(1)}, u32[]{:S(2)}, u32[]{:S(2)}) %all-to-all-start.5) | async-done | bytes 6176 | tf_op jit(solution)/shard_map/all_to_all | solution.py:51
  145.1 0.1 reduce_sum.121
  145.2 0.1 add_rsqrt_fusion
  145.3 0.1 broadcast_multiply_fusion.2
  145.3 0.1 reshape.96
  145.4 0.2 exponential_reduce_fusion
  145.6 0.2 multiply_reduce_fusion.3
  145.8 0.1 multiply_multiply_fusion.5
  145.9 0.1 slice_multiply_fusion.1
  146.0 0.2 convolution_add_fusion.1
  146.2 0.3 convolution_add_fusion
  146.5 2.4 %fusion.2 = bf16[512,192]{1,0:T(8,128)(2,1)} fusion(f32[512,192]{1,0:T(8,128)} %copy.23, f32[8,192]{1,0:T(8,128)S(1)} %multiply_reduce_fusion, f32[512]{0:T(512)S(1)} %reshape.100, f32[8,192]{1,0:T(8,128)S(1)} %pad_maximum_fusion), kind=kLoop, calls=%fused_computation.11 | loop fusion | flops 1671168 | bytes 604160 | tf_op jit(solution)/shard_map/convert_element_type | solution.py:151
  148.9 1.1 copy.26
  150.0 0.1 broadcast_in_dim.17
  150.1 23.7 %all_to_all.56 = bf16[8,192,512]{2,1,0:T(8,128)(2,1)S(1)} all-to-all(bf16[8,192,512]{2,1,0:T(8,128)(2,1)S(1)} %broadcast_in_dim.17), channel_id=1, replica_groups=mesh['x'=4,'yh'=2,'zh'=4,'zl'=4,'yl'=2,'c'=2] {'x','yh'}, dimensions={0} | all-to-all | bytes 3145728 | tf_op jit(solution)/shard_map/all_to_all | solution.py:156
  173.8 1.8 fusion.17
  175.6 0.2 copy.35
  175.9 8.1 %all_to_all.57 = f32[2,4,4,2,1024,8]{4,5,3,2,1,0:T(8,128)} all-to-all(f32[2,4,4,2,1024,8]{4,5,3,2,1,0:T(8,128)S(1)} %bitcast.42), channel_id=1, replica_groups=mesh['x'=4,'yh'=2,'zh'=4,'zl'=4,'yl'=2,'c'=2] {'c'}, dimensions={0} | all-to-all | bytes 4194304 | tf_op jit(solution)/shard_map/all_to_all | solution.py:164
  184.0 2.8 %reduce_sum.125 = f32[4,4,2,1024,8]{3,4,2,1,0:T(8,128)} reduce(f32[2,4,4,2,1024,8]{4,5,3,2,1,0:T(8,128)} %all_to_all.57, f32[]{:T(128)} %constant.8.clone.1), dimensions={0}, to_apply=%region_8.9 | reduce | flops 262144 | bytes 3145732 | tf_op jit(solution)/shard_map/reduce_sum | solution.py:164
  186.8 1.3 copy.29
  188.2 28.6 %all_to_all.58 = f32[8,4,1024,8]{2,3,1,0:T(8,128)} all-to-all(f32[8,4,1024,8]{2,3,1,0:T(8,128)S(1)} %copy.29), channel_id=1, replica_groups=mesh['x'=4,'yh'=2,'zh'=4,'zl'=4,'yl'=2,'c'=2] {'zl','yl'}, dimensions={0} | all-to-all | bytes 2097152 | tf_op jit(solution)/shard_map/all_to_all | solution.py:166
  216.8 1.9 reduce_sum.126
  218.7 3.3 %all-to-all-start.9 = ((f32[4,1024,8]{1,2,0:T(8,128)}), f32[4,1024,8]{1,2,0:T(8,128)S(1)}, u32[]{:S(2)}, u32[]{:S(2)}) async-start(f32[4,1024,8]{1,2,0:T(8,128)} %reduce_sum.126), calls=%async_computation.9 | async-start | bytes 262144 | tf_op jit(solution)/shard_map/all_to_all | solution.py:167
  222.0 0.6 subtract_reduce_fusion
  222.6 11.6 %all-to-all-done.9 = f32[4,1024,8]{1,2,0:T(8,128)S(1)} async-done(((f32[4,1024,8]{1,2,0:T(8,128)}), f32[4,1024,8]{1,2,0:T(8,128)S(1)}, u32[]{:S(2)}, u32[]{:S(2)}) %all-to-all-start.9) | async-done | bytes 131104 | tf_op jit(solution)/shard_map/all_to_all | solution.py:167
  234.2 0.6 reduce_sum.127
  (11 shorter events, 0.1 us)
Async XLA Ops:
  0.6 52.7 %copy-start = (bf16[1536,1024]{1,0:T(8,128)(2,1)S(1)}, bf16[1536,1024]{1,0:T(8,128)(2,1)}, u32[]{:S(2)}) copy-start(bf16[1536,1024]{1,0:T(8,128)(2,1)} %param.5) | copy-start | bytes 9437188
  56.9 6.5 %copy-start.1 = (s32[8]{0:T(128)S(1)}, s32[8]{0:T(128)}, u32[]{:S(2)}) copy-start(s32[8]{0:T(128)} %param.6) | copy-start | bytes 100
  56.9 51.6 %all-to-all-start.3 = ((f32[8,512,192]{1,2,0:T(8,128)}), f32[8,512,192]{1,2,0:T(8,128)}, u32[]{:S(2)}, u32[]{:S(2)}) async-start(f32[8,512,192]{1,2,0:T(8,128)} %convolution_bitcast_fusion), calls=%async_computation.3 | async-start | bytes 6291456 | tf_op jit(solution)/shard_map/all_to_all | solution.py:45
  63.4 82.2 %copy-start.2 = (s32[4]{0:T(128)S(1)}, s32[4]{0:T(128)}, u32[]{:S(2)}) copy-start(s32[4]{0:T(128)} %param.7) | copy-start | bytes 52
  124.9 20.2 %all-to-all-start.5 = ((f32[64,1,24]{2,1,0:T(1,128)}), f32[64,1,24]{2,1,0:T(1,128)S(1)}, u32[]{:S(2)}, u32[]{:S(2)}) async-start(f32[64,1,24]{2,1,0:T(1,128)} %broadcast_in_dim.16), calls=%async_computation.5 | async-start | bytes 65536 | tf_op jit(solution)/shard_map/all_to_all | solution.py:51
  218.7 15.5 %all-to-all-start.9 = ((f32[4,1024,8]{1,2,0:T(8,128)}), f32[4,1024,8]{1,2,0:T(8,128)S(1)}, u32[]{:S(2)}, u32[]{:S(2)}) async-start(f32[4,1024,8]{1,2,0:T(8,128)} %reduce_sum.126), calls=%async_computation.9 | async-start | bytes 262144 | tf_op jit(solution)/shard_map/all_to_all | solution.py:167

commit v14 on v11

--- a/solution.py
+++ b/solution.py
@@ -164,7 +164,12 @@
     grad = jnp.sum(lax.all_to_all(grad, "c", 0, 0, tiled=True), axis=0)
     grad = grad.transpose(1, 2, 0, 3, 4).reshape(n_zl * n_yl, n_zh, width, rows)
     grad = jnp.sum(lax.all_to_all(grad, ("zl", "yl"), 0, 0, tiled=True), axis=0)
-    hidden_grad = jnp.sum(lax.all_to_all(grad, "zh", 0, 0, tiled=True), axis=0).T
+    me = lax.axis_index("zh")
+    hidden_grad = lax.dynamic_index_in_dim(grad, me, 0, keepdims=False)
+    for k in range(1, n_zh):
+        block = lax.dynamic_index_in_dim(grad, (me + k) % n_zh, 0, keepdims=False)
+        hidden_grad = hidden_grad + _shift(block, "zh", n_zh, k)
+    hidden_grad = hidden_grad.T
     return (hidden_grad, loss)
 
 

time: 236 us -> 240 us (1.017)
  blocking collectives: 130 us -> 101 us
  waiting for transfers between devices: 62.9 us -> 83.5 us
  starting transfers between devices: 14.7 us -> 26.8 us
    all_to_all x1 -> x0, blocking collectives: 28.6 us -> none  [local(): grad = jnp.sum(lax.all_to_all(grad, ('zl', 'yl'), 0, 0, tiled=True), axis=0)]
    all_to_all x1, waiting for transfers between devices: 11.6 us -> 25.5 us  [local(): grad = jnp.sum(lax.all_to_all(grad, ('zl', 'yl'), 0, 0, tiled=True), axis=0)]
    ppermute x0 -> x3, starting transfers between devices: none -> 11.2 us  [_shift(): return lax.ppermute(v, axis, [(i, (i + k) % n) for i in range(n)])]
    ppermute x0 -> x3, waiting for transfers between devices: none -> 6.69 us  [_shift(): return lax.ppermute(v, axis, [(i, (i + k) % n) for i in range(n)])]
  transfers between devices with their start and end apart: 3 -> 6, of which waited for: 3 -> 5; matrix products, arithmetic and copies ran while one was open for 0% -> 0% of each run, Pallas kernels for 0% -> 0%
where the time goes in v14:
time: 240 us; the launch traced here: 238 us
  blocking collectives  101 us (42%)
  waiting for transfers between devices  83.5 us (35%)
  starting transfers between devices  26.8 us (11%)
  other arithmetic  12.7 us (5%)
  local copies, waits for them, and re-layouts  6.83 us (3%)
  matrix products  6.03 us (3%)
    all_to_all x3, blocking collectives, _copies_a2a(): lax.all_to_all(jnp.broadcast_to(x[None], (n,) + x.shape), axes, 0, 0, til...  51.5 us
    all_to_all x1, waiting for transfers between devices, _reduce_scatter_a2a(): return jnp.sum(lax.all_to_all(blocks, axes, 0, 0, tiled=True), axis=0)  45 us
    all_to_all x1, waiting for transfers between devices, local(): grad = jnp.sum(lax.all_to_all(grad, ('zl', 'yl'), 0, 0, tiled=True), axis=0)  25.5 us
    all_to_all x1, blocking collectives, local(): lax.all_to_all(copies, SEC, 0, 0, tiled=True).reshape(-1, dlogit.shape[0])  22.2 us
    all_to_all x1, blocking collectives, _all_reduce_a2a(): return jnp.sum(lax.all_to_all(copies, axes, 0, 0, tiled=True), axis=0)  18.1 us
    ppermute x3, starting transfers between devices, _shift(): return lax.ppermute(v, axis, [(i, (i + k) % n) for i in range(n)])  11.2 us
    all_to_all x1, blocking collectives, local(): grad = jnp.sum(lax.all_to_all(grad, 'c', 0, 0, tiled=True), axis=0)  9.63 us
    ppermute x3, waiting for transfers between devices, _shift(): return lax.ppermute(v, axis, [(i, (i + k) % n) for i in range(n)])  6.69 us
  transfers between devices with their start and end apart: 6, of which 5 were waited for; matrix products, arithmetic and copies ran while one was open for 0% of the time, Pallas kernels for 0%

profile of v14, /device:TPU:1, one launch (start us, length us, event | category | flops | bytes accessed | tf_op | source)
XLA Modules:
  0.0 238.1 jit_solution(4838731001196088585)
XLA Ops:
  0.6 0.9 broadcast_in_dim.12
  1.5 28.1 %all_to_all.47 = bf16[4,8,1024]{2,1,0:T(8,128)(2,1)S(1)} all-to-all(bf16[4,8,1024]{2,1,0:T(8,128)(2,1)S(1)} %broadcast_in_dim.12), channel_id=1, replica_groups=mesh['x'=4,'yh'=2,'zh'=4,'zl'=4,'yl'=2,'c'=2] {'zh'}, dimensions={0} | all-to-all | bytes 131072 | tf_op jit(solution)/shard_map/all_to_all | solution.py:38
  29.6 17.1 %all_to_all.48 = bf16[8,4,8,1024]{3,2,1,0:T(8,128)(2,1)S(1)} all-to-all(bf16[8,4,8,1024]{3,2,1,0:T(8,128)(2,1)S(1)} %broadcast_in_dim.13), channel_id=1, replica_groups=mesh['x'=4,'yh'=2,'zh'=4,'zl'=4,'yl'=2,'c'=2] {'zl','yl'}, dimensions={0} | all-to-all | bytes 1048576 | tf_op jit(solution)/shard_map/all_to_all | solution.py:38
  46.8 0.1 broadcast_in_dim.14
  46.9 6.3 %all_to_all.49 = bf16[2,8,4,8,1024]{4,3,1,2,0:T(8,128)(2,1)S(1)} all-to-all(bf16[2,8,4,8,1024]{4,3,1,2,0:T(8,128)(2,1)S(1)} %broadcast_in_dim.14), channel_id=1, replica_groups=mesh['x'=4,'yh'=2,'zh'=4,'zl'=4,'yl'=2,'c'=2] {'c'}, dimensions={0} | all-to-all | bytes 2097152 | tf_op jit(solution)/shard_map/all_to_all | solution.py:38
  53.2 0.1 copy.22
  53.3 3.6 %convolution_bitcast_fusion = f32[8,512,192]{1,2,0:T(8,128)} fusion(bf16[512,1024,1]{1,0,2:T(8,128)(2,1)S(1)} %bitcast.62, bf16[8,192,1024]{2,1,0:T(8,128)(2,1)S(1)} %bitcast.56), kind=kOutput, calls=%fused_computation.1 | convolution fusion | flops 1610612736 | bytes 7340032 | tf_op jit(solution)/shard_map/dot_general | solution.py:99
  56.9 6.5 %all-to-all-start.3 = ((f32[8,512,192]{1,2,0:T(8,128)}), f32[8,512,192]{1,2,0:T(8,128)}, u32[]{:S(2)}, u32[]{:S(2)}) async-start(f32[8,512,192]{1,2,0:T(8,128)} %convolution_bitcast_fusion), calls=%async_computation.3 | async-start | bytes 6291456 | tf_op jit(solution)/shard_map/all_to_all | solution.py:45
  63.5 45.0 %all-to-all-done.3 = f32[8,512,192]{1,2,0:T(8,128)} async-done(((f32[8,512,192]{1,2,0:T(8,128)}), f32[8,512,192]{1,2,0:T(8,128)}, u32[]{:S(2)}, u32[]{:S(2)}) %all-to-all-start.3) | async-done | bytes 3145760 | tf_op jit(solution)/shard_map/all_to_all | solution.py:45
  108.5 2.3 reduce_sum.108
  110.7 1.0 copy.23
  111.7 1.6 multiply_reduce_fusion
  113.3 0.1 multiply_reduce_fusion.1
  113.4 0.1 fusion.8
  113.6 0.1 reshape.95
  113.6 0.1 pad_maximum_fusion.1
  113.8 18.1 %all_to_all.50 = f32[64,1,24]{2,1,0:T(1,128)S(1)} all-to-all(f32[64,1,24]{2,1,0:T(1,128)S(1)} %broadcast_in_dim.15), channel_id=1, replica_groups=mesh['x'=4,'yh'=2,'zh'=4,'zl'=4,'yl'=2,'c'=2] {'zh','zl','yl','c'}, dimensions={0} | all-to-all | bytes 12288 | tf_op jit(solution)/shard_map/all_to_all | solution.py:51
  131.8 0.1 reduce_sum.111
  131.9 0.6 broadcast_in_dim.16
  132.5 4.9 %all-to-all-start.5 = ((f32[8,1,24]{2,1,0:T(1,128)}), f32[8,1,24]{2,1,0:T(1,128)S(1)}, u32[]{:S(2)}, u32[]{:S(2)}) async-start(f32[8,1,24]{2,1,0:T(1,128)} %broadcast_in_dim.16), calls=%async_computation.5 | async-start | bytes 8192 | tf_op jit(solution)/shard_map/all_to_all | solution.py:51
  137.5 6.4 %all-to-all-done.5 = f32[8,1,24]{2,1,0:T(1,128)S(1)} async-done(((f32[8,1,24]{2,1,0:T(1,128)}), f32[8,1,24]{2,1,0:T(1,128)S(1)}, u32[]{:S(2)}, u32[]{:S(2)}) %all-to-all-start.5) | async-done | bytes 800 | tf_op jit(solution)/shard_map/all_to_all | solution.py:51
  143.8 0.1 add_rsqrt_fusion
  144.0 0.1 reshape.96
  144.1 0.2 exponential_reduce_fusion
  144.3 0.2 multiply_reduce_fusion.3
  144.5 0.1 multiply_multiply_fusion.5
  144.6 0.1 slice_multiply_fusion.1
  144.6 0.2 convolution_add_fusion.1
  144.8 0.3 convolution_add_fusion
  145.1 2.4 %fusion.2 = bf16[512,192]{1,0:T(8,128)(2,1)} fusion(f32[512,192]{1,0:T(8,128)} %copy.23, f32[8,192]{1,0:T(8,128)S(1)} %multiply_reduce_fusion, f32[512]{0:T(512)S(1)} %reshape.100, f32[8,192]{1,0:T(8,128)S(1)} %pad_maximum_fusion), kind=kLoop, calls=%fused_computation.11 | loop fusion | flops 1671168 | bytes 604160 | tf_op jit(solution)/shard_map/convert_element_type | solution.py:151
  147.6 1.1 copy.26
  148.6 0.1 broadcast_in_dim.17
  148.8 22.2 %all_to_all.51 = bf16[8,192,512]{2,1,0:T(8,128)(2,1)S(1)} all-to-all(bf16[8,192,512]{2,1,0:T(8,128)(2,1)S(1)} %broadcast_in_dim.17), channel_id=1, replica_groups=mesh['x'=4,'yh'=2,'zh'=4,'zl'=4,'yl'=2,'c'=2] {'x','yh'}, dimensions={0} | all-to-all | bytes 3145728 | tf_op jit(solution)/shard_map/all_to_all | solution.py:156
  171.0 1.8 fusion.20
  172.8 0.2 copy.33
  173.0 9.6 %all_to_all.52 = f32[2,4,4,2,1024,8]{4,5,3,2,1,0:T(8,128)} all-to-all(f32[2,4,4,2,1024,8]{4,5,3,2,1,0:T(8,128)S(1)} %bitcast.57), channel_id=1, replica_groups=mesh['x'=4,'yh'=2,'zh'=4,'zl'=4,'yl'=2,'c'=2] {'c'}, dimensions={0} | all-to-all | bytes 4194304 | tf_op jit(solution)/shard_map/all_to_all | solution.py:164
  182.7 2.8 %reduce_sum.116 = f32[4,4,2,1024,8]{3,4,2,1,0:T(8,128)} reduce(f32[2,4,4,2,1024,8]{4,5,3,2,1,0:T(8,128)} %all_to_all.52, f32[]{:T(128)} %constant.53.clone.1), dimensions={0}, to_apply=%region_8.9 | reduce | flops 262144 | bytes 3145732 | tf_op jit(solution)/shard_map/reduce_sum | solution.py:164
  185.5 2.3 copy.29
  187.8 4.2 %all-to-all-start.8 = ((f32[8,4,1024,8]{2,3,1,0:T(8,128)}), f32[8,4,1024,8]{2,3,1,0:T(8,128)}, u32[]{:S(2)}, u32[]{:S(2)}) async-start(f32[8,4,1024,8]{2,3,1,0:T(8,128)} %copy.29), calls=%async_computation.8 | async-start | bytes 2097152 | tf_op jit(solution)/shard_map/all_to_all | solution.py:166
  192.1 25.5 %all-to-all-done.8 = f32[8,4,1024,8]{2,3,1,0:T(8,128)} async-done(((f32[8,4,1024,8]{2,3,1,0:T(8,128)}), f32[8,4,1024,8]{2,3,1,0:T(8,128)}, u32[]{:S(2)}, u32[]{:S(2)}) %all-to-all-start.8) | async-done | bytes 1048608 | tf_op jit(solution)/shard_map/all_to_all | solution.py:166
  217.6 1.3 reduce_sum.117
  218.9 2.2 collective-permute-start
  221.1 6.9 %collective-permute-start.1 = (f32[1024,8]{0,1:T(8,128)S(1)}, f32[1024,8]{0,1:T(8,128)S(1)}, u32[]{:S(2)}, u32[]{:S(2)}) collective-permute-start(f32[1024,8]{0,1:T(8,128)S(1)} %get-tuple-element.8), channel_id=1, source_target_pairs={{0,32},{16,48},{32,0},{48,16},{1,33},{17,49},{33,1},{49,17},{2,34}... | collective-permute-start | bytes 98312 | tf_op jit(solution)/shard_map/ppermute | solution.py:55
  228.0 2.1 collective-permute-start.2
  230.1 0.6 subtract_reduce_fusion
  230.7 3.8 %collective-permute-done.1 = f32[1024,8]{0,1:T(8,128)S(1)} collective-permute-done((f32[1024,8]{0,1:T(8,128)S(1)}, f32[1024,8]{0,1:T(8,128)S(1)}, u32[]{:S(2)}, u32[]{:S(2)}) %collective-permute-start.1) | collective-permute-done | bytes 32800 | tf_op jit(solution)/shard_map/ppermute | solution.py:55
  234.5 2.9 %collective-permute-done.2 = f32[1024,8]{0,1:T(8,128)S(1)} collective-permute-done((f32[1024,8]{0,1:T(8,128)S(1)}, f32[1024,8]{0,1:T(8,128)S(1)}, u32[]{:S(2)}, u32[]{:S(2)}) %collective-permute-start.2) | collective-permute-done | bytes 32800 | tf_op jit(solution)/shard_map/ppermute | solution.py:55
  237.4 0.6 fusion.5
  (17 shorter events, 0.4 us)
Async XLA Ops:
  0.6 52.7 %copy-start = (bf16[1536,1024]{1,0:T(8,128)(2,1)S(1)}, bf16[1536,1024]{1,0:T(8,128)(2,1)}, u32[]{:S(2)}) copy-start(bf16[1536,1024]{1,0:T(8,128)(2,1)} %param.5) | copy-start | bytes 9437188
  56.9 6.5 %copy-start.1 = (s32[8]{0:T(128)S(1)}, s32[8]{0:T(128)}, u32[]{:S(2)}) copy-start(s32[8]{0:T(128)} %param.6) | copy-start | bytes 100
  56.9 51.6 %all-to-all-start.3 = ((f32[8,512,192]{1,2,0:T(8,128)}), f32[8,512,192]{1,2,0:T(8,128)}, u32[]{:S(2)}, u32[]{:S(2)}) async-start(f32[8,512,192]{1,2,0:T(8,128)} %convolution_bitcast_fusion), calls=%async_computation.3 | async-start | bytes 6291456 | tf_op jit(solution)/shard_map/all_to_all | solution.py:45
  63.4 80.9 %copy-start.2 = (s32[4]{0:T(128)S(1)}, s32[4]{0:T(128)}, u32[]{:S(2)}) copy-start(s32[4]{0:T(128)} %param.7) | copy-start | bytes 52
  132.5 11.3 %all-to-all-start.5 = ((f32[8,1,24]{2,1,0:T(1,128)}), f32[8,1,24]{2,1,0:T(1,128)S(1)}, u32[]{:S(2)}, u32[]{:S(2)}) async-start(f32[8,1,24]{2,1,0:T(1,128)} %broadcast_in_dim.16), calls=%async_computation.5 | async-start | bytes 8192 | tf_op jit(solution)/shard_map/all_to_all | solution.py:51
  187.8 29.8 %all-to-all-start.8 = ((f32[8,4,1024,8]{2,3,1,0:T(8,128)}), f32[8,4,1024,8]{2,3,1,0:T(8,128)}, u32[]{:S(2)}, u32[]{:S(2)}) async-start(f32[8,4,1024,8]{2,3,1,0:T(8,128)} %copy.29), calls=%async_computation.8 | async-start | bytes 2097152 | tf_op jit(solution)/shard_map/all_to_all | solution.py:166
  218.9 11.8 %collective-permute-start = (f32[1024,8]{0,1:T(8,128)S(1)}, f32[1024,8]{0,1:T(8,128)S(1)}, u32[]{:S(2)}, u32[]{:S(2)}) collective-permute-start(f32[1024,8]{0,1:T(8,128)S(1)} %get-tuple-element.6), channel_id=1, source_target_pairs={{0,16},{16,32},{32,48},{48,0},{1,17},{17,33},{33,49},{49,1},{2,18}... | collective-permute-start | bytes 98312 | tf_op jit(solution)/shard_map/ppermute | solution.py:55
  221.1 13.4 %collective-permute-start.1 = (f32[1024,8]{0,1:T(8,128)S(1)}, f32[1024,8]{0,1:T(8,128)S(1)}, u32[]{:S(2)}, u32[]{:S(2)}) collective-permute-start(f32[1024,8]{0,1:T(8,128)S(1)} %get-tuple-element.8), channel_id=1, source_target_pairs={{0,32},{16,48},{32,0},{48,16},{1,33},{17,49},{33,1},{49,17},{2,34}... | collective-permute-start | bytes 98312 | tf_op jit(solution)/shard_map/ppermute | solution.py:55
  228.0 9.4 %collective-permute-start.2 = (f32[1024,8]{0,1:T(8,128)S(1)}, f32[1024,8]{0,1:T(8,128)S(1)}, u32[]{:S(2)}, u32[]{:S(2)}) collective-permute-start(f32[1024,8]{0,1:T(8,128)S(1)} %get-tuple-element.7), channel_id=1, source_target_pairs={{0,48},{16,0},{32,16},{48,32},{1,49},{17,1},{33,17},{49,33},{2,50}... | collective-permute-start | bytes 98312 | tf_op jit(solution)/shard_map/ppermute | solution.py:55
